TPU v7x, 256 devices: a whole 4x4x8 slice. The times are simulated.
256 devices in a mesh: seg: 128 (over y, x_hi, z, core), fsdp: 2 (over x_lo).
Axes of the slice: x: 4 (x_hi: 2, x_lo: 2; x = x_hi * 2 + x_lo), y: 4, z: 8, core: 2. Of those that a mesh axis runs over, the one named last changes fastest.
Arguments:
- hidden_states: bfloat16 [98304, 2048], P(('seg', 'fsdp'))
- queries: bfloat16 [98304, 2048], P(('seg', 'fsdp'))
- w_key: bfloat16 [2048, 2048], P('fsdp')
- w_value: bfloat16 [2048, 2048], P('fsdp'), may hold values from -0.125 to 0.125
Outputs:
- attended: bfloat16 [98304, 2048], P(('seg', 'fsdp'))
All inputs are finite; a program needn't handle non-finite values.
Results may differ from a plain program's by a relative error of at most 0.0076.
Values may be sent and summed in bfloat16 or wider, within the bound.
No kernel may reach another device: no remote copies, remote signals or barrier semaphores. Data moves between devices by JAX's collectives and lax.ppermute only.
A program may use at most 128 MiB of HBM per device.

v0:
```python
import jax
import jax.numpy as jnp
from jax import lax
from jax.sharding import PartitionSpec as P

HD = 128
MEM = 2


def from_behind(value, axis, steps):
    count = lax.axis_size(axis)
    leading, last = (max(0, -steps), min(count, count - steps))
    return lax.ppermute(value, axis, [(source, source + steps) for source in range(leading, last)])


def attend_group(query_rows, key_flat, value_flat, allowed, group_number):
    span = 4 * HD
    count = query_rows.shape[0]
    query_part = lax.dynamic_slice_in_dim(query_rows, group_number * span, span, 1).reshape(
        count, 4, HD
    )
    key_part = lax.dynamic_slice_in_dim(key_flat, group_number * span, span, 1).reshape(
        key_flat.shape[0], 4, HD
    )
    value_part = lax.dynamic_slice_in_dim(value_flat, group_number * span, span, 1).reshape(
        value_flat.shape[0], 4, HD
    )
    scores = jnp.einsum(
        "qhd,khd->hqk", query_part, key_part, preferred_element_type=jnp.float32
    ) * HD ** (-0.5)
    scores = jnp.where(allowed[None], scores, jnp.float32(-1e30))
    top_score = jnp.max(scores, axis=-1, keepdims=True)
    expo = jnp.where(allowed[None], jnp.exp(scores - top_score), jnp.float32(0.0))
    total = jnp.sum(expo, axis=-1)
    weights = expo.astype(jnp.bfloat16)
    mixed = jnp.einsum("hqk,khd->qhd", weights, value_part, preferred_element_type=jnp.float32)
    mixed = mixed / jnp.transpose(total)[:, :, None]
    return mixed.reshape(count, span).astype(jnp.bfloat16)


def body(hidden_states, queries, w_key, w_value):
    tok_rows = hidden_states.shape[0]
    width = w_key.shape[1]
    key_sum = jnp.dot(
        hidden_states,
        lax.all_gather(w_key, "fsdp", axis=0, tiled=True),
        preferred_element_type=jnp.float32,
    )
    value_sum = jnp.dot(
        hidden_states,
        lax.all_gather(w_value, "fsdp", axis=0, tiled=True),
        preferred_element_type=jnp.float32,
    )
    own_pair = jnp.stack([key_sum.astype(jnp.bfloat16), value_sum.astype(jnp.bfloat16)])
    own_unit = lax.all_gather(own_pair, "fsdp", axis=1, tiled=True)
    earlier = []
    for distance in range(1, MEM + 1):
        arrived = from_behind(own_unit, "seg", distance)
        earlier.insert(0, arrived)
    context = jnp.stack(earlier + [own_unit])
    seg_rows = context.shape[2]
    key_flat = context[:, 0].reshape((MEM + 1) * seg_rows, width)
    value_flat = context[:, 1].reshape((MEM + 1) * seg_rows, width)
    seg_number = lax.axis_index("seg")
    half_number = lax.axis_index("fsdp")
    query_pos = half_number * tok_rows + jnp.arange(tok_rows, dtype=jnp.int32)
    key_pos = jnp.arange((MEM + 1) * seg_rows, dtype=jnp.int32)
    block_of = key_pos // seg_rows
    within = key_pos % seg_rows
    earlier_ok = (block_of < MEM) & (seg_number >= MEM - block_of)
    own_ok = (block_of == MEM)[None, :] & (within[None, :] <= query_pos[:, None])
    allowed = earlier_ok[None, :] | own_ok

    def one_group(group_number):
        return attend_group(queries, key_flat, value_flat, allowed, group_number)

    grouped = lax.map(one_group, jnp.arange(width // (4 * HD), dtype=jnp.int32))
    return jnp.transpose(grouped, (1, 0, 2)).reshape(tok_rows, width)


def solution(mesh):
    placed = (P(("seg", "fsdp"), None), P(("seg", "fsdp"), None), P("fsdp", None), P("fsdp", None))
    return jax.shard_map(
        body, mesh=mesh, in_specs=placed, out_specs=P(("seg", "fsdp"), None), check_vma=False
    )
```

profile of v0, /device:TPU:24, one launch (start us, length us, event | category | flops | bytes accessed | tf_op | source)
XLA Modules:
  0.0 692.8 jit_solution(751616169947207539)
XLA Ops:
  6.5 0.0 copy-start
  6.5 0.0 all-gather.4.cloned.1.call-start
  6.5 0.7 all-gather.4.cloned.1.call-update
  7.3 0.0 all-gather.6.cloned.1.call-start
  7.3 0.7 all-gather.6.cloned.1.call-update
  8.0 0.0 all-gather.8.cloned.1.call-start
  8.1 112.9 %all-gather.4.cloned.1.call-done = bf16[2048,2048]{1,0:T(8,128)(2,1)} async-done(((bf16[1024,2048]{1,0:T(8,128)(2,1)}), bf16[2048,2048]{1,0:T(8,128)(2,1)}) %all-gather.4.cloned.1.call-update) | async-done | bytes 8388624 | tf_op jit(solution)/shard_map/all_gather | solution.py:46
  120.9 0.0 copy-done
  120.9 6.8 fusion.22
  127.7 105.1 %all-gather.6.cloned.1.call-done = bf16[2048,2048]{1,0:T(8,128)(2,1)} async-done(((bf16[1024,2048]{1,0:T(8,128)(2,1)}), bf16[2048,2048]{1,0:T(8,128)(2,1)}) %all-gather.6.cloned.1.call-update) | async-done | bytes 8388624 | tf_op jit(solution)/shard_map/all_gather | solution.py:51
  232.8 6.8 fusion.23
  239.6 2.0 pad_maximum_fusion.1
  241.6 0.0 all-gather.8.cloned.1.call-update
  241.6 86.6 %all-gather.8.cloned.1.call-done = bf16[2,768,2048]{2,1,0:T(8,128)(2,1)} async-done(((bf16[2,384,2048]{2,1,0:T(8,128)(2,1)}), bf16[2,768,2048]{2,1,0:T(8,128)(2,1)}) %all-gather.8.cloned.1.call-update) | async-done | bytes 6291472 | tf_op jit(solution)/shard_map/all_gather | solution.py:55
  328.2 3.5 collective-permute-start
  331.6 2.1 collective-permute-start.1
  333.8 139.5 %collective-permute-done = bf16[2,768,2048]{2,1,0:T(8,128)(2,1)} collective-permute-done((bf16[2,768,2048]{2,1,0:T(8,128)(2,1)}, bf16[2,768,2048]{2,1,0:T(8,128)(2,1)}, u32[]{:S(2)}, u32[]{:S(2)}) %collective-permute-start) | collective-permute-done | bytes 6291488 | tf_op jit(solution)/shard_map/ppermute | solution.py:13
  473.3 66.1 %collective-permute-done.1 = bf16[2,768,2048]{2,1,0:T(8,128)(2,1)} collective-permute-done((bf16[2,768,2048]{2,1,0:T(8,128)(2,1)}, bf16[2,768,2048]{2,1,0:T(8,128)(2,1)}, u32[]{:S(2)}, u32[]{:S(2)}) %collective-permute-start.1) | collective-permute-done | bytes 6291488 | tf_op jit(solution)/shard_map/ppermute | solution.py:13
  539.4 9.6 %pad_maximum_fusion = bf16[3,2,768,2048]{3,2,1,0:T(8,128)(2,1)S(1)} fusion(bf16[1,2,768,2048]{3,2,1,0:T(8,128)(2,1)} %bitcast.62, bf16[1,2,768,2048]{3,2,1,0:T(8,128)(2,1)} %bitcast.3, bf16[1,2,768,2048]{3,2,1,0:T(8,128)(2,1)} %bitcast.2), kind=kLoop, calls=%fused_computation.21 | loop fusion | flops 18874368 | bytes 37748736 | tf_op jit(solution)/shard_map/stack | solution.py:60
  549.0 6.8 fusion.33
  555.7 127.8 %while.11 = (s32[]{:T(128)}, bf16[4,384,512]{1,2,0:T(8,128)(2,1)}, s32[4]{0:T(128)S(1)}, bf16[2304,2048]{1,0:T(8,128)(2,1)}, bf16[384,2048]{1,0:T(8,128)(2,1)}, ...) while((s32[]{:T(128)}, bf16[4,384,512]{1,2,0:T(8,128)(2,1)}, ...), condition=%wide.region_3.4_spmd.clone, body=%wide.region_0.3_spmd.clone.sunk | while | flops 1836222720 | bytes 42692296 | solution.py:77
  555.7 0.6 dynamic_slice.25
  557.0 4.1 constant_dynamic-slice_fusion.5
  561.1 4.3 copy.24
  565.4 1.0 constant_dynamic-slice_fusion.6
  566.4 0.9 copy.23
  567.3 0.8 and_or_fusion.2
  568.1 10.5 %fusion.54 = (f32[4,384]{1,0:T(4,128)S(1)}, bf16[4,384,2304]{2,1,0:T(8,128)(2,1)}) fusion(pred[384,2304]{1,0:T(8,128)(4,1)S(1)} %and_or_fusion.2, bf16[384,4,128]{0,2,1:T(8,128)(2,1)} %bitcast.60, bf16[2304,4,128]{0,2,1:T(8,128)(2,1)} %bitcast.56), kind=kOutput, calls=%fused_computation.42.clone.1 | convolution fusion | flops 927205632 | bytes 10721280 | tf_op jit(solution)/shard_map/while/body/eval_jaxpr/sub | solution.py:33
  578.6 2.5 copy.22
  581.1 5.7 fusion.55
  586.9 0.8 constant_dynamic-update-slice_fusion.2
  587.7 0.6 dynamic_slice.25
  588.9 4.1 constant_dynamic-slice_fusion.5
  593.0 4.3 copy.24
  597.3 1.0 constant_dynamic-slice_fusion.6
  598.4 0.9 copy.23
  599.3 0.8 and_or_fusion.2
  600.0 10.5 %fusion.54 = (f32[4,384]{1,0:T(4,128)S(1)}, bf16[4,384,2304]{2,1,0:T(8,128)(2,1)}) fusion(pred[384,2304]{1,0:T(8,128)(4,1)S(1)} %and_or_fusion.2, bf16[384,4,128]{0,2,1:T(8,128)(2,1)} %bitcast.60, bf16[2304,4,128]{0,2,1:T(8,128)(2,1)} %bitcast.56), kind=kOutput, calls=%fused_computation.42.clone.1 | convolution fusion | flops 927205632 | bytes 10721280 | tf_op jit(solution)/shard_map/while/body/eval_jaxpr/sub | solution.py:33
  610.5 2.5 copy.22
  613.1 5.7 fusion.55
  618.8 0.8 constant_dynamic-update-slice_fusion.2
  619.6 0.6 dynamic_slice.25
  620.9 4.1 constant_dynamic-slice_fusion.5
  625.0 4.3 copy.24
  629.3 1.0 constant_dynamic-slice_fusion.6
  630.3 0.9 copy.23
  631.2 0.8 and_or_fusion.2
  632.0 10.5 %fusion.54 = (f32[4,384]{1,0:T(4,128)S(1)}, bf16[4,384,2304]{2,1,0:T(8,128)(2,1)}) fusion(pred[384,2304]{1,0:T(8,128)(4,1)S(1)} %and_or_fusion.2, bf16[384,4,128]{0,2,1:T(8,128)(2,1)} %bitcast.60, bf16[2304,4,128]{0,2,1:T(8,128)(2,1)} %bitcast.56), kind=kOutput, calls=%fused_computation.42.clone.1 | convolution fusion | flops 927205632 | bytes 10721280 | tf_op jit(solution)/shard_map/while/body/eval_jaxpr/sub | solution.py:33
  642.5 2.5 copy.22
  645.0 5.8 fusion.55
  650.8 0.8 constant_dynamic-update-slice_fusion.2
  651.6 0.6 dynamic_slice.25
  652.8 4.1 constant_dynamic-slice_fusion.5
  656.9 4.3 copy.24
  661.2 1.0 constant_dynamic-slice_fusion.6
  662.3 0.9 copy.23
  663.2 0.8 and_or_fusion.2
  664.0 10.5 %fusion.54 = (f32[4,384]{1,0:T(4,128)S(1)}, bf16[4,384,2304]{2,1,0:T(8,128)(2,1)}) fusion(pred[384,2304]{1,0:T(8,128)(4,1)S(1)} %and_or_fusion.2, bf16[384,4,128]{0,2,1:T(8,128)(2,1)} %bitcast.60, bf16[2304,4,128]{0,2,1:T(8,128)(2,1)} %bitcast.56), kind=kOutput, calls=%fused_computation.42.clone.1 | convolution fusion | flops 927205632 | bytes 10721280 | tf_op jit(solution)/shard_map/while/body/eval_jaxpr/sub | solution.py:33
  674.5 2.5 copy.22
  677.0 5.7 fusion.55
  682.7 0.8 constant_dynamic-update-slice_fusion.2
  683.6 0.0 copy-start.1
  683.6 2.7 copy.15
  686.3 0.0 copy-done.1
  (5 shorter events, 0.0 us)
Async XLA Ops:
  6.5 114.4 %copy-start = (bf16[384,2048]{1,0:T(8,128)(2,1)S(1)}, bf16[384,2048]{1,0:T(8,128)(2,1)}, u32[]{:S(2)}) copy-start(bf16[384,2048]{1,0:T(8,128)(2,1)} %param.6) | copy-start | bytes 4718596
  6.5 114.4 %all-gather.4.cloned.1.call-start = ((), (), s32[]{:S(2)}) async-start(), calls=%async_computation | async-start | bytes 12582912 | tf_op jit(solution)/shard_map/all_gather | solution.py:46
  7.3 225.5 %all-gather.6.cloned.1.call-start = ((), (), s32[]{:S(2)}) async-start(), calls=%async_computation.1 | async-start | bytes 12582912 | tf_op jit(solution)/shard_map/all_gather | solution.py:51
  8.0 320.2 %all-gather.8.cloned.1.call-start = ((), (), s32[]{:S(2)}) async-start(), calls=%async_computation.2 | async-start | bytes 9437184 | tf_op jit(solution)/shard_map/all_gather | solution.py:55
  328.2 145.1 %collective-permute-start = (bf16[2,768,2048]{2,1,0:T(8,128)(2,1)}, bf16[2,768,2048]{2,1,0:T(8,128)(2,1)}, u32[]{:S(2)}, u32[]{:S(2)}) collective-permute-start(bf16[2,768,2048]{2,1,0:T(8,128)(2,1)} %all-gather.8.cloned.1.call-done), channel_id=1, source_target_pairs={{0,4},{2,6},{4,8},{6,10},{8,12},{10,14},{12,16},{14,18},{16,20},{1... | collective-permute-start | bytes 18874376 | tf_op jit(solution)/shard_map/ppermute | solution.py:13
  331.6 207.8 %collective-permute-start.1 = (bf16[2,768,2048]{2,1,0:T(8,128)(2,1)}, bf16[2,768,2048]{2,1,0:T(8,128)(2,1)}, u32[]{:S(2)}, u32[]{:S(2)}) collective-permute-start(bf16[2,768,2048]{2,1,0:T(8,128)(2,1)} %all-gather.8.cloned.1.call-done), channel_id=1, source_target_pairs={{0,2},{2,4},{4,6},{6,8},{8,10},{10,12},{12,14},{14,16},{16,18},{18... | collective-permute-start | bytes 18874376 | tf_op jit(solution)/shard_map/ppermute | solution.py:13
  683.6 2.7 copy-start.1
Sparse Core Ops, SparseCore 0:
  9.1 111.7 all-gather.3
  122.7 110.0 all-gather.5
  241.7 86.4 all-gather.7
where the time goes:
time: 694 us; the launch traced here: 693 us
  waiting for transfers between devices  511 us (74%)
  matrix products  78.6 us (11%)
  local copies, waits for them, and re-layouts  66.5 us (10%)
  other arithmetic  14.6 us (2%)
  between operations  13.2 us (2%)
    ppermute x2, waiting for transfers between devices, from_behind(): lax.ppermute(value, axis, [(source, source + steps) for source in range(l...  206 us
    all_gather x1, waiting for transfers between devices, body(): lax.all_gather(w_key, 'fsdp', axis=0, tiled=True)  113 us
    all_gather x1, waiting for transfers between devices, body(): lax.all_gather(w_value, 'fsdp', axis=0, tiled=True)  105 us
    all_gather x1, waiting for transfers between devices, body(): own_unit = lax.all_gather(own_pair, 'fsdp', axis=1, tiled=True)  86.6 us
    sub x4, matrix products, attend_group(): scores - top_score  42 us
    dynamic_slice x8, local copies, waits for them, and re-layouts, attend_group(): lax.dynamic_slice_in_dim(key_flat, group_number * span, span, 1)  33.7 us
    dot_general x4, matrix products, attend_group(): jnp.einsum('hqk,khd->qhd', weights, value_part, preferred_element_type=jn...  23 us
  transfers between devices with their start and end apart: 5, of which 5 were waited for; matrix products, arithmetic and copies ran while one was open for 1% of the time, Pallas kernels for 0%

commit v1 on v0

v1 whole, which is shorter than its diff:
```python
import jax
import jax.numpy as jnp
from jax import lax
from jax.sharding import PartitionSpec as P

HD = 128
MEM = 2
GROUP = 2


def from_behind(value, axis, steps):
    count = lax.axis_size(axis)
    leading, last = (max(0, -steps), min(count, count - steps))
    return lax.ppermute(value, axis, [(source, source + steps) for source in range(leading, last)])


def swap_halves(value):
    return lax.ppermute(value, "fsdp", [(0, 1), (1, 0)])


def in_order(first_is_mine, mine, other, axis):
    lead = jnp.where(first_is_mine, mine, other)
    tail = jnp.where(first_is_mine, other, mine)
    return jnp.concatenate([lead, tail], axis=axis)


def attend_group(query_rows, key_flat, value_flat, allowed, group_number):
    span = GROUP * HD
    count = query_rows.shape[0]
    query_part = lax.dynamic_slice_in_dim(query_rows, group_number * span, span, 1).reshape(
        count, GROUP, HD
    )
    key_part = lax.dynamic_slice_in_dim(key_flat, group_number * span, span, 1).reshape(
        key_flat.shape[0], GROUP, HD
    )
    value_part = lax.dynamic_slice_in_dim(value_flat, group_number * span, span, 1).reshape(
        value_flat.shape[0], GROUP, HD
    )
    scores = jnp.einsum(
        "qhd,khd->hqk", query_part, key_part, preferred_element_type=jnp.float32
    ) * HD ** (-0.5)
    scores = jnp.where(allowed[None], scores, jnp.float32(-1e30))
    top_score = jnp.max(scores, axis=-1, keepdims=True)
    expo = jnp.where(allowed[None], jnp.exp(scores - top_score), jnp.float32(0.0))
    total = jnp.sum(expo, axis=-1)
    weights = expo.astype(jnp.bfloat16)
    mixed = jnp.einsum("hqk,khd->qhd", weights, value_part, preferred_element_type=jnp.float32)
    mixed = mixed / jnp.transpose(total)[:, :, None]
    return mixed.reshape(count, span).astype(jnp.bfloat16)


def body(hidden_states, queries, w_key, w_value):
    tok_rows = hidden_states.shape[0]
    width = w_key.shape[1]
    halves = lax.axis_size("fsdp")
    cols = width // halves
    half_number = lax.axis_index("fsdp")
    other_half = 1 - half_number
    first_is_mine = half_number == 0

    def mine_of(array):
        return lax.dynamic_slice_in_dim(array, half_number * cols, cols, 1)

    def theirs_of(array):
        return lax.dynamic_slice_in_dim(array, other_half * cols, cols, 1)

    key_got = swap_halves(theirs_of(w_key))
    value_got = swap_halves(theirs_of(w_value))
    hidden_got = swap_halves(hidden_states)
    query_got = swap_halves(theirs_of(queries))

    key_weights = in_order(first_is_mine, mine_of(w_key), key_got, 0)
    value_weights = in_order(first_is_mine, mine_of(w_value), value_got, 0)
    hidden_rows = in_order(first_is_mine, hidden_states, hidden_got, 0)
    query_rows = in_order(first_is_mine, mine_of(queries), query_got, 0)

    own_key = jnp.dot(hidden_rows, key_weights, preferred_element_type=jnp.float32).astype(jnp.bfloat16)
    own_value = jnp.dot(hidden_rows, value_weights, preferred_element_type=jnp.float32).astype(
        jnp.bfloat16
    )
    own_unit = jnp.stack([own_key, own_value])
    earlier = []
    for distance in range(1, MEM + 1):
        earlier.insert(0, from_behind(own_unit, "seg", distance))
    context = jnp.stack(earlier + [own_unit])
    seg_rows = context.shape[2]
    key_flat = context[:, 0].reshape((MEM + 1) * seg_rows, cols)
    value_flat = context[:, 1].reshape((MEM + 1) * seg_rows, cols)
    seg_number = lax.axis_index("seg")
    query_pos = jnp.arange(seg_rows, dtype=jnp.int32)
    key_pos = jnp.arange((MEM + 1) * seg_rows, dtype=jnp.int32)
    block_of = key_pos // seg_rows
    within = key_pos % seg_rows
    earlier_ok = (block_of < MEM) & (seg_number >= MEM - block_of)
    own_ok = (block_of == MEM)[None, :] & (within[None, :] <= query_pos[:, None])
    allowed = earlier_ok[None, :] | own_ok

    def one_group(group_number):
        return attend_group(query_rows, key_flat, value_flat, allowed, group_number)

    grouped = lax.map(one_group, jnp.arange(cols // (GROUP * HD), dtype=jnp.int32))
    attended = jnp.transpose(grouped, (1, 0, 2)).reshape(seg_rows, cols)
    mine_rows = lax.dynamic_slice_in_dim(attended, half_number * tok_rows, tok_rows, 0)
    their_rows = lax.dynamic_slice_in_dim(attended, other_half * tok_rows, tok_rows, 0)
    rows_got = swap_halves(their_rows)
    return in_order(first_is_mine, mine_rows, rows_got, 1)


def solution(mesh):
    placed = (P(("seg", "fsdp"), None), P(("seg", "fsdp"), None), P("fsdp", None), P("fsdp", None))
    return jax.shard_map(
        body, mesh=mesh, in_specs=placed, out_specs=P(("seg", "fsdp"), None), check_vma=False
    )
```

time: 694 us -> 403 us (0.58)
  waiting for transfers between devices: 511 us -> 256 us
  local copies, waits for them, and re-layouts: 66.5 us -> 40.9 us
  between operations: 13.2 us -> 0.13 us
  matrix products: 78.6 us -> 66.7 us
  other arithmetic: 14.6 us -> 23.4 us
    all_gather x3 -> x0, waiting for transfers between devices: 305 us -> none  [the longest x1 113 us: body(): lax.all_gather(w_key, 'fsdp', axis=0, tiled=True)]
    ppermute x0 -> x5, waiting for transfers between devices: none -> 256 us  [swap_halves(): return lax.ppermute(value, 'fsdp', [(0, 1), (1, 0)])]
    ppermute x2, waiting for transfers between devices: 206 us -> 0.01 us  [from_behind(): lax.ppermute(value, axis, [(source, source + steps) for source in range(l...]
    dynamic_slice x8, local copies, waits for them, and re-layouts: 33.7 us -> 13.4 us  [attend_group(): lax.dynamic_slice_in_dim(key_flat, group_number * span, span, 1)]
    select_n x0 -> x4, other arithmetic: none -> 7.83 us  [in_order(): lead = jnp.where(first_is_mine, mine, other)]
    dynamic_slice x4 -> x8, local copies, waits for them, and re-layouts: 2.33 us -> 9.82 us  [the longest x3 5.7 us: theirs_of(): return lax.dynamic_slice_in_dim(array, other_half * cols, cols, 1)]
    dynamic_slice x4, local copies, waits for them, and re-layouts: 10.1 us -> 2.88 us  [attend_group(): lax.dynamic_slice_in_dim(value_flat, group_number * span, span, 1)]
  transfers between devices with their start and end apart: 5 -> 7, of which waited for: 5 -> 4; matrix products, arithmetic and copies ran while one was open for 1% -> 2% of each run, Pallas kernels for 0% -> 0%
where the time goes in v1:
time: 403 us; the launch traced here: 402 us
  waiting for transfers between devices  256 us (64%)
  matrix products  66.7 us (17%)
  local copies, waits for them, and re-layouts  40.9 us (10%)
  other arithmetic  23.4 us (6%)
  starting transfers between devices  11.4 us (3%)
    ppermute x5, waiting for transfers between devices, swap_halves(): return lax.ppermute(value, 'fsdp', [(0, 1), (1, 0)])  256 us
    sub x4, matrix products, attend_group(): scores - top_score  38.3 us
    dot_general x4, matrix products, attend_group(): jnp.einsum('hqk,khd->qhd', weights, value_part, preferred_element_type=jn...  21.5 us
    dynamic_slice x8, local copies, waits for them, and re-layouts, attend_group(): lax.dynamic_slice_in_dim(key_flat, group_number * span, span, 1)  13.4 us
  transfers between devices with their start and end apart: 7, of which 4 were waited for; matrix products, arithmetic and copies ran while one was open for 2% of the time, Pallas kernels for 0%

profile of v1, /device:TPU:24, one launch (start us, length us, event | category | flops | bytes accessed | tf_op | source)
XLA Modules:
  0.0 401.7 jit_solution(17694478403239629191)
XLA Ops:
  0.0 3.3 constant_dynamic-slice_fusion.7
  3.3 1.5 collective-permute-start.1
  4.8 0.5 collective-permute-start
  5.3 1.5 constant_dynamic-slice_fusion.6
  6.8 1.5 collective-permute-start.2
  8.3 77.5 %collective-permute-done = bf16[384,2048]{1,0:T(8,128)(2,1)} collective-permute-done((bf16[384,2048]{1,0:T(8,128)(2,1)}, bf16[384,2048]{1,0:T(8,128)(2,1)}, u32[]{:S(2)}, u32[]{:S(2)}) %collective-permute-start) | collective-permute-done | bytes 1572896 | tf_op jit(solution)/shard_map/ppermute | solution.py:18
  85.8 2.1 broadcast_select_fusion.5
  87.9 41.7 %collective-permute-done.2 = bf16[1024,1024]{1,0:T(8,128)(2,1)} collective-permute-done((bf16[1024,1024]{1,0:T(8,128)(2,1)}, bf16[1024,1024]{1,0:T(8,128)(2,1)}, u32[]{:S(2)}, u32[]{:S(2)}) %collective-permute-start.2) | collective-permute-done | bytes 2097184 | tf_op jit(solution)/shard_map/ppermute | solution.py:18
  129.6 3.9 broadcast_select_fusion.1
  133.5 3.4 fusion.38
  136.9 3.4 fusion.41
  140.4 3.1 pad_maximum_fusion.2
  143.4 3.8 collective-permute-start.3
  147.3 1.9 collective-permute-start.4
  149.2 0.9 constant_dynamic-slice_fusion.5
  150.2 1.5 collective-permute-start.5
  151.7 118.5 %collective-permute-done.5 = bf16[384,1024]{1,0:T(8,128)(2,1)} collective-permute-done((bf16[384,1024]{1,0:T(8,128)(2,1)}, bf16[384,1024]{1,0:T(8,128)(2,1)}, u32[]{:S(2)}, u32[]{:S(2)}) %collective-permute-start.5) | collective-permute-done | bytes 786464 | tf_op jit(solution)/shard_map/ppermute | solution.py:18
  270.1 1.8 broadcast_select_fusion.9
  271.9 1.3 pad_maximum_fusion.9
  273.2 1.6 copy-done.3
  274.9 3.9 pad_maximum_fusion
  278.7 4.7 %fusion.56 = (bf16[3,1,768,1024]{3,2,1,0:T(8,128)(2,1)}, bf16[3,1,768,1024]{3,2,1,0:T(8,128)(2,1)}) fusion(bf16[3,2,768,1024]{3,2,1,0:T(8,128)(2,1)S(1)} %pad_maximum_fusion), kind=kLoop, calls=%fused_computation.73 | loop fusion | bytes 18874368 | tf_op jit(solution)/shard_map/slice | solution.py:87
  283.4 95.4 %while.11 = (s32[]{:T(128)}, bf16[4,768,256]{1,2,0:T(8,128)(2,1)}, s32[4]{0:T(128)S(1)}, bf16[2304,1024]{1,0:T(8,128)(2,1)}, bf16[768,1024]{1,0:T(8,128)(2,1)}, ...) while((s32[]{:T(128)}, bf16[4,768,256]{1,2,0:T(8,128)(2,1)}, ...), condition=%wide.region_3.4_spmd.clone, body=%wide.region_0.3_spmd.clone.sunk | while | flops 1838876928 | bytes 32663744 | solution.py:101
  283.4 0.6 dynamic_slice.68
  284.7 1.8 constant_dynamic-slice_fusion.10
  286.5 1.5 copy.26
  288.1 1.0 constant_dynamic-slice_fusion.11
  289.3 1.5 fusion.74
  290.8 9.6 %fusion.75 = (f32[2,768]{1,0:T(2,128)S(1)}, bf16[2,768,2304]{2,1,0:T(8,128)(2,1)}) fusion(pred[768,2304]{1,0:T(8,128)(4,1)S(1)} %fusion.74, bf16[768,2,128]{0,2,1:T(8,128)(2,1)S(1)} %bitcast.57, bf16[2304,2,128]{0,2,1:T(8,128)(2,1)} %bitcast.53), kind=kOutput, calls=%fused_computation.72.clone.1 | convolution fusion | flops 927205632 | bytes 10426368 | tf_op jit(solution)/shard_map/while/body/eval_jaxpr/sub | solution.py:44
  300.4 0.7 copy.24
  301.1 5.4 %fusion.76 = bf16[768,2,128]{0,2,1:T(8,128)(2,1)S(1)} fusion(bf16[2304,2,128]{0,2,1:T(8,128)(2,1)S(1)} %bitcast.54, bf16[2,768,2304]{2,1,0:T(8,128)(2,1)} %get-tuple-element.189, f32[768,2]{0,1:T(2,128)S(1)} %bitcast.60), kind=kOutput, calls=%fused_computation.16.clone.1 | convolution fusion | flops 906362880 | bytes 8656896 | tf_op jit(solution)/shard_map/while/body/eval_jaxpr/hqk,khd->qhd/dot_general | solution.py:47
  306.5 0.8 constant_dynamic-update-slice_fusion.2
  307.3 0.6 dynamic_slice.68
  308.6 1.8 constant_dynamic-slice_fusion.10
  310.4 1.5 copy.26
  311.9 1.0 constant_dynamic-slice_fusion.11
  313.1 1.5 fusion.74
  314.7 9.6 %fusion.75 = (f32[2,768]{1,0:T(2,128)S(1)}, bf16[2,768,2304]{2,1,0:T(8,128)(2,1)}) fusion(pred[768,2304]{1,0:T(8,128)(4,1)S(1)} %fusion.74, bf16[768,2,128]{0,2,1:T(8,128)(2,1)S(1)} %bitcast.57, bf16[2304,2,128]{0,2,1:T(8,128)(2,1)} %bitcast.53), kind=kOutput, calls=%fused_computation.72.clone.1 | convolution fusion | flops 927205632 | bytes 10426368 | tf_op jit(solution)/shard_map/while/body/eval_jaxpr/sub | solution.py:44
  324.2 0.7 copy.24
  325.0 5.4 %fusion.76 = bf16[768,2,128]{0,2,1:T(8,128)(2,1)S(1)} fusion(bf16[2304,2,128]{0,2,1:T(8,128)(2,1)S(1)} %bitcast.54, bf16[2,768,2304]{2,1,0:T(8,128)(2,1)} %get-tuple-element.189, f32[768,2]{0,1:T(2,128)S(1)} %bitcast.60), kind=kOutput, calls=%fused_computation.16.clone.1 | convolution fusion | flops 906362880 | bytes 8656896 | tf_op jit(solution)/shard_map/while/body/eval_jaxpr/hqk,khd->qhd/dot_general | solution.py:47
  330.4 0.8 constant_dynamic-update-slice_fusion.2
  331.1 0.6 dynamic_slice.68
  332.4 1.8 constant_dynamic-slice_fusion.10
  334.2 1.5 copy.26
  335.8 1.0 constant_dynamic-slice_fusion.11
  337.0 1.5 fusion.74
  338.5 9.6 %fusion.75 = (f32[2,768]{1,0:T(2,128)S(1)}, bf16[2,768,2304]{2,1,0:T(8,128)(2,1)}) fusion(pred[768,2304]{1,0:T(8,128)(4,1)S(1)} %fusion.74, bf16[768,2,128]{0,2,1:T(8,128)(2,1)S(1)} %bitcast.57, bf16[2304,2,128]{0,2,1:T(8,128)(2,1)} %bitcast.53), kind=kOutput, calls=%fused_computation.72.clone.1 | convolution fusion | flops 927205632 | bytes 10426368 | tf_op jit(solution)/shard_map/while/body/eval_jaxpr/sub | solution.py:44
  348.1 0.7 copy.24
  348.8 5.4 %fusion.76 = bf16[768,2,128]{0,2,1:T(8,128)(2,1)S(1)} fusion(bf16[2304,2,128]{0,2,1:T(8,128)(2,1)S(1)} %bitcast.54, bf16[2,768,2304]{2,1,0:T(8,128)(2,1)} %get-tuple-element.189, f32[768,2]{0,1:T(2,128)S(1)} %bitcast.60), kind=kOutput, calls=%fused_computation.16.clone.1 | convolution fusion | flops 906362880 | bytes 8656896 | tf_op jit(solution)/shard_map/while/body/eval_jaxpr/hqk,khd->qhd/dot_general | solution.py:47
  354.2 0.8 constant_dynamic-update-slice_fusion.2
  355.0 0.6 dynamic_slice.68
  356.3 1.8 constant_dynamic-slice_fusion.10
  358.1 1.5 copy.26
  359.6 1.0 constant_dynamic-slice_fusion.11
  360.8 1.5 fusion.74
  362.4 9.6 %fusion.75 = (f32[2,768]{1,0:T(2,128)S(1)}, bf16[2,768,2304]{2,1,0:T(8,128)(2,1)}) fusion(pred[768,2304]{1,0:T(8,128)(4,1)S(1)} %fusion.74, bf16[768,2,128]{0,2,1:T(8,128)(2,1)S(1)} %bitcast.57, bf16[2304,2,128]{0,2,1:T(8,128)(2,1)} %bitcast.53), kind=kOutput, calls=%fused_computation.72.clone.1 | convolution fusion | flops 927205632 | bytes 10426368 | tf_op jit(solution)/shard_map/while/body/eval_jaxpr/sub | solution.py:44
  372.0 0.7 copy.24
  372.7 5.4 %fusion.76 = bf16[768,2,128]{0,2,1:T(8,128)(2,1)S(1)} fusion(bf16[2304,2,128]{0,2,1:T(8,128)(2,1)S(1)} %bitcast.54, bf16[2,768,2304]{2,1,0:T(8,128)(2,1)} %get-tuple-element.189, f32[768,2]{0,1:T(2,128)S(1)} %bitcast.60), kind=kOutput, calls=%fused_computation.16.clone.1 | convolution fusion | flops 906362880 | bytes 8656896 | tf_op jit(solution)/shard_map/while/body/eval_jaxpr/hqk,khd->qhd/dot_general | solution.py:47
  378.1 0.8 constant_dynamic-update-slice_fusion.2
  378.9 1.5 constant_dynamic-slice_fusion.4
  380.4 0.3 copy.20
  380.7 0.6 collective-permute-start.6
  381.6 18.7 %collective-permute-done.6 = bf16[384,1024]{1,0:T(8,128)(2,1)S(1)} collective-permute-done((bf16[384,1024]{1,0:T(8,128)(2,1)S(1)}, bf16[384,1024]{1,0:T(8,128)(2,1)S(1)}, u32[]{:S(2)}, u32[]{:S(2)}) %collective-permute-start.6) | collective-permute-done | bytes 786464 | tf_op jit(solution)/shard_map/ppermute | solution.py:18
  400.4 1.2 pad_maximum_fusion.10
  (22 shorter events, 1.1 us)
Async XLA Ops:
  0.0 5.3 %copy-start.1 = (bf16[1024,2048]{1,0:T(8,128)(2,1)S(1)}, bf16[1024,2048]{1,0:T(8,128)(2,1)}, u32[]{:S(2)}) copy-start(bf16[1024,2048]{1,0:T(8,128)(2,1)} %param.9) | copy-start | bytes 12582916
  3.3 84.6 %collective-permute-start.1 = (bf16[1024,1024]{1,0:T(8,128)(2,1)}, bf16[1024,1024]{1,0:T(8,128)(2,1)S(1)}, u32[]{:S(2)}, u32[]{:S(2)}) collective-permute-start(bf16[1024,1024]{1,0:T(8,128)(2,1)} %constant_dynamic-slice_fusion.7), channel_id=1, source_target_pairs={{0,1},{1,0},{2,3},{3,2},{4,5},{5,4},{6,7},{7,6},{8,9},{9,8},{10,11... | collective-permute-start | bytes 6291464 | tf_op jit(solution)/shard_map/ppermute | solution.py:18
  4.8 81.0 %collective-permute-start = (bf16[384,2048]{1,0:T(8,128)(2,1)}, bf16[384,2048]{1,0:T(8,128)(2,1)}, u32[]{:S(2)}, u32[]{:S(2)}) collective-permute-start(bf16[384,2048]{1,0:T(8,128)(2,1)} %param.6), channel_id=1, source_target_pairs={{0,1},{1,0},{2,3},{3,2},{4,5},{5,4},{6,7},{7,6},{8,9},{9,8},{10,11... | collective-permute-start | bytes 4718600 | tf_op jit(solution)/shard_map/ppermute | solution.py:18
  6.8 122.8 %collective-permute-start.2 = (bf16[1024,1024]{1,0:T(8,128)(2,1)}, bf16[1024,1024]{1,0:T(8,128)(2,1)}, u32[]{:S(2)}, u32[]{:S(2)}) collective-permute-start(bf16[1024,1024]{1,0:T(8,128)(2,1)} %constant_dynamic-slice_fusion.6), channel_id=1, source_target_pairs={{0,1},{1,0},{2,3},{3,2},{4,5},{5,4},{6,7},{7,6},{8,9},{9,8},{10,11... | collective-permute-start | bytes 6291464 | tf_op jit(solution)/shard_map/ppermute | solution.py:18
  8.3 121.3 %copy-start.2 = (bf16[1024,2048]{1,0:T(8,128)(2,1)S(1)}, bf16[1024,2048]{1,0:T(8,128)(2,1)}, u32[]{:S(2)}) copy-start(bf16[1024,2048]{1,0:T(8,128)(2,1)} %param.9) | copy-start | bytes 12582916
  140.4 8.8 %copy-start.4 = (bf16[384,2048]{1,0:T(8,128)(2,1)S(1)}, bf16[384,2048]{1,0:T(8,128)(2,1)}, u32[]{:S(2)}) copy-start(bf16[384,2048]{1,0:T(8,128)(2,1)} %param.7) | copy-start | bytes 4718596
  143.4 129.8 %collective-permute-start.3 = (bf16[2,768,1024]{2,1,0:T(8,128)(2,1)}, bf16[2,768,1024]{2,1,0:T(8,128)(2,1)S(1)}, u32[]{:S(2)}, u32[]{:S(2)}) collective-permute-start(bf16[2,768,1024]{2,1,0:T(8,128)(2,1)} %get-tuple-element.112), channel_id=1, source_target_pairs={{0,4},{2,6},{4,8},{6,10},{8,12},{10,14},{12,16},{14,18},{16,20},{1... | collective-permute-start | bytes 9437192 | tf_op jit(solution)/shard_map/ppermute | solution.py:14
  147.3 125.9 %collective-permute-start.4 = (bf16[2,768,1024]{2,1,0:T(8,128)(2,1)}, bf16[2,768,1024]{2,1,0:T(8,128)(2,1)}, u32[]{:S(2)}, u32[]{:S(2)}) collective-permute-start(bf16[2,768,1024]{2,1,0:T(8,128)(2,1)} %get-tuple-element.112), channel_id=1, source_target_pairs={{0,2},{2,4},{4,6},{6,8},{8,10},{10,12},{12,14},{14,16},{16,18},{18... | collective-permute-start | bytes 9437192 | tf_op jit(solution)/shard_map/ppermute | solution.py:14
  150.2 120.0 %collective-permute-start.5 = (bf16[384,1024]{1,0:T(8,128)(2,1)}, bf16[384,1024]{1,0:T(8,128)(2,1)}, u32[]{:S(2)}, u32[]{:S(2)}) collective-permute-start(bf16[384,1024]{1,0:T(8,128)(2,1)} %constant_dynamic-slice_fusion.5), channel_id=1, source_target_pairs={{0,1},{1,0},{2,3},{3,2},{4,5},{5,4},{6,7},{7,6},{8,9},{9,8},{10,11... | collective-permute-start | bytes 2359304 | tf_op jit(solution)/shard_map/ppermute | solution.py:18
  271.9 3.0 copy-start
  273.2 1.7 copy-start.3
  380.7 19.7 %collective-permute-start.6 = (bf16[384,1024]{1,0:T(8,128)(2,1)S(1)}, bf16[384,1024]{1,0:T(8,128)(2,1)S(1)}, u32[]{:S(2)}, u32[]{:S(2)}) collective-permute-start(bf16[384,1024]{1,0:T(8,128)(2,1)S(1)} %copy.20), channel_id=1, source_target_pairs={{0,1},{1,0},{2,3},{3,2},{4,5},{5,4},{6,7},{7,6},{8,9},{9,8},{10,11... | collective-permute-start | bytes 2359304 | tf_op jit(solution)/shard_map/ppermute | solution.py:18

commit v2 on v1

v2 whole, which is shorter than its diff:
```python
import functools

import jax
import jax.numpy as jnp
from jax import lax
from jax.experimental import pallas as pl
from jax.experimental.pallas import tpu as pltpu
from jax.sharding import PartitionSpec as P

HD = 128
MEM = 2
QBLOCK = 384
INTERPRET = False


def from_behind(value, axis, steps):
    count = lax.axis_size(axis)
    leading, last = (max(0, -steps), min(count, count - steps))
    return lax.ppermute(value, axis, [(source, source + steps) for source in range(leading, last)])


def swap_halves(value):
    return lax.ppermute(value, "fsdp", [(0, 1), (1, 0)])


def in_order(first_is_mine, mine, other, axis):
    lead = jnp.where(first_is_mine, mine, other)
    tail = jnp.where(first_is_mine, other, mine)
    return jnp.concatenate([lead, tail], axis=axis)


def attention_kernel(seg_ref, q_ref, k2_ref, k1_ref, k0_ref, v2_ref, v1_ref, v0_ref, o_ref):
    block = pl.program_id(1)
    seg = seg_ref[0]
    query = q_ref[...]
    seg_rows = k0_ref.shape[0]
    count = query.shape[0]
    dims = (((1,), (1,)), ((), ()))

    def scores_of(key_ref):
        raw = lax.dot_general(query, key_ref[...], dims, preferred_element_type=jnp.float32)
        return raw * HD ** (-0.5)

    col = lax.broadcasted_iota(jnp.int32, (count, seg_rows), 1)
    row = lax.broadcasted_iota(jnp.int32, (count, seg_rows), 0) + block * count
    ok2 = col < jnp.where(seg >= 2, seg_rows, 0)
    ok1 = col < jnp.where(seg >= 1, seg_rows, 0)
    ok0 = col <= row
    low = jnp.float32(-1e30)
    s2 = jnp.where(ok2, scores_of(k2_ref), low)
    s1 = jnp.where(ok1, scores_of(k1_ref), low)
    s0 = jnp.where(ok0, scores_of(k0_ref), low)
    top = jnp.maximum(
        jnp.maximum(jnp.max(s2, axis=1, keepdims=True), jnp.max(s1, axis=1, keepdims=True)),
        jnp.max(s0, axis=1, keepdims=True),
    )
    e2 = jnp.where(ok2, jnp.exp(s2 - top), 0.0)
    e1 = jnp.where(ok1, jnp.exp(s1 - top), 0.0)
    e0 = jnp.where(ok0, jnp.exp(s0 - top), 0.0)
    total = (
        jnp.sum(e2, axis=1, keepdims=True)
        + jnp.sum(e1, axis=1, keepdims=True)
        + jnp.sum(e0, axis=1, keepdims=True)
    )
    mixed = jnp.dot(e2.astype(jnp.bfloat16), v2_ref[...], preferred_element_type=jnp.float32)
    mixed = mixed + jnp.dot(e1.astype(jnp.bfloat16), v1_ref[...], preferred_element_type=jnp.float32)
    mixed = mixed + jnp.dot(e0.astype(jnp.bfloat16), v0_ref[...], preferred_element_type=jnp.float32)
    o_ref[...] = (mixed / total).astype(o_ref.dtype)


def attend(seg_number, query_rows, keys, values):
    seg_rows, cols = query_rows.shape
    heads = cols // HD
    blocks = seg_rows // QBLOCK
    q_spec = pl.BlockSpec((QBLOCK, HD), lambda h, i, seg: (i, h))
    kv_spec = pl.BlockSpec((seg_rows, HD), lambda h, i, seg: (0, h))
    grid_spec = pltpu.PrefetchScalarGridSpec(
        num_scalar_prefetch=1,
        grid=(heads, blocks),
        in_specs=[q_spec] + [kv_spec] * 6,
        out_specs=q_spec,
    )
    return pl.pallas_call(
        attention_kernel,
        grid_spec=grid_spec,
        out_shape=jax.ShapeDtypeStruct((seg_rows, cols), jnp.bfloat16),
        interpret=INTERPRET,
    )(seg_number.reshape(1).astype(jnp.int32), query_rows, *keys, *values)


def body(hidden_states, queries, w_key, w_value):
    tok_rows = hidden_states.shape[0]
    width = w_key.shape[1]
    halves = lax.axis_size("fsdp")
    segs = lax.axis_size("seg")
    cols = width // halves
    piece = cols // 2
    half_number = lax.axis_index("fsdp")
    seg_number = lax.axis_index("seg")
    other_half = 1 - half_number
    first_is_mine = half_number == 0
    core = seg_number % 2
    is_key_core = core == 0

    def mine_of(array):
        return lax.dynamic_slice_in_dim(array, half_number * cols, cols, 1)

    def theirs_of(array):
        return lax.dynamic_slice_in_dim(array, other_half * cols, cols, 1)

    served = jnp.where(is_key_core, theirs_of(w_key), theirs_of(w_value))
    left_got = swap_halves(served[:, :piece])
    stride = segs // 8 if segs >= 16 else 0
    wrap_pairs = []
    for seg in range(segs):
        for half in range(halves):
            wrap_pairs.append(((seg ^ stride) * halves + (1 - half), seg * halves + half))
    right_got = lax.ppermute(served[:, piece:], ("seg", "fsdp"), wrap_pairs)
    piece_got = jnp.concatenate([left_got, right_got], axis=1)
    core_pairs = [(seg, seg ^ 1) for seg in range(segs)]
    piece_other = lax.ppermute(piece_got, "seg", core_pairs)
    key_got = jnp.where(is_key_core, piece_got, piece_other)
    value_got = jnp.where(is_key_core, piece_other, piece_got)

    hidden_got = swap_halves(hidden_states)
    query_got = swap_halves(theirs_of(queries))

    key_weights = in_order(first_is_mine, mine_of(w_key), key_got, 0)
    value_weights = in_order(first_is_mine, mine_of(w_value), value_got, 0)
    hidden_rows = in_order(first_is_mine, hidden_states, hidden_got, 0)
    query_rows = in_order(first_is_mine, mine_of(queries), query_got, 0)

    own_key = jnp.dot(hidden_rows, key_weights, preferred_element_type=jnp.float32).astype(jnp.bfloat16)
    own_value = jnp.dot(hidden_rows, value_weights, preferred_element_type=jnp.float32).astype(
        jnp.bfloat16
    )
    own_unit = jnp.stack([own_key, own_value])
    one_back = from_behind(own_unit, "seg", 1)
    even_two = lax.ppermute(own_unit, "seg", [(s, s + 2) for s in range(0, segs - 2, 2)])
    odd_two = lax.ppermute(one_back, "seg", [(s, s + 1) for s in range(0, segs - 1, 2)])
    two_back = jnp.where(is_key_core, even_two, odd_two)

    attended = attend(
        seg_number,
        query_rows,
        (two_back[0], one_back[0], own_unit[0]),
        (two_back[1], one_back[1], own_unit[1]),
    )
    mine_rows = lax.dynamic_slice_in_dim(attended, half_number * tok_rows, tok_rows, 0)
    their_rows = lax.dynamic_slice_in_dim(attended, other_half * tok_rows, tok_rows, 0)
    rows_got = swap_halves(their_rows)
    return in_order(first_is_mine, mine_rows, rows_got, 1)


def solution(mesh):
    placed = (P(("seg", "fsdp"), None), P(("seg", "fsdp"), None), P("fsdp", None), P("fsdp", None))
    return jax.shard_map(
        body, mesh=mesh, in_specs=placed, out_specs=P(("seg", "fsdp"), None), check_vma=False
    )
```

time: 403 us -> 248 us (0.62)
  waiting for transfers between devices: 256 us -> 149 us
  matrix products: 66.7 us -> 6.85 us
  Pallas kernels: 0 us -> 46.8 us
  local copies, waits for them, and re-layouts: 40.9 us -> 9.35 us
  other arithmetic: 23.4 us -> 16.4 us
    ppermute x5 -> x4, waiting for transfers between devices: 256 us -> 79.8 us  [swap_halves(): return lax.ppermute(value, 'fsdp', [(0, 1), (1, 0)])]
    ppermute x2 -> x1, waiting for transfers between devices: 0.01 us -> 68.3 us  [from_behind(): lax.ppermute(value, axis, [(source, source + steps) for source in range(l...]
    pallas_call x0 -> x1, Pallas kernels: none -> 46.8 us  [attend(): pl.pallas_call(attention_kernel, grid_spec=grid_spec, out_shape=jax.Shape...]
    sub x4 -> x0, matrix products: 38.3 us -> none  [attend_group(): scores - top_score]
    dynamic_slice x25 -> x1, local copies, waits for them, and re-layouts: 25.2 us -> 1.3 us  [body(): lax.dynamic_slice_in_dim(attended, other_half * tok_rows, tok_rows, 0)]
    dot_general x4 -> x0, matrix products: 21.5 us -> none  [attend_group(): jnp.einsum('hqk,khd->qhd', weights, value_part, preferred_element_type=jn...]
    ppermute x0 -> x4, starting transfers between devices: none -> 9.04 us  [the longest x1 3.83 us: body(): lax.ppermute(own_unit, 'seg', [(s, s + 2) for s in range(0, segs - 2, 2)])]
    or x4 -> x0, other arithmetic: 6.13 us -> none  [body(): allowed = earlier_ok[None, :] | own_ok]
  transfers between devices with their start and end apart: 7 -> 9, of which waited for: 4 -> 6; matrix products, arithmetic and copies ran while one was open for 2% -> 4% of each run, Pallas kernels for 0% -> 0%
where the time goes in v2:
time: 248 us; the launch traced here: 244 us
  waiting for transfers between devices  149 us (60%)
  Pallas kernels  46.8 us (19%)
  other arithmetic  16.4 us (7%)
  starting transfers between devices  15.3 us (6%)
  local copies, waits for them, and re-layouts  9.35 us (4%)
  matrix products  6.85 us (3%)
    ppermute x4, waiting for transfers between devices, swap_halves(): return lax.ppermute(value, 'fsdp', [(0, 1), (1, 0)])  79.8 us
    ppermute x1, waiting for transfers between devices, from_behind(): lax.ppermute(value, axis, [(source, source + steps) for source in range(l...  68.3 us
    pallas_call x1, Pallas kernels, attend(): pl.pallas_call(attention_kernel, grid_spec=grid_spec, out_shape=jax.Shape...  46.8 us
    select_n x4, other arithmetic, in_order(): lead = jnp.where(first_is_mine, mine, other)  8.21 us
  transfers between devices with their start and end apart: 9, of which 6 were waited for; matrix products, arithmetic and copies ran while one was open for 4% of the time, Pallas kernels for 0%

profile of v2, /device:TPU:24, one launch (start us, length us, event | category | flops | bytes accessed | tf_op | source)
XLA Modules:
  0.0 244.3 jit_solution(16316833457499913938)
XLA Ops:
  0.0 3.2 %dynamic-slice_select_fusion = bf16[1024,1024]{1,0:T(8,128)(2,1)S(1)} fusion(bf16[1024,2048]{1,0:T(8,128)(2,1)} %param.7, s32[]{:T(128)S(6)} %select_n.99, bf16[1024,2048]{1,0:T(8,128)(2,1)} %param.6, pred[]{:T(512)S(6)} %eq.9), kind=kLoop, calls=%fused_computation.11 | loop fusion | flops 1048576 | bytes 6291461 | tf_op jit(solution)/shard_map/jit(_where)/select_n | solution.py:111
  3.2 0.2 fusion.16
  3.4 1.6 collective-permute-start.2
  4.9 2.1 collective-permute-start.3
  7.0 0.6 collective-permute-start.1
  7.6 21.9 %collective-permute-done.2 = bf16[1024,512]{1,0:T(8,128)(2,1)S(1)} collective-permute-done((bf16[1024,512]{1,0:T(8,128)(2,1)S(1)}, bf16[1024,512]{1,0:T(8,128)(2,1)S(1)}, u32[]{:S(2)}, u32[]{:S(2)}) %collective-permute-start.2) | collective-permute-done | bytes 1048608 | tf_op jit(solution)/shard_map/ppermute | solution.py:23
  29.5 0.1 constant_dynamic-update-slice_fusion.1
  29.6 1.1 collective-permute-done.3
  30.8 0.1 constant_dynamic-update-slice_fusion
  30.9 0.1 collective-permute-start.4
  31.0 0.0 copy-start.3
  31.0 31.1 %collective-permute-done.1 = bf16[384,2048]{1,0:T(8,128)(2,1)} collective-permute-done((bf16[384,2048]{1,0:T(8,128)(2,1)}, bf16[384,2048]{1,0:T(8,128)(2,1)}, u32[]{:S(2)}, u32[]{:S(2)}) %collective-permute-start.1) | collective-permute-done | bytes 1572896 | tf_op jit(solution)/shard_map/ppermute | solution.py:23
  62.2 2.1 broadcast_select_fusion.8
  64.2 0.0 collective-permute-done.4
  64.3 0.0 copy-done.3
  64.3 4.0 %broadcast_select_fusion.6 = (bf16[1024,1024]{1,0:T(8,128)(2,1)S(1)}, bf16[1024,1024]{1,0:T(8,128)(2,1)S(1)}, bf16[1024,1024]{1,0:T(8,128)(2,1)S(1)}, bf16[1024,1024]{1,0:T(8,128)(2,1)S(1)}) fusion(pred[]{:T(512)S(6)} %eq.8, bf16[1024,2048]{1,0:T(8,128)(2,1)S(1)} %copy-done.3, s32[]{:T(128)S(6)} %select_n.98, ...), kind=kLoop, calls=%fused_computation.17 | loop fusion | flops 6291456 | bytes 16777222 | tf_op jit(solution)/shard_map/jit(_where)/select_n | solution.py:27
  68.2 3.4 %fusion.11.k0_ref = bf16[768,1024]{1,0:T(8,128)(2,1)S(1)} fusion(bf16[1024,1024]{1,0:T(8,128)(2,1)S(1)} %get-tuple-element.6, bf16[1024,1024]{1,0:T(8,128)(2,1)S(1)} %get-tuple-element.5, bf16[384,2048]{1,0:T(8,128)(2,1)S(1)} %get-tuple-element.16, bf16[384,2048]{1,0:T(8,128)(2,1)S(1)} %get-tuple-element.15), kind=kOutput, calls=%fused_computation.19 | convolution fusion | flops 3236691968 | bytes 8912896 | tf_op jit(solution)/shard_map/dot_general | solution.py:133
  71.7 0.0 copy-start
  71.7 3.4 %fusion.8.v0_ref = bf16[768,1024]{1,0:T(8,128)(2,1)S(1)} fusion(bf16[1024,1024]{1,0:T(8,128)(2,1)S(1)} %get-tuple-element.9, bf16[1024,1024]{1,0:T(8,128)(2,1)S(1)} %get-tuple-element.10, bf16[384,2048]{1,0:T(8,128)(2,1)S(1)} %get-tuple-element.16, bf16[384,2048]{1,0:T(8,128)(2,1)S(1)} %get-tuple-element.15), kind=kOutput, calls=%fused_computation.18 | convolution fusion | flops 3236691968 | bytes 8912896 | tf_op jit(solution)/shard_map/dot_general | solution.py:134
  75.1 0.0 copy-start.1
  75.1 0.0 copy-done
  75.1 0.0 copy-start.4
  75.2 0.3 pad_maximum_fusion.1
  75.5 0.8 copy-done.1
  76.3 1.9 collective-permute-start.6
  78.2 3.8 %collective-permute-start.5 = (bf16[2,768,1024]{2,1,0:T(8,128)(2,1)S(1)}, bf16[2,768,1024]{2,1,0:T(8,128)(2,1)}, u32[]{:S(2)}, u32[]{:S(2)}) collective-permute-start(bf16[2,768,1024]{2,1,0:T(8,128)(2,1)S(1)} %pad_maximum_fusion.1), channel_id=1, source_target_pairs={{0,4},{4,8},{8,12},{12,16},{16,20},{20,24},{24,28},{28,32},{32,36}... | collective-permute-start | bytes 9437192 | tf_op jit(solution)/shard_map/ppermute | solution.py:139
  82.0 68.3 %collective-permute-done.6 = bf16[2,768,1024]{2,1,0:T(8,128)(2,1)} collective-permute-done((bf16[2,768,1024]{2,1,0:T(8,128)(2,1)S(1)}, bf16[2,768,1024]{2,1,0:T(8,128)(2,1)}, u32[]{:S(2)}, u32[]{:S(2)}) %collective-permute-start.6) | collective-permute-done | bytes 3145760 | tf_op jit(solution)/shard_map/ppermute | solution.py:19
  150.4 3.0 %collective-permute-start.7 = (bf16[2,768,1024]{2,1,0:T(8,128)(2,1)}, bf16[2,768,1024]{2,1,0:T(8,128)(2,1)}, u32[]{:S(2)}, u32[]{:S(2)}) collective-permute-start(bf16[2,768,1024]{2,1,0:T(8,128)(2,1)} %collective-permute-done.6), channel_id=1, source_target_pairs={{0,2},{4,6},{8,10},{12,14},{16,18},{20,22},{24,26},{28,30},{32,34}... | collective-permute-start | bytes 9437192 | tf_op jit(solution)/shard_map/ppermute | solution.py:140
  153.4 0.0 copy-done.4
  153.4 1.0 constant_dynamic-slice_fusion.1
  154.4 0.7 collective-permute-start
  155.1 14.2 %collective-permute-done = bf16[384,1024]{1,0:T(8,128)(2,1)} collective-permute-done((bf16[384,1024]{1,0:T(8,128)(2,1)}, bf16[384,1024]{1,0:T(8,128)(2,1)}, u32[]{:S(2)}, u32[]{:S(2)}) %collective-permute-start) | collective-permute-done | bytes 786464 | tf_op jit(solution)/shard_map/ppermute | solution.py:23
  169.2 1.8 broadcast_select_fusion.12
  171.0 1.3 pad_maximum_fusion.8.q_ref
  172.3 3.8 %slice_bitcast_fusion = (bf16[768,1024]{1,0:T(8,128)(2,1)}, bf16[768,1024]{1,0:T(8,128)(2,1)}) fusion(bf16[2,768,1024]{2,1,0:T(8,128)(2,1)} %collective-permute-done.6), kind=kLoop, calls=%fused_computation.20 | loop fusion | bytes 6291456 | tf_op jit(solution)/shard_map/squeeze | solution.py:147
  176.1 0.0 collective-permute-done.5
  176.1 0.0 collective-permute-done.7
  176.1 2.2 broadcast_select_fusion
  178.3 2.0 slice_bitcast_fusion.1
  180.3 46.8 %shard_map.46 = bf16[768,1024]{1,0:T(8,128)(2,1)} custom-call(s32[1]{0:T(128)} %bitcast.seg_ref, bf16[768,1024]{1,0:T(8,128)(2,1)} %pad_maximum_fusion.8.q_ref, bf16[768,1024]{1,0:T(8,128)(2,1)} %get-tuple-element.14.k2_ref, bf16[768,1024]{1,0:T(8,128)(2,1)} %get-tuple-element.12.k1_ref, bf16[768,1024]{1,0:T(8,128)(2,1)} %copy-done, ...), custom_call_target="tpu_custom_call" | custom-call | tf_op jit(solution)/shard_map/pallas_call | solution.py:83
  227.1 0.0 copy-start.2
  227.1 1.3 constant_dynamic-slice_fusion
  228.4 1.5 collective-permute-start.8
  229.9 12.7 %collective-permute-done.8 = bf16[384,1024]{1,0:T(8,128)(2,1)S(1)} collective-permute-done((bf16[384,1024]{1,0:T(8,128)(2,1)S(1)}, bf16[384,1024]{1,0:T(8,128)(2,1)S(1)}, u32[]{:S(2)}, u32[]{:S(2)}) %collective-permute-start.8) | collective-permute-done | bytes 786464 | tf_op jit(solution)/shard_map/ppermute | solution.py:23
  242.6 0.0 copy-done.2
  242.6 0.4 broadcast_select_fusion.10
  243.0 1.2 pad_maximum_fusion.9
Async XLA Ops:
  3.4 26.1 %collective-permute-start.2 = (bf16[1024,512]{1,0:T(8,128)(2,1)S(1)}, bf16[1024,512]{1,0:T(8,128)(2,1)S(1)}, u32[]{:S(2)}, u32[]{:S(2)}) collective-permute-start(bf16[1024,512]{1,0:T(8,128)(2,1)S(1)} %get-tuple-element.22), channel_id=1, source_target_pairs={{0,1},{1,0},{2,3},{3,2},{4,5},{5,4},{6,7},{7,6},{8,9},{9,8},{10,11... | collective-permute-start | bytes 3145736 | tf_op jit(solution)/shard_map/ppermute | solution.py:23
  4.9 25.8 %collective-permute-start.3 = (bf16[1024,512]{1,0:T(8,128)(2,1)S(1)}, bf16[1024,512]{1,0:T(8,128)(2,1)S(1)}, u32[]{:S(2)}, u32[]{:S(2)}) collective-permute-start(bf16[1024,512]{1,0:T(8,128)(2,1)S(1)} %get-tuple-element.21), channel_id=1, source_target_pairs={{33,0},{32,1},{35,2},{34,3},{37,4},{36,5},{39,6},{38,7},{41,8},{40... | collective-permute-start | bytes 3145736 | tf_op jit(solution)/shard_map/ppermute | solution.py:118
  7.0 55.1 %collective-permute-start.1 = (bf16[384,2048]{1,0:T(8,128)(2,1)}, bf16[384,2048]{1,0:T(8,128)(2,1)}, u32[]{:S(2)}, u32[]{:S(2)}) collective-permute-start(bf16[384,2048]{1,0:T(8,128)(2,1)} %param.4), channel_id=1, source_target_pairs={{0,1},{1,0},{2,3},{3,2},{4,5},{5,4},{6,7},{7,6},{8,9},{9,8},{10,11... | collective-permute-start | bytes 4718600 | tf_op jit(solution)/shard_map/ppermute | solution.py:23
  30.9 33.3 %collective-permute-start.4 = (bf16[1024,1024]{1,0:T(8,128)(2,1)S(1)}, bf16[1024,1024]{1,0:T(8,128)(2,1)}, u32[]{:S(2)}, u32[]{:S(2)}) collective-permute-start(bf16[1024,1024]{1,0:T(8,128)(2,1)S(1)} %constant_dynamic-update-slice_fusion), channel_id=1, source_target_pairs={{0,2},{2,0},{4,6},{6,4},{8,10},{10,8},{12,14},{14,12},{16,18},{18,... | collective-permute-start | bytes 6291464 | tf_op jit(solution)/shard_map/ppermute | solution.py:121
  31.0 33.2 %copy-start.3 = (bf16[1024,2048]{1,0:T(8,128)(2,1)S(1)}, bf16[1024,2048]{1,0:T(8,128)(2,1)}, u32[]{:S(2)}) copy-start(bf16[1024,2048]{1,0:T(8,128)(2,1)} %param.6) | copy-start | bytes 12582916
  71.7 3.5 %copy-start = (bf16[768,1024]{1,0:T(8,128)(2,1)}, bf16[768,1024]{1,0:T(8,128)(2,1)S(1)}, u32[]{:S(2)}) copy-start(bf16[768,1024]{1,0:T(8,128)(2,1)S(1)} %fusion.11.k0_ref) | copy-start | bytes 4718596
  75.1 1.2 copy-start.1
  75.1 78.3 %copy-start.4 = (bf16[384,2048]{1,0:T(8,128)(2,1)S(1)}, bf16[384,2048]{1,0:T(8,128)(2,1)}, u32[]{:S(2)}) copy-start(bf16[384,2048]{1,0:T(8,128)(2,1)} %param.5) | copy-start | bytes 4718596
  76.3 74.1 %collective-permute-start.6 = (bf16[2,768,1024]{2,1,0:T(8,128)(2,1)S(1)}, bf16[2,768,1024]{2,1,0:T(8,128)(2,1)}, u32[]{:S(2)}, u32[]{:S(2)}) collective-permute-start(bf16[2,768,1024]{2,1,0:T(8,128)(2,1)S(1)} %pad_maximum_fusion.1), channel_id=1, source_target_pairs={{0,2},{2,4},{4,6},{6,8},{8,10},{10,12},{12,14},{14,16},{16,18},{18... | collective-permute-start | bytes 9437192 | tf_op jit(solution)/shard_map/ppermute | solution.py:19
  78.2 97.9 %collective-permute-start.5 = (bf16[2,768,1024]{2,1,0:T(8,128)(2,1)S(1)}, bf16[2,768,1024]{2,1,0:T(8,128)(2,1)}, u32[]{:S(2)}, u32[]{:S(2)}) collective-permute-start(bf16[2,768,1024]{2,1,0:T(8,128)(2,1)S(1)} %pad_maximum_fusion.1), channel_id=1, source_target_pairs={{0,4},{4,8},{8,12},{12,16},{16,20},{20,24},{24,28},{28,32},{32,36}... | collective-permute-start | bytes 9437192 | tf_op jit(solution)/shard_map/ppermute | solution.py:139
  150.4 25.7 %collective-permute-start.7 = (bf16[2,768,1024]{2,1,0:T(8,128)(2,1)}, bf16[2,768,1024]{2,1,0:T(8,128)(2,1)}, u32[]{:S(2)}, u32[]{:S(2)}) collective-permute-start(bf16[2,768,1024]{2,1,0:T(8,128)(2,1)} %collective-permute-done.6), channel_id=1, source_target_pairs={{0,2},{4,6},{8,10},{12,14},{16,18},{20,22},{24,26},{28,30},{32,34}... | collective-permute-start | bytes 9437192 | tf_op jit(solution)/shard_map/ppermute | solution.py:140
  154.4 14.9 %collective-permute-start = (bf16[384,1024]{1,0:T(8,128)(2,1)}, bf16[384,1024]{1,0:T(8,128)(2,1)}, u32[]{:S(2)}, u32[]{:S(2)}) collective-permute-start(bf16[384,1024]{1,0:T(8,128)(2,1)} %constant_dynamic-slice_fusion.1), channel_id=1, source_target_pairs={{0,1},{1,0},{2,3},{3,2},{4,5},{5,4},{6,7},{7,6},{8,9},{9,8},{10,11... | collective-permute-start | bytes 2359304 | tf_op jit(solution)/shard_map/ppermute | solution.py:23
  227.1 15.5 %copy-start.2 = (bf16[768,1024]{1,0:T(8,128)(2,1)S(1)}, bf16[768,1024]{1,0:T(8,128)(2,1)}, u32[]{:S(2)}) copy-start(bf16[768,1024]{1,0:T(8,128)(2,1)} %shard_map.46) | copy-start | bytes 4718596
  228.4 14.2 %collective-permute-start.8 = (bf16[384,1024]{1,0:T(8,128)(2,1)S(1)}, bf16[384,1024]{1,0:T(8,128)(2,1)S(1)}, u32[]{:S(2)}, u32[]{:S(2)}) collective-permute-start(bf16[384,1024]{1,0:T(8,128)(2,1)S(1)} %constant_dynamic-slice_fusion), channel_id=1, source_target_pairs={{0,1},{1,0},{2,3},{3,2},{4,5},{5,4},{6,7},{7,6},{8,9},{9,8},{10,11... | collective-permute-start | bytes 2359304 | tf_op jit(solution)/shard_map/ppermute | solution.py:23

commit v3 on v2

--- a/solution.py
+++ b/solution.py
@@ -30,8 +30,8 @@
 
 
 def attention_kernel(seg_ref, q_ref, k2_ref, k1_ref, k0_ref, v2_ref, v1_ref, v0_ref, o_ref):
-    block = pl.program_id(1)
     seg = seg_ref[0]
+    first_row = seg_ref[1]
     query = q_ref[...]
     seg_rows = k0_ref.shape[0]
     count = query.shape[0]
@@ -42,7 +42,7 @@
         return raw * HD ** (-0.5)
 
     col = lax.broadcasted_iota(jnp.int32, (count, seg_rows), 1)
-    row = lax.broadcasted_iota(jnp.int32, (count, seg_rows), 0) + block * count
+    row = lax.broadcasted_iota(jnp.int32, (count, seg_rows), 0) + first_row
     ok2 = col < jnp.where(seg >= 2, seg_rows, 0)
     ok1 = col < jnp.where(seg >= 1, seg_rows, 0)
     ok0 = col <= row
@@ -68,24 +68,25 @@
     o_ref[...] = (mixed / total).astype(o_ref.dtype)
 
 
-def attend(seg_number, query_rows, keys, values):
-    seg_rows, cols = query_rows.shape
+def attend(seg_number, first_row, query_rows, keys, values):
+    count, cols = query_rows.shape
+    seg_rows = keys[0].shape[0]
     heads = cols // HD
-    blocks = seg_rows // QBLOCK
-    q_spec = pl.BlockSpec((QBLOCK, HD), lambda h, i, seg: (i, h))
-    kv_spec = pl.BlockSpec((seg_rows, HD), lambda h, i, seg: (0, h))
+    q_spec = pl.BlockSpec((count, HD), lambda h, scalars: (0, h))
+    kv_spec = pl.BlockSpec((seg_rows, HD), lambda h, scalars: (0, h))
     grid_spec = pltpu.PrefetchScalarGridSpec(
         num_scalar_prefetch=1,
-        grid=(heads, blocks),
+        grid=(heads,),
         in_specs=[q_spec] + [kv_spec] * 6,
         out_specs=q_spec,
     )
+    scalars = jnp.stack([seg_number, first_row]).astype(jnp.int32)
     return pl.pallas_call(
         attention_kernel,
         grid_spec=grid_spec,
-        out_shape=jax.ShapeDtypeStruct((seg_rows, cols), jnp.bfloat16),
+        out_shape=jax.ShapeDtypeStruct((count, cols), jnp.bfloat16),
         interpret=INTERPRET,
-    )(seg_number.reshape(1).astype(jnp.int32), query_rows, *keys, *values)
+    )(scalars, query_rows, *keys, *values)
 
 
 def body(hidden_states, queries, w_key, w_value):
@@ -123,32 +124,35 @@
     value_got = jnp.where(is_key_core, piece_other, piece_got)
 
     hidden_got = swap_halves(hidden_states)
-    query_got = swap_halves(theirs_of(queries))
 
     key_weights = in_order(first_is_mine, mine_of(w_key), key_got, 0)
     value_weights = in_order(first_is_mine, mine_of(w_value), value_got, 0)
     hidden_rows = in_order(first_is_mine, hidden_states, hidden_got, 0)
-    query_rows = in_order(first_is_mine, mine_of(queries), query_got, 0)
 
     own_key = jnp.dot(hidden_rows, key_weights, preferred_element_type=jnp.float32).astype(jnp.bfloat16)
     own_value = jnp.dot(hidden_rows, value_weights, preferred_element_type=jnp.float32).astype(
         jnp.bfloat16
     )
-    own_unit = jnp.stack([own_key, own_value])
-    one_back = from_behind(own_unit, "seg", 1)
-    even_two = lax.ppermute(own_unit, "seg", [(s, s + 2) for s in range(0, segs - 2, 2)])
-    odd_two = lax.ppermute(one_back, "seg", [(s, s + 1) for s in range(0, segs - 1, 2)])
-    two_back = jnp.where(is_key_core, even_two, odd_two)
+    query_sent, own_key, own_value = lax.optimization_barrier((theirs_of(queries), own_key, own_value))
+    query_got = swap_halves(query_sent)
 
-    attended = attend(
-        seg_number,
-        query_rows,
-        (two_back[0], one_back[0], own_unit[0]),
-        (two_back[1], one_back[1], own_unit[1]),
-    )
-    mine_rows = lax.dynamic_slice_in_dim(attended, half_number * tok_rows, tok_rows, 0)
-    their_rows = lax.dynamic_slice_in_dim(attended, other_half * tok_rows, tok_rows, 0)
+    even_pairs = [(s, s + 2) for s in range(0, segs - 2, 2)]
+    forward_pairs = [(s, s + 1) for s in range(0, segs - 1, 2)]
+
+    def shifted(own):
+        one = from_behind(own, "seg", 1)
+        even_two = lax.ppermute(own, "seg", even_pairs)
+        odd_two = lax.ppermute(one, "seg", forward_pairs)
+        return jnp.where(is_key_core, even_two, odd_two), one
+
+    key_two, key_one = shifted(own_key)
+    value_two, value_one = shifted(own_value)
+    keys = (key_two, key_one, own_key)
+    values = (value_two, value_one, own_value)
+
+    their_rows = attend(seg_number, other_half * tok_rows, query_got, keys, values)
     rows_got = swap_halves(their_rows)
+    mine_rows = attend(seg_number, half_number * tok_rows, mine_of(queries), keys, values)
     return in_order(first_is_mine, mine_rows, rows_got, 1)
 
 

time: 248 us -> 224 us (0.903)
  waiting for transfers between devices: 149 us -> 121 us
  starting transfers between devices: 15.3 us -> 23.4 us
  local copies, waits for them, and re-layouts: 9.35 us -> 3.28 us
  Pallas kernels: 46.8 us -> 50 us
    ppermute x4, waiting for transfers between devices: 79.8 us -> 62.5 us  [swap_halves(): return lax.ppermute(value, 'fsdp', [(0, 1), (1, 0)])]
    ppermute x1 -> x2, waiting for transfers between devices: 68.3 us -> 56.7 us  [from_behind(): lax.ppermute(value, axis, [(source, source + steps) for source in range(l...]
    squeeze x2 -> x0, local copies, waits for them, and re-layouts: 5.79 us -> none  [the longest x1 3.82 us: body(): one_back[1]]
    ppermute x1 -> x2, starting transfers between devices: 1.91 us -> 5.85 us  [from_behind(): lax.ppermute(value, axis, [(source, source + steps) for source in range(l...]
    ppermute x2 -> x4, starting transfers between devices: 6.84 us -> 10.6 us  [the longest x2 5.74 us: shifted(): even_two = lax.ppermute(own, 'seg', even_pairs)]
    select_n x1 -> x2, other arithmetic: 2.22 us -> 5.44 us  [shifted(): return (jnp.where(is_key_core, even_two, odd_two), one)]
    pallas_call x1 -> x2, Pallas kernels: 46.8 us -> 50 us  [attend(): pl.pallas_call(attention_kernel, grid_spec=grid_spec, out_shape=jax.Shape...]
    select_n x4 -> x3, other arithmetic: 8.21 us -> 7.01 us  [in_order(): lead = jnp.where(first_is_mine, mine, other)]
  transfers between devices with their start and end apart: 9 -> 12, of which waited for: 6 -> 7; matrix products, arithmetic and copies ran while one was open for 4% -> 5% of each run, Pallas kernels for 0% -> 11%
where the time goes in v3:
time: 224 us; the launch traced here: 222 us
  waiting for transfers between devices  121 us (54%)
  Pallas kernels  50 us (22%)
  starting transfers between devices  23.4 us (10%)
  other arithmetic  18.2 us (8%)
  matrix products  6.85 us (3%)
  local copies, waits for them, and re-layouts  3.28 us (1%)
    ppermute x4, waiting for transfers between devices, swap_halves(): return lax.ppermute(value, 'fsdp', [(0, 1), (1, 0)])  62.5 us
    ppermute x2, waiting for transfers between devices, from_behind(): lax.ppermute(value, axis, [(source, source + steps) for source in range(l...  56.7 us
    pallas_call x2, Pallas kernels, attend(): pl.pallas_call(attention_kernel, grid_spec=grid_spec, out_shape=jax.Shape...  50 us
    select_n x3, other arithmetic, in_order(): lead = jnp.where(first_is_mine, mine, other)  7.01 us
    ppermute x2, starting transfers between devices, from_behind(): lax.ppermute(value, axis, [(source, source + steps) for source in range(l...  5.85 us
    ppermute x2, starting transfers between devices, shifted(): even_two = lax.ppermute(own, 'seg', even_pairs)  5.74 us
    select_n x2, other arithmetic, shifted(): return (jnp.where(is_key_core, even_two, odd_two), one)  5.44 us
    ppermute x2, starting transfers between devices, shifted(): odd_two = lax.ppermute(one, 'seg', forward_pairs)  4.89 us
  transfers between devices with their start and end apart: 12, of which 7 were waited for; matrix products, arithmetic and copies ran while one was open for 5% of the time, Pallas kernels for 11%

profile of v3, /device:TPU:24, one launch (start us, length us, event | category | flops | bytes accessed | tf_op | source)
XLA Modules:
  0.0 222.4 jit_solution(11105588213921576573)
XLA Ops:
  0.0 3.2 %dynamic-slice_select_fusion = bf16[1024,1024]{1,0:T(8,128)(2,1)S(1)} fusion(bf16[1024,2048]{1,0:T(8,128)(2,1)} %param.7, s32[]{:T(128)S(6)} %select_n.91, bf16[1024,2048]{1,0:T(8,128)(2,1)} %param.6, pred[]{:T(512)S(6)} %eq.9), kind=kLoop, calls=%fused_computation.9 | loop fusion | flops 1048576 | bytes 6291461 | tf_op jit(solution)/shard_map/jit(_where)/select_n | solution.py:112
  3.2 0.2 fusion.16
  3.4 1.6 collective-permute-start.1
  4.9 2.1 collective-permute-start.2
  7.0 0.6 collective-permute-start
  7.6 21.9 %collective-permute-done.1 = bf16[1024,512]{1,0:T(8,128)(2,1)S(1)} collective-permute-done((bf16[1024,512]{1,0:T(8,128)(2,1)S(1)}, bf16[1024,512]{1,0:T(8,128)(2,1)S(1)}, u32[]{:S(2)}, u32[]{:S(2)}) %collective-permute-start.1) | collective-permute-done | bytes 1048608 | tf_op jit(solution)/shard_map/ppermute | solution.py:23
  29.5 0.1 constant_dynamic-update-slice_fusion.1
  29.6 1.1 collective-permute-done.2
  30.8 0.1 constant_dynamic-update-slice_fusion
  30.9 0.1 collective-permute-start.3
  31.0 0.0 copy-start.3
  31.0 2.8 %constant_dynamic-slice_fusion.1 = (bf16[384,1024]{1,0:T(8,128)(2,1)}, bf16[384,1024]{1,0:T(8,128)(2,1)}) fusion(bf16[384,2048]{1,0:T(8,128)(2,1)} %param.5, s32[]{:T(128)S(6)} %select_n.88, s32[]{:T(128)S(6)} %select_n.91), kind=kLoop, calls=%fused_computation.28 | loop fusion | bytes 3145736 | tf_op jit(solution)/shard_map/dynamic_slice | solution.py:107
  33.8 0.0 copy-start.2
  33.8 28.3 %collective-permute-done = bf16[384,2048]{1,0:T(8,128)(2,1)} collective-permute-done((bf16[384,2048]{1,0:T(8,128)(2,1)}, bf16[384,2048]{1,0:T(8,128)(2,1)}, u32[]{:S(2)}, u32[]{:S(2)}) %collective-permute-start) | collective-permute-done | bytes 1572896 | tf_op jit(solution)/shard_map/ppermute | solution.py:23
  62.2 2.1 broadcast_select_fusion.7
  64.2 0.0 collective-permute-done.3
  64.3 0.0 copy-done.3
  64.3 0.0 copy-done.2
  64.3 3.7 %broadcast_select_fusion.3 = (bf16[1024,1024]{1,0:T(8,128)(2,1)S(1)}, bf16[1024,1024]{1,0:T(8,128)(2,1)S(1)}, bf16[1024,1024]{1,0:T(8,128)(2,1)S(1)}, bf16[1024,1024]{1,0:T(8,128)(2,1)S(1)}) fusion(pred[]{:T(512)S(6)} %eq.8, bf16[1024,2048]{1,0:T(8,128)(2,1)S(1)} %copy-done.2, s32[]{:T(128)S(6)} %select_n.88, bf16[1024,1024]{1,0:T(8,128)(2,1)} %collective-permute-done.3, ...), kind=kLoop, calls=%fused_computation.13 | loop fusion | flops 6291456 | bytes 16777222 | tf_op jit(solution)/shard_map/jit(_where)/select_n | solution.py:27
  68.0 3.4 %fusion.8.v0_ref = bf16[768,1024]{1,0:T(8,128)(2,1)S(1)} fusion(bf16[1024,1024]{1,0:T(8,128)(2,1)S(1)} %get-tuple-element.12, bf16[1024,1024]{1,0:T(8,128)(2,1)S(1)} %get-tuple-element.11, bf16[384,2048]{1,0:T(8,128)(2,1)S(1)} %get-tuple-element.18, bf16[384,2048]{1,0:T(8,128)(2,1)S(1)} %get-tuple-element.17), kind=kOutput, calls=%fused_computation.16 | convolution fusion | flops 3236691968 | bytes 8912896 | tf_op jit(solution)/shard_map/dot_general | solution.py:133
  71.4 0.0 copy-start
  71.4 3.4 %fusion.11.k0_ref = bf16[768,1024]{1,0:T(8,128)(2,1)S(1)} fusion(bf16[1024,1024]{1,0:T(8,128)(2,1)S(1)} %get-tuple-element.15, bf16[1024,1024]{1,0:T(8,128)(2,1)S(1)} %get-tuple-element.16, bf16[384,2048]{1,0:T(8,128)(2,1)S(1)} %get-tuple-element.18, bf16[384,2048]{1,0:T(8,128)(2,1)S(1)} %get-tuple-element.17), kind=kOutput, calls=%fused_computation.17 | convolution fusion | flops 3236691968 | bytes 8912896 | tf_op jit(solution)/shard_map/dot_general | solution.py:132
  74.8 0.0 copy-start.1
  74.9 1.9 collective-permute-start.8
  76.8 3.9 %collective-permute-start.5 = (bf16[768,1024]{1,0:T(8,128)(2,1)S(1)}, bf16[768,1024]{1,0:T(8,128)(2,1)}, u32[]{:S(2)}, u32[]{:S(2)}) collective-permute-start(bf16[768,1024]{1,0:T(8,128)(2,1)S(1)} %fusion.11.k0_ref), channel_id=1, source_target_pairs={{0,2},{2,4},{4,6},{6,8},{8,10},{10,12},{12,14},{14,16},{16,18},{18... | collective-permute-start | bytes 4718600 | tf_op jit(solution)/shard_map/ppermute | solution.py:19
  80.7 0.0 copy-done
  80.7 3.8 %collective-permute-start.7 = (bf16[768,1024]{1,0:T(8,128)(2,1)S(1)}, bf16[768,1024]{1,0:T(8,128)(2,1)}, u32[]{:S(2)}, u32[]{:S(2)}) collective-permute-start(bf16[768,1024]{1,0:T(8,128)(2,1)S(1)} %fusion.8.v0_ref), channel_id=1, source_target_pairs={{0,4},{4,8},{8,12},{12,16},{16,20},{20,24},{24,28},{28,32},{32,36}... | collective-permute-start | bytes 4718600 | tf_op jit(solution)/shard_map/ppermute | solution.py:144
  84.6 28.7 %collective-permute-done.8.v1_ref = bf16[768,1024]{1,0:T(8,128)(2,1)} collective-permute-done((bf16[768,1024]{1,0:T(8,128)(2,1)S(1)}, bf16[768,1024]{1,0:T(8,128)(2,1)}, u32[]{:S(2)}, u32[]{:S(2)}) %collective-permute-start.8) | collective-permute-done | bytes 1572896 | tf_op jit(solution)/shard_map/ppermute | solution.py:19
  113.3 2.5 %collective-permute-start.9 = (bf16[768,1024]{1,0:T(8,128)(2,1)}, bf16[768,1024]{1,0:T(8,128)(2,1)}, u32[]{:S(2)}, u32[]{:S(2)}) collective-permute-start(bf16[768,1024]{1,0:T(8,128)(2,1)} %collective-permute-done.8.v1_ref), channel_id=1, source_target_pairs={{0,2},{4,6},{8,10},{12,14},{16,18},{20,22},{24,26},{28,30},{32,34}... | collective-permute-start | bytes 4718600 | tf_op jit(solution)/shard_map/ppermute | solution.py:145
  115.7 1.9 collective-permute-start.4
  117.7 28.0 %collective-permute-done.5.k1_ref = bf16[768,1024]{1,0:T(8,128)(2,1)} collective-permute-done((bf16[768,1024]{1,0:T(8,128)(2,1)S(1)}, bf16[768,1024]{1,0:T(8,128)(2,1)}, u32[]{:S(2)}, u32[]{:S(2)}) %collective-permute-start.5) | collective-permute-done | bytes 1572896 | tf_op jit(solution)/shard_map/ppermute | solution.py:19
  145.7 2.4 %collective-permute-start.6 = (bf16[768,1024]{1,0:T(8,128)(2,1)}, bf16[768,1024]{1,0:T(8,128)(2,1)}, u32[]{:S(2)}, u32[]{:S(2)}) collective-permute-start(bf16[768,1024]{1,0:T(8,128)(2,1)} %collective-permute-done.5.k1_ref), channel_id=1, source_target_pairs={{0,2},{4,6},{8,10},{12,14},{16,18},{20,22},{24,26},{28,30},{32,34}... | collective-permute-start | bytes 4718600 | tf_op jit(solution)/shard_map/ppermute | solution.py:145
  148.1 1.1 collective-permute-start.10
  149.2 0.7 pad_add_fusion.1.seg_ref
  149.9 0.0 collective-permute-done.7
  149.9 0.0 collective-permute-done.9
  149.9 2.7 %broadcast_select_fusion.8.v2_ref = bf16[768,1024]{1,0:T(8,128)(2,1)} fusion(bf16[768,1024]{1,0:T(8,128)(2,1)} %collective-permute-done.7, bf16[768,1024]{1,0:T(8,128)(2,1)} %collective-permute-done.9, pred[]{:T(512)S(6)} %eq.9), kind=kLoop, calls=%fused_computation.21 | loop fusion | flops 786432 | bytes 4718593 | tf_op jit(solution)/shard_map/jit(_where)/select_n | solution.py:146
  152.6 0.0 copy-done.1
  152.6 0.1 collective-permute-done.4
  152.7 0.0 collective-permute-done.6
  152.7 2.7 %broadcast_select_fusion.9.k2_ref = bf16[768,1024]{1,0:T(8,128)(2,1)} fusion(bf16[768,1024]{1,0:T(8,128)(2,1)} %collective-permute-done.4, bf16[768,1024]{1,0:T(8,128)(2,1)} %collective-permute-done.6, pred[]{:T(512)S(6)} %eq.9), kind=kLoop, calls=%fused_computation.22 | loop fusion | flops 786432 | bytes 4718593 | tf_op jit(solution)/shard_map/jit(_where)/select_n | solution.py:146
  155.4 12.4 %collective-permute-done.10.q_ref = bf16[384,1024]{1,0:T(8,128)(2,1)} collective-permute-done((bf16[384,1024]{1,0:T(8,128)(2,1)}, bf16[384,1024]{1,0:T(8,128)(2,1)}, u32[]{:S(2)}, u32[]{:S(2)}) %collective-permute-start.10) | collective-permute-done | bytes 786464 | tf_op jit(solution)/shard_map/ppermute | solution.py:23
  167.8 25.0 %shard_map.47 = bf16[384,1024]{1,0:T(8,128)(2,1)} custom-call(s32[2]{0:T(128)} %pad_add_fusion.1.seg_ref, bf16[384,1024]{1,0:T(8,128)(2,1)} %collective-permute-done.10.q_ref, bf16[768,1024]{1,0:T(8,128)(2,1)} %broadcast_select_fusion.9.k2_ref, bf16[768,1024]{1,0:T(8,128)(2,1)} %collective-permute-done.5.k1_ref, bf16[768,1024]{1,0:T(8,128)(2,1)} %copy-done.1, ...), custom_call_target="tpu_custom_call" | custom-call | tf_op jit(solution)/shard_map/pallas_call | solution.py:84
  192.8 1.4 collective-permute-start.11
  194.3 0.6 pad_add_fusion.seg_ref
  194.9 25.0 %shard_map.46 = bf16[384,1024]{1,0:T(8,128)(2,1)} custom-call(s32[2]{0:T(128)} %pad_add_fusion.seg_ref, bf16[384,1024]{1,0:T(8,128)(2,1)} %get-tuple-element.23.q_ref, bf16[768,1024]{1,0:T(8,128)(2,1)} %broadcast_select_fusion.9.k2_ref, bf16[768,1024]{1,0:T(8,128)(2,1)} %collective-permute-done.5.k1_ref, bf16[768,1024]{1,0:T(8,128)(2,1)} %copy-done.1, ...), custom_call_target="tpu_custom_call" | custom-call | tf_op jit(solution)/shard_map/pallas_call | solution.py:84
  219.9 0.0 collective-permute-done.11
  219.9 1.2 broadcast_select_fusion.11
  221.2 1.2 pad_maximum_fusion.7
Async XLA Ops:
  3.4 26.1 %collective-permute-start.1 = (bf16[1024,512]{1,0:T(8,128)(2,1)S(1)}, bf16[1024,512]{1,0:T(8,128)(2,1)S(1)}, u32[]{:S(2)}, u32[]{:S(2)}) collective-permute-start(bf16[1024,512]{1,0:T(8,128)(2,1)S(1)} %get-tuple-element.20), channel_id=1, source_target_pairs={{0,1},{1,0},{2,3},{3,2},{4,5},{5,4},{6,7},{7,6},{8,9},{9,8},{10,11... | collective-permute-start | bytes 3145736 | tf_op jit(solution)/shard_map/ppermute | solution.py:23
  4.9 25.8 %collective-permute-start.2 = (bf16[1024,512]{1,0:T(8,128)(2,1)S(1)}, bf16[1024,512]{1,0:T(8,128)(2,1)S(1)}, u32[]{:S(2)}, u32[]{:S(2)}) collective-permute-start(bf16[1024,512]{1,0:T(8,128)(2,1)S(1)} %get-tuple-element.19), channel_id=1, source_target_pairs={{33,0},{32,1},{35,2},{34,3},{37,4},{36,5},{39,6},{38,7},{41,8},{40... | collective-permute-start | bytes 3145736 | tf_op jit(solution)/shard_map/ppermute | solution.py:119
  7.0 55.1 %collective-permute-start = (bf16[384,2048]{1,0:T(8,128)(2,1)}, bf16[384,2048]{1,0:T(8,128)(2,1)}, u32[]{:S(2)}, u32[]{:S(2)}) collective-permute-start(bf16[384,2048]{1,0:T(8,128)(2,1)} %param.4), channel_id=1, source_target_pairs={{0,1},{1,0},{2,3},{3,2},{4,5},{5,4},{6,7},{7,6},{8,9},{9,8},{10,11... | collective-permute-start | bytes 4718600 | tf_op jit(solution)/shard_map/ppermute | solution.py:23
  30.9 33.3 %collective-permute-start.3 = (bf16[1024,1024]{1,0:T(8,128)(2,1)S(1)}, bf16[1024,1024]{1,0:T(8,128)(2,1)}, u32[]{:S(2)}, u32[]{:S(2)}) collective-permute-start(bf16[1024,1024]{1,0:T(8,128)(2,1)S(1)} %constant_dynamic-update-slice_fusion), channel_id=1, source_target_pairs={{0,2},{2,0},{4,6},{6,4},{8,10},{10,8},{12,14},{14,12},{16,18},{18,... | collective-permute-start | bytes 6291464 | tf_op jit(solution)/shard_map/ppermute | solution.py:122
  31.0 33.2 %copy-start.3 = (bf16[1024,2048]{1,0:T(8,128)(2,1)S(1)}, bf16[1024,2048]{1,0:T(8,128)(2,1)}, u32[]{:S(2)}) copy-start(bf16[1024,2048]{1,0:T(8,128)(2,1)} %param.6) | copy-start | bytes 12582916
  33.8 30.4 %copy-start.2 = (bf16[1024,2048]{1,0:T(8,128)(2,1)S(1)}, bf16[1024,2048]{1,0:T(8,128)(2,1)}, u32[]{:S(2)}) copy-start(bf16[1024,2048]{1,0:T(8,128)(2,1)} %param.7) | copy-start | bytes 12582916
  71.4 9.3 %copy-start = (bf16[768,1024]{1,0:T(8,128)(2,1)}, bf16[768,1024]{1,0:T(8,128)(2,1)S(1)}, u32[]{:S(2)}) copy-start(bf16[768,1024]{1,0:T(8,128)(2,1)S(1)} %fusion.8.v0_ref) | copy-start | bytes 4718596
  74.8 77.8 %copy-start.1 = (bf16[768,1024]{1,0:T(8,128)(2,1)}, bf16[768,1024]{1,0:T(8,128)(2,1)S(1)}, u32[]{:S(2)}) copy-start(bf16[768,1024]{1,0:T(8,128)(2,1)S(1)} %fusion.11.k0_ref) | copy-start | bytes 4718596
  74.9 38.4 %collective-permute-start.8 = (bf16[768,1024]{1,0:T(8,128)(2,1)S(1)}, bf16[768,1024]{1,0:T(8,128)(2,1)}, u32[]{:S(2)}, u32[]{:S(2)}) collective-permute-start(bf16[768,1024]{1,0:T(8,128)(2,1)S(1)} %fusion.8.v0_ref), channel_id=1, source_target_pairs={{0,2},{2,4},{4,6},{6,8},{8,10},{10,12},{12,14},{14,16},{16,18},{18... | collective-permute-start | bytes 4718600 | tf_op jit(solution)/shard_map/ppermute | solution.py:19
  76.8 68.9 %collective-permute-start.5 = (bf16[768,1024]{1,0:T(8,128)(2,1)S(1)}, bf16[768,1024]{1,0:T(8,128)(2,1)}, u32[]{:S(2)}, u32[]{:S(2)}) collective-permute-start(bf16[768,1024]{1,0:T(8,128)(2,1)S(1)} %fusion.11.k0_ref), channel_id=1, source_target_pairs={{0,2},{2,4},{4,6},{6,8},{8,10},{10,12},{12,14},{14,16},{16,18},{18... | collective-permute-start | bytes 4718600 | tf_op jit(solution)/shard_map/ppermute | solution.py:19
  80.7 69.1 %collective-permute-start.7 = (bf16[768,1024]{1,0:T(8,128)(2,1)S(1)}, bf16[768,1024]{1,0:T(8,128)(2,1)}, u32[]{:S(2)}, u32[]{:S(2)}) collective-permute-start(bf16[768,1024]{1,0:T(8,128)(2,1)S(1)} %fusion.8.v0_ref), channel_id=1, source_target_pairs={{0,4},{4,8},{8,12},{12,16},{16,20},{20,24},{24,28},{28,32},{32,36}... | collective-permute-start | bytes 4718600 | tf_op jit(solution)/shard_map/ppermute | solution.py:144
  113.3 36.6 %collective-permute-start.9 = (bf16[768,1024]{1,0:T(8,128)(2,1)}, bf16[768,1024]{1,0:T(8,128)(2,1)}, u32[]{:S(2)}, u32[]{:S(2)}) collective-permute-start(bf16[768,1024]{1,0:T(8,128)(2,1)} %collective-permute-done.8.v1_ref), channel_id=1, source_target_pairs={{0,2},{4,6},{8,10},{12,14},{16,18},{20,22},{24,26},{28,30},{32,34}... | collective-permute-start | bytes 4718600 | tf_op jit(solution)/shard_map/ppermute | solution.py:145
  115.7 37.0 %collective-permute-start.4 = (bf16[768,1024]{1,0:T(8,128)(2,1)S(1)}, bf16[768,1024]{1,0:T(8,128)(2,1)}, u32[]{:S(2)}, u32[]{:S(2)}) collective-permute-start(bf16[768,1024]{1,0:T(8,128)(2,1)S(1)} %fusion.11.k0_ref), channel_id=1, source_target_pairs={{0,4},{4,8},{8,12},{12,16},{16,20},{20,24},{24,28},{28,32},{32,36}... | collective-permute-start | bytes 4718600 | tf_op jit(solution)/shard_map/ppermute | solution.py:144
  145.7 7.0 %collective-permute-start.6 = (bf16[768,1024]{1,0:T(8,128)(2,1)}, bf16[768,1024]{1,0:T(8,128)(2,1)}, u32[]{:S(2)}, u32[]{:S(2)}) collective-permute-start(bf16[768,1024]{1,0:T(8,128)(2,1)} %collective-permute-done.5.k1_ref), channel_id=1, source_target_pairs={{0,2},{4,6},{8,10},{12,14},{16,18},{20,22},{24,26},{28,30},{32,34}... | collective-permute-start | bytes 4718600 | tf_op jit(solution)/shard_map/ppermute | solution.py:145
  148.1 19.7 %collective-permute-start.10 = (bf16[384,1024]{1,0:T(8,128)(2,1)}, bf16[384,1024]{1,0:T(8,128)(2,1)}, u32[]{:S(2)}, u32[]{:S(2)}) collective-permute-start(bf16[384,1024]{1,0:T(8,128)(2,1)} %get-tuple-element.10), channel_id=1, source_target_pairs={{0,1},{1,0},{2,3},{3,2},{4,5},{5,4},{6,7},{7,6},{8,9},{9,8},{10,11... | collective-permute-start | bytes 2359304 | tf_op jit(solution)/shard_map/ppermute | solution.py:23
  192.8 27.1 %collective-permute-start.11 = (bf16[384,1024]{1,0:T(8,128)(2,1)}, bf16[384,1024]{1,0:T(8,128)(2,1)S(1)}, u32[]{:S(2)}, u32[]{:S(2)}) collective-permute-start(bf16[384,1024]{1,0:T(8,128)(2,1)} %shard_map.47), channel_id=1, source_target_pairs={{0,1},{1,0},{2,3},{3,2},{4,5},{5,4},{6,7},{7,6},{8,9},{9,8},{10,11... | collective-permute-start | bytes 2359304 | tf_op jit(solution)/shard_map/ppermute | solution.py:23

commit v4 on v3

--- a/solution.py
+++ b/solution.py
@@ -43,48 +43,63 @@
 
     col = lax.broadcasted_iota(jnp.int32, (count, seg_rows), 1)
     row = lax.broadcasted_iota(jnp.int32, (count, seg_rows), 0) + first_row
-    ok2 = col < jnp.where(seg >= 2, seg_rows, 0)
-    ok1 = col < jnp.where(seg >= 1, seg_rows, 0)
-    ok0 = col <= row
     low = jnp.float32(-1e30)
-    s2 = jnp.where(ok2, scores_of(k2_ref), low)
-    s1 = jnp.where(ok1, scores_of(k1_ref), low)
-    s0 = jnp.where(ok0, scores_of(k0_ref), low)
-    top = jnp.maximum(
-        jnp.maximum(jnp.max(s2, axis=1, keepdims=True), jnp.max(s1, axis=1, keepdims=True)),
-        jnp.max(s0, axis=1, keepdims=True),
-    )
-    e2 = jnp.where(ok2, jnp.exp(s2 - top), 0.0)
-    e1 = jnp.where(ok1, jnp.exp(s1 - top), 0.0)
-    e0 = jnp.where(ok0, jnp.exp(s0 - top), 0.0)
-    total = (
-        jnp.sum(e2, axis=1, keepdims=True)
-        + jnp.sum(e1, axis=1, keepdims=True)
-        + jnp.sum(e0, axis=1, keepdims=True)
-    )
-    mixed = jnp.dot(e2.astype(jnp.bfloat16), v2_ref[...], preferred_element_type=jnp.float32)
-    mixed = mixed + jnp.dot(e1.astype(jnp.bfloat16), v1_ref[...], preferred_element_type=jnp.float32)
-    mixed = mixed + jnp.dot(e0.astype(jnp.bfloat16), v0_ref[...], preferred_element_type=jnp.float32)
-    o_ref[...] = (mixed / total).astype(o_ref.dtype)
+    s0 = jnp.where(col <= row, scores_of(k0_ref), low)
+    top0 = jnp.max(s0, axis=1, keepdims=True)
+
+    def finish(s2, s1, e2_of, e1_of):
+        top = jnp.maximum(
+            jnp.maximum(jnp.max(s2, axis=1, keepdims=True), jnp.max(s1, axis=1, keepdims=True)), top0
+        )
+        e2 = e2_of(s2, top)
+        e1 = e1_of(s1, top)
+        e0 = jnp.where(col <= row, jnp.exp(s0 - top), 0.0)
+        total = (
+            jnp.sum(e2, axis=1, keepdims=True)
+            + jnp.sum(e1, axis=1, keepdims=True)
+            + jnp.sum(e0, axis=1, keepdims=True)
+        )
+        mixed = jnp.dot(e2.astype(jnp.bfloat16), v2_ref[...], preferred_element_type=jnp.float32)
+        mixed = mixed + jnp.dot(e1.astype(jnp.bfloat16), v1_ref[...], preferred_element_type=jnp.float32)
+        mixed = mixed + jnp.dot(e0.astype(jnp.bfloat16), v0_ref[...], preferred_element_type=jnp.float32)
+        o_ref[...] = (mixed / total).astype(o_ref.dtype)
+
+    @pl.when(seg >= MEM)
+    def _():
+        plain = lambda s, top: jnp.exp(s - top)
+        finish(scores_of(k2_ref), scores_of(k1_ref), plain, plain)
+
+    @pl.when(seg < MEM)
+    def _():
+        ok2 = col < jnp.where(seg >= 2, seg_rows, 0)
+        ok1 = col < jnp.where(seg >= 1, seg_rows, 0)
+        s2 = jnp.where(ok2, scores_of(k2_ref), low)
+        s1 = jnp.where(ok1, scores_of(k1_ref), low)
+        finish(
+            s2,
+            s1,
+            lambda s, top: jnp.where(ok2, jnp.exp(s - top), 0.0),
+            lambda s, top: jnp.where(ok1, jnp.exp(s - top), 0.0),
+        )
 
 
-def attend(seg_number, first_row, query_rows, keys, values):
-    count, cols = query_rows.shape
+def attend(seg_number, first_row, query_rows, keys, values, head_lo, head_count):
+    count = query_rows.shape[0]
     seg_rows = keys[0].shape[0]
-    heads = cols // HD
-    q_spec = pl.BlockSpec((count, HD), lambda h, scalars: (0, h))
-    kv_spec = pl.BlockSpec((seg_rows, HD), lambda h, scalars: (0, h))
+    q_spec = pl.BlockSpec((count, HD), lambda h, scalars: (0, h + head_lo))
+    kv_spec = pl.BlockSpec((seg_rows, HD), lambda h, scalars: (0, h + head_lo))
+    o_spec = pl.BlockSpec((count, HD), lambda h, scalars: (0, h))
     grid_spec = pltpu.PrefetchScalarGridSpec(
         num_scalar_prefetch=1,
-        grid=(heads,),
+        grid=(head_count,),
         in_specs=[q_spec] + [kv_spec] * 6,
-        out_specs=q_spec,
+        out_specs=o_spec,
     )
     scalars = jnp.stack([seg_number, first_row]).astype(jnp.int32)
     return pl.pallas_call(
         attention_kernel,
         grid_spec=grid_spec,
-        out_shape=jax.ShapeDtypeStruct((count, cols), jnp.bfloat16),
+        out_shape=jax.ShapeDtypeStruct((count, head_count * HD), jnp.bfloat16),
         interpret=INTERPRET,
     )(scalars, query_rows, *keys, *values)
 
@@ -150,9 +165,14 @@
     keys = (key_two, key_one, own_key)
     values = (value_two, value_one, own_value)
 
-    their_rows = attend(seg_number, other_half * tok_rows, query_got, keys, values)
-    rows_got = swap_halves(their_rows)
-    mine_rows = attend(seg_number, half_number * tok_rows, mine_of(queries), keys, values)
+    heads = cols // HD
+    mine_rows = attend(seg_number, half_number * tok_rows, mine_of(queries), keys, values, 0, heads)
+    query_got, mine_rows = lax.optimization_barrier((query_got, mine_rows))
+    got = []
+    for head_lo in range(0, heads, heads // 2):
+        their_rows = attend(seg_number, other_half * tok_rows, query_got, keys, values, head_lo, heads // 2)
+        got.append(swap_halves(their_rows))
+    rows_got = jnp.concatenate(got, axis=1)
     return in_order(first_is_mine, mine_rows, rows_got, 1)
 
 

time: 224 us -> 219 us (0.978)
  waiting for transfers between devices: 121 us -> 116 us
    ppermute x4 -> x5, waiting for transfers between devices: 62.5 us -> 57.7 us  [swap_halves(): return lax.ppermute(value, 'fsdp', [(0, 1), (1, 0)])]
    pallas_call x2 -> x3, Pallas kernels: 50 us -> 51.4 us  [attend(): pl.pallas_call(attention_kernel, grid_spec=grid_spec, out_shape=jax.Shape...]
    ppermute x4 -> x5, starting transfers between devices: 4.71 us -> 5.29 us  [swap_halves(): return lax.ppermute(value, 'fsdp', [(0, 1), (1, 0)])]
  transfers between devices with their start and end apart: 12 -> 13, of which waited for: 7 -> 6; matrix products, arithmetic and copies ran while one was open for 5% -> 5% of each run, Pallas kernels for 11% -> 17%
where the time goes in v4:
time: 219 us; the launch traced here: 218 us
  waiting for transfers between devices  116 us (53%)
  Pallas kernels  51.4 us (23%)
  starting transfers between devices  24 us (11%)
  other arithmetic  17 us (8%)
  matrix products  6.85 us (3%)
  local copies, waits for them, and re-layouts  3.34 us (2%)
    ppermute x5, waiting for transfers between devices, swap_halves(): return lax.ppermute(value, 'fsdp', [(0, 1), (1, 0)])  57.7 us
    ppermute x2, waiting for transfers between devices, from_behind(): lax.ppermute(value, axis, [(source, source + steps) for source in range(l...  56.7 us
    pallas_call x3, Pallas kernels, attend(): pl.pallas_call(attention_kernel, grid_spec=grid_spec, out_shape=jax.Shape...  51.4 us
    select_n x3, other arithmetic, in_order(): lead = jnp.where(first_is_mine, mine, other)  5.88 us
    ppermute x2, starting transfers between devices, from_behind(): lax.ppermute(value, axis, [(source, source + steps) for source in range(l...  5.85 us
    ppermute x2, starting transfers between devices, shifted(): even_two = lax.ppermute(own, 'seg', even_pairs)  5.74 us
    select_n x2, other arithmetic, shifted(): return (jnp.where(is_key_core, even_two, odd_two), one)  5.46 us
    ppermute x5, starting transfers between devices, swap_halves(): return lax.ppermute(value, 'fsdp', [(0, 1), (1, 0)])  5.29 us
  transfers between devices with their start and end apart: 13, of which 6 were waited for; matrix products, arithmetic and copies ran while one was open for 5% of the time, Pallas kernels for 17%

profile of v4, /device:TPU:24, one launch (start us, length us, event | category | flops | bytes accessed | tf_op | source)
XLA Modules:
  0.0 218.3 jit_solution(5540916004295286957)
XLA Ops:
  0.0 3.2 %dynamic-slice_select_fusion = bf16[1024,1024]{1,0:T(8,128)(2,1)S(1)} fusion(bf16[1024,2048]{1,0:T(8,128)(2,1)} %param.7, s32[]{:T(128)S(6)} %select_n.88, bf16[1024,2048]{1,0:T(8,128)(2,1)} %param.6, pred[]{:T(512)S(6)} %eq.9), kind=kLoop, calls=%fused_computation.9 | loop fusion | flops 1048576 | bytes 6291461 | tf_op jit(solution)/shard_map/jit(_where)/select_n | solution.py:127
  3.2 0.2 fusion.16
  3.4 1.6 collective-permute-start.1
  4.9 2.1 collective-permute-start.2
  7.0 0.6 collective-permute-start
  7.6 21.9 %collective-permute-done.1 = bf16[1024,512]{1,0:T(8,128)(2,1)S(1)} collective-permute-done((bf16[1024,512]{1,0:T(8,128)(2,1)S(1)}, bf16[1024,512]{1,0:T(8,128)(2,1)S(1)}, u32[]{:S(2)}, u32[]{:S(2)}) %collective-permute-start.1) | collective-permute-done | bytes 1048608 | tf_op jit(solution)/shard_map/ppermute | solution.py:23
  29.5 0.1 constant_dynamic-update-slice_fusion.1
  29.6 1.1 collective-permute-done.2
  30.8 0.1 constant_dynamic-update-slice_fusion
  30.9 0.1 collective-permute-start.3
  31.0 0.0 copy-start.3
  31.0 2.8 %constant_dynamic-slice_fusion = (bf16[384,1024]{1,0:T(8,128)(2,1)}, bf16[384,1024]{1,0:T(8,128)(2,1)}) fusion(bf16[384,2048]{1,0:T(8,128)(2,1)} %param.5, s32[]{:T(128)S(6)} %select_n.93, s32[]{:T(128)S(6)} %select_n.88), kind=kLoop, calls=%fused_computation.29 | loop fusion | bytes 3145736 | tf_op jit(solution)/shard_map/dynamic_slice | solution.py:122
  33.8 0.0 copy-start.2
  33.8 28.3 %collective-permute-done = bf16[384,2048]{1,0:T(8,128)(2,1)} collective-permute-done((bf16[384,2048]{1,0:T(8,128)(2,1)}, bf16[384,2048]{1,0:T(8,128)(2,1)}, u32[]{:S(2)}, u32[]{:S(2)}) %collective-permute-start) | collective-permute-done | bytes 1572896 | tf_op jit(solution)/shard_map/ppermute | solution.py:23
  62.2 2.1 broadcast_select_fusion.9
  64.2 0.0 collective-permute-done.3
  64.3 0.0 copy-done.3
  64.3 0.0 copy-done.2
  64.3 3.7 %broadcast_select_fusion.3 = (bf16[1024,1024]{1,0:T(8,128)(2,1)S(1)}, bf16[1024,1024]{1,0:T(8,128)(2,1)S(1)}, bf16[1024,1024]{1,0:T(8,128)(2,1)S(1)}, bf16[1024,1024]{1,0:T(8,128)(2,1)S(1)}) fusion(pred[]{:T(512)S(6)} %eq.8, bf16[1024,2048]{1,0:T(8,128)(2,1)S(1)} %copy-done.2, s32[]{:T(128)S(6)} %select_n.93, bf16[1024,1024]{1,0:T(8,128)(2,1)} %collective-permute-done.3, ...), kind=kLoop, calls=%fused_computation.13 | loop fusion | flops 6291456 | bytes 16777222 | tf_op jit(solution)/shard_map/jit(_where)/select_n | solution.py:27
  68.0 3.4 %fusion.8.v0_ref = bf16[768,1024]{1,0:T(8,128)(2,1)S(1)} fusion(bf16[1024,1024]{1,0:T(8,128)(2,1)S(1)} %get-tuple-element.16, bf16[1024,1024]{1,0:T(8,128)(2,1)S(1)} %get-tuple-element.15, bf16[384,2048]{1,0:T(8,128)(2,1)S(1)} %get-tuple-element.22, bf16[384,2048]{1,0:T(8,128)(2,1)S(1)} %get-tuple-element.21), kind=kOutput, calls=%fused_computation.16 | convolution fusion | flops 3236691968 | bytes 8912896 | tf_op jit(solution)/shard_map/dot_general | solution.py:148
  71.4 0.0 copy-start
  71.4 3.4 %fusion.11.k0_ref = bf16[768,1024]{1,0:T(8,128)(2,1)S(1)} fusion(bf16[1024,1024]{1,0:T(8,128)(2,1)S(1)} %get-tuple-element.19, bf16[1024,1024]{1,0:T(8,128)(2,1)S(1)} %get-tuple-element.20, bf16[384,2048]{1,0:T(8,128)(2,1)S(1)} %get-tuple-element.22, bf16[384,2048]{1,0:T(8,128)(2,1)S(1)} %get-tuple-element.21), kind=kOutput, calls=%fused_computation.17 | convolution fusion | flops 3236691968 | bytes 8912896 | tf_op jit(solution)/shard_map/dot_general | solution.py:147
  74.8 0.0 copy-start.1
  74.9 1.9 collective-permute-start.9
  76.8 3.9 %collective-permute-start.6 = (bf16[768,1024]{1,0:T(8,128)(2,1)S(1)}, bf16[768,1024]{1,0:T(8,128)(2,1)}, u32[]{:S(2)}, u32[]{:S(2)}) collective-permute-start(bf16[768,1024]{1,0:T(8,128)(2,1)S(1)} %fusion.11.k0_ref), channel_id=1, source_target_pairs={{0,2},{2,4},{4,6},{6,8},{8,10},{10,12},{12,14},{14,16},{16,18},{18... | collective-permute-start | bytes 4718600 | tf_op jit(solution)/shard_map/ppermute | solution.py:19
  80.7 0.0 copy-done
  80.7 3.8 %collective-permute-start.8 = (bf16[768,1024]{1,0:T(8,128)(2,1)S(1)}, bf16[768,1024]{1,0:T(8,128)(2,1)}, u32[]{:S(2)}, u32[]{:S(2)}) collective-permute-start(bf16[768,1024]{1,0:T(8,128)(2,1)S(1)} %fusion.8.v0_ref), channel_id=1, source_target_pairs={{0,4},{4,8},{8,12},{12,16},{16,20},{20,24},{24,28},{28,32},{32,36}... | collective-permute-start | bytes 4718600 | tf_op jit(solution)/shard_map/ppermute | solution.py:159
  84.6 28.7 %collective-permute-done.9.v1_ref = bf16[768,1024]{1,0:T(8,128)(2,1)} collective-permute-done((bf16[768,1024]{1,0:T(8,128)(2,1)S(1)}, bf16[768,1024]{1,0:T(8,128)(2,1)}, u32[]{:S(2)}, u32[]{:S(2)}) %collective-permute-start.9) | collective-permute-done | bytes 1572896 | tf_op jit(solution)/shard_map/ppermute | solution.py:19
  113.3 2.5 %collective-permute-start.10 = (bf16[768,1024]{1,0:T(8,128)(2,1)}, bf16[768,1024]{1,0:T(8,128)(2,1)}, u32[]{:S(2)}, u32[]{:S(2)}) collective-permute-start(bf16[768,1024]{1,0:T(8,128)(2,1)} %collective-permute-done.9.v1_ref), channel_id=1, source_target_pairs={{0,2},{4,6},{8,10},{12,14},{16,18},{20,22},{24,26},{28,30},{32,34}... | collective-permute-start | bytes 4718600 | tf_op jit(solution)/shard_map/ppermute | solution.py:160
  115.7 1.9 collective-permute-start.5
  117.7 28.0 %collective-permute-done.6.k1_ref = bf16[768,1024]{1,0:T(8,128)(2,1)} collective-permute-done((bf16[768,1024]{1,0:T(8,128)(2,1)S(1)}, bf16[768,1024]{1,0:T(8,128)(2,1)}, u32[]{:S(2)}, u32[]{:S(2)}) %collective-permute-start.6) | collective-permute-done | bytes 1572896 | tf_op jit(solution)/shard_map/ppermute | solution.py:19
  145.7 2.4 %collective-permute-start.7 = (bf16[768,1024]{1,0:T(8,128)(2,1)}, bf16[768,1024]{1,0:T(8,128)(2,1)}, u32[]{:S(2)}, u32[]{:S(2)}) collective-permute-start(bf16[768,1024]{1,0:T(8,128)(2,1)} %collective-permute-done.6.k1_ref), channel_id=1, source_target_pairs={{0,2},{4,6},{8,10},{12,14},{16,18},{20,22},{24,26},{28,30},{32,34}... | collective-permute-start | bytes 4718600 | tf_op jit(solution)/shard_map/ppermute | solution.py:160
  148.1 0.7 pad_add_fusion.seg_ref
  148.8 1.1 collective-permute-start.4
  149.9 0.6 pad_add_fusion.1.seg_ref
  150.5 0.0 collective-permute-done.8
  150.5 0.0 collective-permute-done.10
  150.5 2.7 %broadcast_select_fusion.6.v2_ref = bf16[768,1024]{1,0:T(8,128)(2,1)} fusion(bf16[768,1024]{1,0:T(8,128)(2,1)} %collective-permute-done.8, bf16[768,1024]{1,0:T(8,128)(2,1)} %collective-permute-done.10, pred[]{:T(512)S(6)} %eq.9), kind=kLoop, calls=%fused_computation.19 | loop fusion | flops 786432 | bytes 4718593 | tf_op jit(solution)/shard_map/jit(_where)/select_n | solution.py:161
  153.2 0.0 copy-done.1
  153.2 0.0 collective-permute-done.5
  153.2 0.0 collective-permute-done.7
  153.2 2.7 %broadcast_select_fusion.7.k2_ref = bf16[768,1024]{1,0:T(8,128)(2,1)} fusion(bf16[768,1024]{1,0:T(8,128)(2,1)} %collective-permute-done.5, bf16[768,1024]{1,0:T(8,128)(2,1)} %collective-permute-done.7, pred[]{:T(512)S(6)} %eq.9), kind=kLoop, calls=%fused_computation.20 | loop fusion | flops 786432 | bytes 4718593 | tf_op jit(solution)/shard_map/jit(_where)/select_n | solution.py:161
  155.9 24.3 %shard_map.46 = bf16[384,1024]{1,0:T(8,128)(2,1)} custom-call(s32[2]{0:T(128)} %pad_add_fusion.seg_ref, bf16[384,1024]{1,0:T(8,128)(2,1)} %get-tuple-element.27.q_ref, bf16[768,1024]{1,0:T(8,128)(2,1)} %broadcast_select_fusion.7.k2_ref, bf16[768,1024]{1,0:T(8,128)(2,1)} %collective-permute-done.6.k1_ref, bf16[768,1024]{1,0:T(8,128)(2,1)} %copy-done.1, ...), custom_call_target="tpu_custom_call" | custom-call | tf_op jit(solution)/shard_map/pallas_call | solution.py:99
  180.3 0.0 collective-permute-done.4.q_ref
  180.3 13.5 %shard_map.47 = bf16[384,512]{1,0:T(8,128)(2,1)} custom-call(s32[2]{0:T(128)} %pad_add_fusion.1.seg_ref, bf16[384,1024]{1,0:T(8,128)(2,1)} %collective-permute-done.4.q_ref, bf16[768,1024]{1,0:T(8,128)(2,1)} %broadcast_select_fusion.7.k2_ref, bf16[768,1024]{1,0:T(8,128)(2,1)} %collective-permute-done.6.k1_ref, bf16[768,1024]{1,0:T(8,128)(2,1)} %copy-done.1, ...), custom_call_target="tpu_custom_call" | custom-call | tf_op jit(solution)/shard_map/pallas_call | solution.py:99
  193.8 0.9 collective-permute-start.11
  194.7 13.5 %shard_map.48 = bf16[384,512]{1,0:T(8,128)(2,1)} custom-call(s32[2]{0:T(128)} %pad_add_fusion.1.seg_ref, bf16[384,1024]{1,0:T(8,128)(2,1)} %collective-permute-done.4.q_ref, bf16[768,1024]{1,0:T(8,128)(2,1)} %broadcast_select_fusion.7.k2_ref, bf16[768,1024]{1,0:T(8,128)(2,1)} %collective-permute-done.6.k1_ref, bf16[768,1024]{1,0:T(8,128)(2,1)} %copy-done.1, ...), custom_call_target="tpu_custom_call" | custom-call | tf_op jit(solution)/shard_map/pallas_call | solution.py:99
  208.2 0.0 copy-start.4
  208.2 1.1 collective-permute-start.12
  209.4 0.0 collective-permute-done.11
  209.4 7.5 %collective-permute-done.12 = bf16[384,512]{1,0:T(8,128)(2,1)S(1)} collective-permute-done((bf16[384,512]{1,0:T(8,128)(2,1)}, bf16[384,512]{1,0:T(8,128)(2,1)S(1)}, u32[]{:S(2)}, u32[]{:S(2)}) %collective-permute-start.12) | collective-permute-done | bytes 393248 | tf_op jit(solution)/shard_map/ppermute | solution.py:23
  216.9 0.0 copy-done.4
  216.9 0.1 broadcast_select_fusion.11
  217.0 1.2 pad_maximum_fusion.7
  (2 shorter events, 0.1 us)
Async XLA Ops:
  3.4 26.1 %collective-permute-start.1 = (bf16[1024,512]{1,0:T(8,128)(2,1)S(1)}, bf16[1024,512]{1,0:T(8,128)(2,1)S(1)}, u32[]{:S(2)}, u32[]{:S(2)}) collective-permute-start(bf16[1024,512]{1,0:T(8,128)(2,1)S(1)} %get-tuple-element.24), channel_id=1, source_target_pairs={{0,1},{1,0},{2,3},{3,2},{4,5},{5,4},{6,7},{7,6},{8,9},{9,8},{10,11... | collective-permute-start | bytes 3145736 | tf_op jit(solution)/shard_map/ppermute | solution.py:23
  4.9 25.8 %collective-permute-start.2 = (bf16[1024,512]{1,0:T(8,128)(2,1)S(1)}, bf16[1024,512]{1,0:T(8,128)(2,1)S(1)}, u32[]{:S(2)}, u32[]{:S(2)}) collective-permute-start(bf16[1024,512]{1,0:T(8,128)(2,1)S(1)} %get-tuple-element.23), channel_id=1, source_target_pairs={{33,0},{32,1},{35,2},{34,3},{37,4},{36,5},{39,6},{38,7},{41,8},{40... | collective-permute-start | bytes 3145736 | tf_op jit(solution)/shard_map/ppermute | solution.py:134
  7.0 55.1 %collective-permute-start = (bf16[384,2048]{1,0:T(8,128)(2,1)}, bf16[384,2048]{1,0:T(8,128)(2,1)}, u32[]{:S(2)}, u32[]{:S(2)}) collective-permute-start(bf16[384,2048]{1,0:T(8,128)(2,1)} %param.4), channel_id=1, source_target_pairs={{0,1},{1,0},{2,3},{3,2},{4,5},{5,4},{6,7},{7,6},{8,9},{9,8},{10,11... | collective-permute-start | bytes 4718600 | tf_op jit(solution)/shard_map/ppermute | solution.py:23
  30.9 33.3 %collective-permute-start.3 = (bf16[1024,1024]{1,0:T(8,128)(2,1)S(1)}, bf16[1024,1024]{1,0:T(8,128)(2,1)}, u32[]{:S(2)}, u32[]{:S(2)}) collective-permute-start(bf16[1024,1024]{1,0:T(8,128)(2,1)S(1)} %constant_dynamic-update-slice_fusion), channel_id=1, source_target_pairs={{0,2},{2,0},{4,6},{6,4},{8,10},{10,8},{12,14},{14,12},{16,18},{18,... | collective-permute-start | bytes 6291464 | tf_op jit(solution)/shard_map/ppermute | solution.py:137
  31.0 33.2 %copy-start.3 = (bf16[1024,2048]{1,0:T(8,128)(2,1)S(1)}, bf16[1024,2048]{1,0:T(8,128)(2,1)}, u32[]{:S(2)}) copy-start(bf16[1024,2048]{1,0:T(8,128)(2,1)} %param.6) | copy-start | bytes 12582916
  33.8 30.4 %copy-start.2 = (bf16[1024,2048]{1,0:T(8,128)(2,1)S(1)}, bf16[1024,2048]{1,0:T(8,128)(2,1)}, u32[]{:S(2)}) copy-start(bf16[1024,2048]{1,0:T(8,128)(2,1)} %param.7) | copy-start | bytes 12582916
  71.4 9.3 %copy-start = (bf16[768,1024]{1,0:T(8,128)(2,1)}, bf16[768,1024]{1,0:T(8,128)(2,1)S(1)}, u32[]{:S(2)}) copy-start(bf16[768,1024]{1,0:T(8,128)(2,1)S(1)} %fusion.8.v0_ref) | copy-start | bytes 4718596
  74.8 78.4 %copy-start.1 = (bf16[768,1024]{1,0:T(8,128)(2,1)}, bf16[768,1024]{1,0:T(8,128)(2,1)S(1)}, u32[]{:S(2)}) copy-start(bf16[768,1024]{1,0:T(8,128)(2,1)S(1)} %fusion.11.k0_ref) | copy-start | bytes 4718596
  74.9 38.4 %collective-permute-start.9 = (bf16[768,1024]{1,0:T(8,128)(2,1)S(1)}, bf16[768,1024]{1,0:T(8,128)(2,1)}, u32[]{:S(2)}, u32[]{:S(2)}) collective-permute-start(bf16[768,1024]{1,0:T(8,128)(2,1)S(1)} %fusion.8.v0_ref), channel_id=1, source_target_pairs={{0,2},{2,4},{4,6},{6,8},{8,10},{10,12},{12,14},{14,16},{16,18},{18... | collective-permute-start | bytes 4718600 | tf_op jit(solution)/shard_map/ppermute | solution.py:19
  76.8 68.9 %collective-permute-start.6 = (bf16[768,1024]{1,0:T(8,128)(2,1)S(1)}, bf16[768,1024]{1,0:T(8,128)(2,1)}, u32[]{:S(2)}, u32[]{:S(2)}) collective-permute-start(bf16[768,1024]{1,0:T(8,128)(2,1)S(1)} %fusion.11.k0_ref), channel_id=1, source_target_pairs={{0,2},{2,4},{4,6},{6,8},{8,10},{10,12},{12,14},{14,16},{16,18},{18... | collective-permute-start | bytes 4718600 | tf_op jit(solution)/shard_map/ppermute | solution.py:19
  80.7 69.7 %collective-permute-start.8 = (bf16[768,1024]{1,0:T(8,128)(2,1)S(1)}, bf16[768,1024]{1,0:T(8,128)(2,1)}, u32[]{:S(2)}, u32[]{:S(2)}) collective-permute-start(bf16[768,1024]{1,0:T(8,128)(2,1)S(1)} %fusion.8.v0_ref), channel_id=1, source_target_pairs={{0,4},{4,8},{8,12},{12,16},{16,20},{20,24},{24,28},{28,32},{32,36}... | collective-permute-start | bytes 4718600 | tf_op jit(solution)/shard_map/ppermute | solution.py:159
  113.3 37.2 %collective-permute-start.10 = (bf16[768,1024]{1,0:T(8,128)(2,1)}, bf16[768,1024]{1,0:T(8,128)(2,1)}, u32[]{:S(2)}, u32[]{:S(2)}) collective-permute-start(bf16[768,1024]{1,0:T(8,128)(2,1)} %collective-permute-done.9.v1_ref), channel_id=1, source_target_pairs={{0,2},{4,6},{8,10},{12,14},{16,18},{20,22},{24,26},{28,30},{32,34}... | collective-permute-start | bytes 4718600 | tf_op jit(solution)/shard_map/ppermute | solution.py:160
  115.7 37.5 %collective-permute-start.5 = (bf16[768,1024]{1,0:T(8,128)(2,1)S(1)}, bf16[768,1024]{1,0:T(8,128)(2,1)}, u32[]{:S(2)}, u32[]{:S(2)}) collective-permute-start(bf16[768,1024]{1,0:T(8,128)(2,1)S(1)} %fusion.11.k0_ref), channel_id=1, source_target_pairs={{0,4},{4,8},{8,12},{12,16},{16,20},{20,24},{24,28},{28,32},{32,36}... | collective-permute-start | bytes 4718600 | tf_op jit(solution)/shard_map/ppermute | solution.py:159
  145.7 7.5 %collective-permute-start.7 = (bf16[768,1024]{1,0:T(8,128)(2,1)}, bf16[768,1024]{1,0:T(8,128)(2,1)}, u32[]{:S(2)}, u32[]{:S(2)}) collective-permute-start(bf16[768,1024]{1,0:T(8,128)(2,1)} %collective-permute-done.6.k1_ref), channel_id=1, source_target_pairs={{0,2},{4,6},{8,10},{12,14},{16,18},{20,22},{24,26},{28,30},{32,34}... | collective-permute-start | bytes 4718600 | tf_op jit(solution)/shard_map/ppermute | solution.py:160
  148.8 31.5 %collective-permute-start.4 = (bf16[384,1024]{1,0:T(8,128)(2,1)}, bf16[384,1024]{1,0:T(8,128)(2,1)}, u32[]{:S(2)}, u32[]{:S(2)}) collective-permute-start(bf16[384,1024]{1,0:T(8,128)(2,1)} %get-tuple-element.10), channel_id=1, source_target_pairs={{0,1},{1,0},{2,3},{3,2},{4,5},{5,4},{6,7},{7,6},{8,9},{9,8},{10,11... | collective-permute-start | bytes 2359304 | tf_op jit(solution)/shard_map/ppermute | solution.py:23
  193.8 15.6 %collective-permute-start.11 = (bf16[384,512]{1,0:T(8,128)(2,1)}, bf16[384,512]{1,0:T(8,128)(2,1)S(1)}, u32[]{:S(2)}, u32[]{:S(2)}) collective-permute-start(bf16[384,512]{1,0:T(8,128)(2,1)} %shard_map.47), channel_id=1, source_target_pairs={{0,1},{1,0},{2,3},{3,2},{4,5},{5,4},{6,7},{7,6},{8,9},{9,8},{10,11... | collective-permute-start | bytes 1179656 | tf_op jit(solution)/shard_map/ppermute | solution.py:23
  208.2 8.7 %copy-start.4 = (bf16[384,1024]{1,0:T(8,128)(2,1)S(1)}, bf16[384,1024]{1,0:T(8,128)(2,1)}, u32[]{:S(2)}) copy-start(bf16[384,1024]{1,0:T(8,128)(2,1)} %shard_map.46) | copy-start | bytes 2359300
  208.2 8.6 %collective-permute-start.12 = (bf16[384,512]{1,0:T(8,128)(2,1)}, bf16[384,512]{1,0:T(8,128)(2,1)S(1)}, u32[]{:S(2)}, u32[]{:S(2)}) collective-permute-start(bf16[384,512]{1,0:T(8,128)(2,1)} %shard_map.48), channel_id=1, source_target_pairs={{0,1},{1,0},{2,3},{3,2},{4,5},{5,4},{6,7},{7,6},{8,9},{9,8},{10,11... | collective-permute-start | bytes 1179656 | tf_op jit(solution)/shard_map/ppermute | solution.py:23

commit v5 on v4

--- a/solution.py
+++ b/solution.py
@@ -132,24 +132,22 @@
         for half in range(halves):
             wrap_pairs.append(((seg ^ stride) * halves + (1 - half), seg * halves + half))
     right_got = lax.ppermute(served[:, piece:], ("seg", "fsdp"), wrap_pairs)
+    hidden_sent, left_got, right_got = lax.optimization_barrier((hidden_states, left_got, right_got))
+    hidden_got = swap_halves(hidden_sent)
     piece_got = jnp.concatenate([left_got, right_got], axis=1)
     core_pairs = [(seg, seg ^ 1) for seg in range(segs)]
     piece_other = lax.ppermute(piece_got, "seg", core_pairs)
     key_got = jnp.where(is_key_core, piece_got, piece_other)
     value_got = jnp.where(is_key_core, piece_other, piece_got)
 
-    hidden_got = swap_halves(hidden_states)
 
     key_weights = in_order(first_is_mine, mine_of(w_key), key_got, 0)
     value_weights = in_order(first_is_mine, mine_of(w_value), value_got, 0)
-    hidden_rows = in_order(first_is_mine, hidden_states, hidden_got, 0)
 
-    own_key = jnp.dot(hidden_rows, key_weights, preferred_element_type=jnp.float32).astype(jnp.bfloat16)
-    own_value = jnp.dot(hidden_rows, value_weights, preferred_element_type=jnp.float32).astype(
-        jnp.bfloat16
-    )
-    query_sent, own_key, own_value = lax.optimization_barrier((theirs_of(queries), own_key, own_value))
-    query_got = swap_halves(query_sent)
+    def project(rows):
+        key = jnp.dot(rows, key_weights, preferred_element_type=jnp.float32).astype(jnp.bfloat16)
+        value = jnp.dot(rows, value_weights, preferred_element_type=jnp.float32).astype(jnp.bfloat16)
+        return jnp.stack([key, value])
 
     even_pairs = [(s, s + 2) for s in range(0, segs - 2, 2)]
     forward_pairs = [(s, s + 1) for s in range(0, segs - 1, 2)]
@@ -160,10 +158,19 @@
         odd_two = lax.ppermute(one, "seg", forward_pairs)
         return jnp.where(is_key_core, even_two, odd_two), one
 
-    key_two, key_one = shifted(own_key)
-    value_two, value_one = shifted(own_value)
-    keys = (key_two, key_one, own_key)
-    values = (value_two, value_one, own_value)
+    mine_unit = project(hidden_states)
+    mine_two, mine_one = shifted(mine_unit)
+    hidden_got, mine_one = lax.optimization_barrier((hidden_got, mine_one))
+    their_unit = project(hidden_got)
+    query_sent, their_unit = lax.optimization_barrier((theirs_of(queries), their_unit))
+    query_got = swap_halves(query_sent)
+    their_two, their_one = shifted(their_unit)
+
+    def whole(mine, theirs, part):
+        return in_order(first_is_mine, mine[part], theirs[part], 0)
+
+    keys = tuple(whole(m, t, 0) for m, t in ((mine_two, their_two), (mine_one, their_one), (mine_unit, their_unit)))
+    values = tuple(whole(m, t, 1) for m, t in ((mine_two, their_two), (mine_one, their_one), (mine_unit, their_unit)))
 
     heads = cols // HD
     mine_rows = attend(seg_number, half_number * tok_rows, mine_of(queries), keys, values, 0, heads)

time: 219 us -> 265 us (1.21)
  waiting for transfers between devices: 116 us -> 162 us
  other arithmetic: 17 us -> 23.2 us
  starting transfers between devices: 24 us -> 19.1 us
    ppermute x5, waiting for transfers between devices: 57.7 us -> 115 us  [swap_halves(): return lax.ppermute(value, 'fsdp', [(0, 1), (1, 0)])]
    ppermute x2, waiting for transfers between devices: 56.7 us -> 32.2 us  [from_behind(): lax.ppermute(value, axis, [(source, source + steps) for source in range(l...]
    ppermute x2, waiting for transfers between devices: 0.01 us -> 7.69 us  [shifted(): even_two = lax.ppermute(own, 'seg', even_pairs)]
    concatenate x1 -> x4, other arithmetic: 1.25 us -> 7.26 us  [in_order(): return jnp.concatenate([lead, tail], axis=axis)]
    ppermute x1, waiting for transfers between devices: 0.01 us -> 4.16 us  [body(): piece_other = lax.ppermute(piece_got, 'seg', core_pairs)]
    select_n x3 -> x5, other arithmetic: 5.88 us -> 6.97 us  [in_order(): lead = jnp.where(first_is_mine, mine, other)]
    dot_general x2 -> x4, matrix products: 6.85 us -> 7.15 us  [the longest x2 3.57 us: project(): jnp.dot(rows, value_weights, preferred_element_type=jnp.float32)]
  transfers between devices with their start and end apart: 13 -> 13, of which waited for: 6 -> 7; matrix products, arithmetic and copies ran while one was open for 5% -> 9% of each run, Pallas kernels for 17% -> 14%
where the time goes in v5:
time: 265 us; the launch traced here: 264 us
  waiting for transfers between devices  162 us (61%)
  Pallas kernels  51.4 us (19%)
  other arithmetic  23.2 us (9%)
  starting transfers between devices  19.1 us (7%)
  matrix products  7.15 us (3%)
    ppermute x5, waiting for transfers between devices, swap_halves(): return lax.ppermute(value, 'fsdp', [(0, 1), (1, 0)])  115 us
    pallas_call x3, Pallas kernels, attend(): pl.pallas_call(attention_kernel, grid_spec=grid_spec, out_shape=jax.Shape...  51.4 us
    ppermute x2, waiting for transfers between devices, from_behind(): lax.ppermute(value, axis, [(source, source + steps) for source in range(l...  32.2 us
    ppermute x2, waiting for transfers between devices, shifted(): even_two = lax.ppermute(own, 'seg', even_pairs)  7.69 us
    concatenate x4, other arithmetic, in_order(): return jnp.concatenate([lead, tail], axis=axis)  7.26 us
    select_n x5, other arithmetic, in_order(): lead = jnp.where(first_is_mine, mine, other)  6.97 us
  transfers between devices with their start and end apart: 13, of which 7 were waited for; matrix products, arithmetic and copies ran while one was open for 9% of the time, Pallas kernels for 14%

profile of v5, /device:TPU:24, one launch (start us, length us, event | category | flops | bytes accessed | tf_op | source)
XLA Modules:
  0.0 264.5 jit_solution(7580703216394372317)
XLA Ops:
  0.0 3.2 %dynamic-slice_select_fusion = bf16[1024,1024]{1,0:T(8,128)(2,1)S(1)} fusion(bf16[1024,2048]{1,0:T(8,128)(2,1)} %param.7, s32[]{:T(128)S(6)} %select_n.150, bf16[1024,2048]{1,0:T(8,128)(2,1)} %param.6, pred[]{:T(512)S(6)} %eq.9), kind=kLoop, calls=%fused_computation.6 | loop fusion | flops 1048576 | bytes 6291461 | tf_op jit(solution)/shard_map/jit(_where)/select_n | solution.py:127
  3.2 0.2 fusion.14
  3.3 1.6 collective-permute-start
  4.9 2.1 collective-permute-start.1
  7.0 21.3 %collective-permute-done = bf16[1024,512]{1,0:T(8,128)(2,1)S(1)} collective-permute-done((bf16[1024,512]{1,0:T(8,128)(2,1)S(1)}, bf16[1024,512]{1,0:T(8,128)(2,1)S(1)}, u32[]{:S(2)}, u32[]{:S(2)}) %collective-permute-start) | collective-permute-done | bytes 1048608 | tf_op jit(solution)/shard_map/ppermute | solution.py:23
  28.3 2.4 collective-permute-done.1
  30.8 0.1 constant_dynamic-update-slice_fusion.1
  30.9 0.2 constant_dynamic-update-slice_fusion
  31.1 0.1 collective-permute-start.3
  31.2 0.0 copy-start.2
  31.2 0.1 collective-permute-start.2
  31.3 4.2 %collective-permute-done.3 = bf16[1024,1024]{1,0:T(8,128)(2,1)} collective-permute-done((bf16[1024,1024]{1,0:T(8,128)(2,1)S(1)}, bf16[1024,1024]{1,0:T(8,128)(2,1)}, u32[]{:S(2)}, u32[]{:S(2)}) %collective-permute-start.3) | collective-permute-done | bytes 2097184 | tf_op jit(solution)/shard_map/ppermute | solution.py:139
  35.5 4.4 %broadcast_select_fusion.3 = (bf16[1024,1024]{1,0:T(8,128)(2,1)S(1)}, bf16[1024,1024]{1,0:T(8,128)(2,1)S(1)}, bf16[1024,1024]{1,0:T(8,128)(2,1)S(1)}, bf16[1024,1024]{1,0:T(8,128)(2,1)S(1)}) fusion(pred[]{:T(512)S(6)} %eq.8, bf16[1024,2048]{1,0:T(8,128)(2,1)} %param.6, s32[]{:T(128)S(6)} %select_n.155, ...), kind=kLoop, calls=%fused_computation.10 | loop fusion | flops 6291456 | bytes 16777222 | tf_op jit(solution)/shard_map/jit(_where)/select_n | solution.py:27
  39.9 0.0 copy-done.2
  39.9 1.8 fusion.6
  41.7 1.8 fusion.4
  43.5 0.0 copy-start.1
  43.5 1.3 pad_maximum_fusion.6
  44.7 2.0 collective-permute-start.4
  46.8 0.0 copy-done.1
  46.8 1.3 constant_dynamic-slice_fusion
  48.1 87.5 %collective-permute-done.2 = bf16[384,2048]{1,0:T(8,128)(2,1)S(1)} collective-permute-done((bf16[384,2048]{1,0:T(8,128)(2,1)}, bf16[384,2048]{1,0:T(8,128)(2,1)S(1)}, u32[]{:S(2)}, u32[]{:S(2)}) %collective-permute-start.2) | collective-permute-done | bytes 1572896 | tf_op jit(solution)/shard_map/ppermute | solution.py:23
  135.6 0.0 collective-permute-done.4
  135.6 1.8 fusion.8
  137.4 1.8 fusion.9
  139.2 0.1 pad_maximum_fusion.7
  139.3 1.9 collective-permute-start.9
  141.3 1.9 collective-permute-start.6
  143.2 2.5 collective-permute-start.7
  145.7 1.9 collective-permute-start.8
  147.6 32.2 %collective-permute-done.9 = bf16[2,384,1024]{2,1,0:T(8,128)(2,1)} collective-permute-done((bf16[2,384,1024]{2,1,0:T(8,128)(2,1)S(1)}, bf16[2,384,1024]{2,1,0:T(8,128)(2,1)}, u32[]{:S(2)}, u32[]{:S(2)}) %collective-permute-start.9) | collective-permute-done | bytes 1572896 | tf_op jit(solution)/shard_map/ppermute | solution.py:19
  179.8 2.5 collective-permute-start.10
  182.3 0.7 pad_add_fusion.seg_ref
  183.0 0.6 pad_add_fusion.1.seg_ref
  183.5 0.4 collective-permute-start.5
  183.9 0.2 bitcast_select_fusion.1
  184.2 2.0 pad_maximum_fusion.10
  186.2 2.0 select_bitcast_fusion.1
  188.2 2.0 pad_maximum_fusion.9
  190.2 0.0 collective-permute-done.6
  190.2 0.0 collective-permute-done.7
  190.2 1.6 broadcast_select_fusion.7
  191.8 7.7 %collective-permute-done.8 = bf16[2,384,1024]{2,1,0:T(8,128)(2,1)} collective-permute-done((bf16[2,384,1024]{2,1,0:T(8,128)(2,1)S(1)}, bf16[2,384,1024]{2,1,0:T(8,128)(2,1)}, u32[]{:S(2)}, u32[]{:S(2)}) %collective-permute-start.8) | collective-permute-done | bytes 1572896 | tf_op jit(solution)/shard_map/ppermute | solution.py:157
  199.5 0.0 collective-permute-done.10
  199.5 1.6 broadcast_select_fusion.6
  201.1 0.2 select_bitcast_fusion.3
  201.3 2.0 pad_maximum_fusion.8
  203.3 24.4 %shard_map.46 = bf16[384,1024]{1,0:T(8,128)(2,1)} custom-call(s32[2]{0:T(128)} %pad_add_fusion.seg_ref, bf16[384,1024]{1,0:T(8,128)(2,1)} %get-tuple-element.47.q_ref, bf16[768,1024]{1,0:T(8,128)(2,1)} %get-tuple-element.49.k2_ref, bf16[768,1024]{1,0:T(8,128)(2,1)} %get-tuple-element.51.k1_ref, bf16[768,1024]{1,0:T(8,128)(2,1)} %get-tuple-element.53.k0_ref, ...), custom_call_target="tpu_custom_call" | custom-call | tf_op jit(solution)/shard_map/pallas_call | solution.py:99
  227.7 0.0 collective-permute-done.5.q_ref
  227.7 13.5 %shard_map.47 = bf16[384,512]{1,0:T(8,128)(2,1)} custom-call(s32[2]{0:T(128)} %pad_add_fusion.1.seg_ref, bf16[384,1024]{1,0:T(8,128)(2,1)} %collective-permute-done.5.q_ref, bf16[768,1024]{1,0:T(8,128)(2,1)} %get-tuple-element.49.k2_ref, bf16[768,1024]{1,0:T(8,128)(2,1)} %get-tuple-element.51.k1_ref, bf16[768,1024]{1,0:T(8,128)(2,1)} %get-tuple-element.53.k0_ref, ...), custom_call_target="tpu_custom_call" | custom-call | tf_op jit(solution)/shard_map/pallas_call | solution.py:99
  241.2 0.4 collective-permute-start.11
  241.5 13.6 %shard_map.48 = bf16[384,512]{1,0:T(8,128)(2,1)} custom-call(s32[2]{0:T(128)} %pad_add_fusion.1.seg_ref, bf16[384,1024]{1,0:T(8,128)(2,1)} %collective-permute-done.5.q_ref, bf16[768,1024]{1,0:T(8,128)(2,1)} %get-tuple-element.49.k2_ref, bf16[768,1024]{1,0:T(8,128)(2,1)} %get-tuple-element.51.k1_ref, bf16[768,1024]{1,0:T(8,128)(2,1)} %get-tuple-element.53.k0_ref, ...), custom_call_target="tpu_custom_call" | custom-call | tf_op jit(solution)/shard_map/pallas_call | solution.py:99
  255.1 0.0 copy-start
  255.1 1.7 collective-permute-start.12
  256.8 0.0 collective-permute-done.11
  256.8 6.3 %collective-permute-done.12 = bf16[384,512]{1,0:T(8,128)(2,1)S(1)} collective-permute-done((bf16[384,512]{1,0:T(8,128)(2,1)}, bf16[384,512]{1,0:T(8,128)(2,1)S(1)}, u32[]{:S(2)}, u32[]{:S(2)}) %collective-permute-start.12) | collective-permute-done | bytes 393248 | tf_op jit(solution)/shard_map/ppermute | solution.py:23
  263.1 0.0 copy-done
  263.1 0.1 broadcast_select_fusion.9
  263.3 1.2 pad_maximum_fusion.14
  (2 shorter events, 0.1 us)
Async XLA Ops:
  3.3 25.0 %collective-permute-start = (bf16[1024,512]{1,0:T(8,128)(2,1)S(1)}, bf16[1024,512]{1,0:T(8,128)(2,1)S(1)}, u32[]{:S(2)}, u32[]{:S(2)}) collective-permute-start(bf16[1024,512]{1,0:T(8,128)(2,1)S(1)} %get-tuple-element.42), channel_id=1, source_target_pairs={{0,1},{1,0},{2,3},{3,2},{4,5},{5,4},{6,7},{7,6},{8,9},{9,8},{10,11... | collective-permute-start | bytes 3145736 | tf_op jit(solution)/shard_map/ppermute | solution.py:23
  4.9 25.8 %collective-permute-start.1 = (bf16[1024,512]{1,0:T(8,128)(2,1)S(1)}, bf16[1024,512]{1,0:T(8,128)(2,1)S(1)}, u32[]{:S(2)}, u32[]{:S(2)}) collective-permute-start(bf16[1024,512]{1,0:T(8,128)(2,1)S(1)} %get-tuple-element.41), channel_id=1, source_target_pairs={{33,0},{32,1},{35,2},{34,3},{37,4},{36,5},{39,6},{38,7},{41,8},{40... | collective-permute-start | bytes 3145736 | tf_op jit(solution)/shard_map/ppermute | solution.py:134
  31.1 4.4 %collective-permute-start.3 = (bf16[1024,1024]{1,0:T(8,128)(2,1)S(1)}, bf16[1024,1024]{1,0:T(8,128)(2,1)}, u32[]{:S(2)}, u32[]{:S(2)}) collective-permute-start(bf16[1024,1024]{1,0:T(8,128)(2,1)S(1)} %constant_dynamic-update-slice_fusion), channel_id=1, source_target_pairs={{0,2},{2,0},{4,6},{6,4},{8,10},{10,8},{12,14},{14,12},{16,18},{18,... | collective-permute-start | bytes 6291464 | tf_op jit(solution)/shard_map/ppermute | solution.py:139
  31.2 8.7 %copy-start.2 = (bf16[384,2048]{1,0:T(8,128)(2,1)S(1)}, bf16[384,2048]{1,0:T(8,128)(2,1)}, u32[]{:S(2)}) copy-start(bf16[384,2048]{1,0:T(8,128)(2,1)} %param.4) | copy-start | bytes 4718596
  31.2 104.4 %collective-permute-start.2 = (bf16[384,2048]{1,0:T(8,128)(2,1)}, bf16[384,2048]{1,0:T(8,128)(2,1)S(1)}, u32[]{:S(2)}, u32[]{:S(2)}) collective-permute-start(bf16[384,2048]{1,0:T(8,128)(2,1)} %param.4), channel_id=1, source_target_pairs={{0,1},{1,0},{2,3},{3,2},{4,5},{5,4},{6,7},{7,6},{8,9},{9,8},{10,11... | collective-permute-start | bytes 4718600 | tf_op jit(solution)/shard_map/ppermute | solution.py:23
  43.5 3.3 %copy-start.1 = (bf16[384,2048]{1,0:T(8,128)(2,1)S(1)}, bf16[384,2048]{1,0:T(8,128)(2,1)}, u32[]{:S(2)}) copy-start(bf16[384,2048]{1,0:T(8,128)(2,1)} %param.5) | copy-start | bytes 4718596
  44.7 90.8 %collective-permute-start.4 = (bf16[2,384,1024]{2,1,0:T(8,128)(2,1)}, bf16[2,384,1024]{2,1,0:T(8,128)(2,1)}, u32[]{:S(2)}, u32[]{:S(2)}) collective-permute-start(bf16[2,384,1024]{2,1,0:T(8,128)(2,1)} %pad_maximum_fusion.6), channel_id=1, source_target_pairs={{0,2},{2,4},{4,6},{6,8},{8,10},{10,12},{12,14},{14,16},{16,18},{18... | collective-permute-start | bytes 4718600 | tf_op jit(solution)/shard_map/ppermute | solution.py:19
  139.3 40.5 %collective-permute-start.9 = (bf16[2,384,1024]{2,1,0:T(8,128)(2,1)S(1)}, bf16[2,384,1024]{2,1,0:T(8,128)(2,1)}, u32[]{:S(2)}, u32[]{:S(2)}) collective-permute-start(bf16[2,384,1024]{2,1,0:T(8,128)(2,1)S(1)} %pad_maximum_fusion.7), channel_id=1, source_target_pairs={{0,2},{2,4},{4,6},{6,8},{8,10},{10,12},{12,14},{14,16},{16,18},{18... | collective-permute-start | bytes 4718600 | tf_op jit(solution)/shard_map/ppermute | solution.py:19
  141.3 49.0 %collective-permute-start.6 = (bf16[2,384,1024]{2,1,0:T(8,128)(2,1)}, bf16[2,384,1024]{2,1,0:T(8,128)(2,1)}, u32[]{:S(2)}, u32[]{:S(2)}) collective-permute-start(bf16[2,384,1024]{2,1,0:T(8,128)(2,1)} %pad_maximum_fusion.6), channel_id=1, source_target_pairs={{0,4},{4,8},{8,12},{12,16},{16,20},{20,24},{24,28},{28,32},{32,36}... | collective-permute-start | bytes 4718600 | tf_op jit(solution)/shard_map/ppermute | solution.py:157
  143.2 47.0 %collective-permute-start.7 = (bf16[2,384,1024]{2,1,0:T(8,128)(2,1)}, bf16[2,384,1024]{2,1,0:T(8,128)(2,1)}, u32[]{:S(2)}, u32[]{:S(2)}) collective-permute-start(bf16[2,384,1024]{2,1,0:T(8,128)(2,1)} %collective-permute-done.4), channel_id=1, source_target_pairs={{0,2},{4,6},{8,10},{12,14},{16,18},{20,22},{24,26},{28,30},{32,34}... | collective-permute-start | bytes 4718600 | tf_op jit(solution)/shard_map/ppermute | solution.py:158
  145.7 53.8 %collective-permute-start.8 = (bf16[2,384,1024]{2,1,0:T(8,128)(2,1)S(1)}, bf16[2,384,1024]{2,1,0:T(8,128)(2,1)}, u32[]{:S(2)}, u32[]{:S(2)}) collective-permute-start(bf16[2,384,1024]{2,1,0:T(8,128)(2,1)S(1)} %pad_maximum_fusion.7), channel_id=1, source_target_pairs={{0,4},{4,8},{8,12},{12,16},{16,20},{20,24},{24,28},{28,32},{32,36}... | collective-permute-start | bytes 4718600 | tf_op jit(solution)/shard_map/ppermute | solution.py:157
  179.8 19.7 %collective-permute-start.10 = (bf16[2,384,1024]{2,1,0:T(8,128)(2,1)}, bf16[2,384,1024]{2,1,0:T(8,128)(2,1)}, u32[]{:S(2)}, u32[]{:S(2)}) collective-permute-start(bf16[2,384,1024]{2,1,0:T(8,128)(2,1)} %collective-permute-done.9), channel_id=1, source_target_pairs={{0,2},{4,6},{8,10},{12,14},{16,18},{20,22},{24,26},{28,30},{32,34}... | collective-permute-start | bytes 4718600 | tf_op jit(solution)/shard_map/ppermute | solution.py:158
  183.5 44.1 %collective-permute-start.5 = (bf16[384,1024]{1,0:T(8,128)(2,1)}, bf16[384,1024]{1,0:T(8,128)(2,1)}, u32[]{:S(2)}, u32[]{:S(2)}) collective-permute-start(bf16[384,1024]{1,0:T(8,128)(2,1)} %get-tuple-element.18), channel_id=1, source_target_pairs={{0,1},{1,0},{2,3},{3,2},{4,5},{5,4},{6,7},{7,6},{8,9},{9,8},{10,11... | collective-permute-start | bytes 2359304 | tf_op jit(solution)/shard_map/ppermute | solution.py:23
  241.2 15.6 %collective-permute-start.11 = (bf16[384,512]{1,0:T(8,128)(2,1)}, bf16[384,512]{1,0:T(8,128)(2,1)S(1)}, u32[]{:S(2)}, u32[]{:S(2)}) collective-permute-start(bf16[384,512]{1,0:T(8,128)(2,1)} %shard_map.47), channel_id=1, source_target_pairs={{0,1},{1,0},{2,3},{3,2},{4,5},{5,4},{6,7},{7,6},{8,9},{9,8},{10,11... | collective-permute-start | bytes 1179656 | tf_op jit(solution)/shard_map/ppermute | solution.py:23
  255.1 8.0 %copy-start = (bf16[384,1024]{1,0:T(8,128)(2,1)S(1)}, bf16[384,1024]{1,0:T(8,128)(2,1)}, u32[]{:S(2)}) copy-start(bf16[384,1024]{1,0:T(8,128)(2,1)} %shard_map.46) | copy-start | bytes 2359300
  255.1 8.0 %collective-permute-start.12 = (bf16[384,512]{1,0:T(8,128)(2,1)}, bf16[384,512]{1,0:T(8,128)(2,1)S(1)}, u32[]{:S(2)}, u32[]{:S(2)}) collective-permute-start(bf16[384,512]{1,0:T(8,128)(2,1)} %shard_map.48), channel_id=1, source_target_pairs={{0,1},{1,0},{2,3},{3,2},{4,5},{5,4},{6,7},{7,6},{8,9},{9,8},{10,11... | collective-permute-start | bytes 1179656 | tf_op jit(solution)/shard_map/ppermute | solution.py:23

commit v6 on v4

--- a/solution.py
+++ b/solution.py
@@ -32,66 +32,78 @@
 def attention_kernel(seg_ref, q_ref, k2_ref, k1_ref, k0_ref, v2_ref, v1_ref, v0_ref, o_ref):
     seg = seg_ref[0]
     first_row = seg_ref[1]
-    query = q_ref[...]
+    count = q_ref.shape[0]
     seg_rows = k0_ref.shape[0]
-    count = query.shape[0]
     dims = (((1,), (1,)), ((), ()))
+    low = jnp.float32(-1e30)
 
-    def scores_of(key_ref):
-        raw = lax.dot_general(query, key_ref[...], dims, preferred_element_type=jnp.float32)
-        return raw * HD ** (-0.5)
+    def one_head(lanes, masked, own_rows):
+        query = q_ref[:, lanes]
 
-    col = lax.broadcasted_iota(jnp.int32, (count, seg_rows), 1)
-    row = lax.broadcasted_iota(jnp.int32, (count, seg_rows), 0) + first_row
-    low = jnp.float32(-1e30)
-    s0 = jnp.where(col <= row, scores_of(k0_ref), low)
-    top0 = jnp.max(s0, axis=1, keepdims=True)
+        def scores_of(key):
+            raw = lax.dot_general(query, key, dims, preferred_element_type=jnp.float32)
+            return raw * HD ** (-0.5)
 
-    def finish(s2, s1, e2_of, e1_of):
+        own_col = lax.broadcasted_iota(jnp.int32, (count, own_rows), 1)
+        own_row = lax.broadcasted_iota(jnp.int32, (count, own_rows), 0) + first_row
+        causal = own_col <= own_row
+        s0 = jnp.where(causal, scores_of(k0_ref[:own_rows, lanes]), low)
+        s2 = scores_of(k2_ref[:, lanes])
+        s1 = scores_of(k1_ref[:, lanes])
+        if masked:
+            col = lax.broadcasted_iota(jnp.int32, (count, seg_rows), 1)
+            ok2 = col < jnp.where(seg >= 2, seg_rows, 0)
+            ok1 = col < jnp.where(seg >= 1, seg_rows, 0)
+            s2 = jnp.where(ok2, s2, low)
+            s1 = jnp.where(ok1, s1, low)
         top = jnp.maximum(
-            jnp.maximum(jnp.max(s2, axis=1, keepdims=True), jnp.max(s1, axis=1, keepdims=True)), top0
+            jnp.maximum(jnp.max(s2, axis=1, keepdims=True), jnp.max(s1, axis=1, keepdims=True)),
+            jnp.max(s0, axis=1, keepdims=True),
         )
-        e2 = e2_of(s2, top)
-        e1 = e1_of(s1, top)
-        e0 = jnp.where(col <= row, jnp.exp(s0 - top), 0.0)
+        e2 = jnp.exp(s2 - top)
+        e1 = jnp.exp(s1 - top)
+        if masked:
+            e2 = jnp.where(ok2, e2, 0.0)
+            e1 = jnp.where(ok1, e1, 0.0)
+        e0 = jnp.where(causal, jnp.exp(s0 - top), 0.0)
         total = (
             jnp.sum(e2, axis=1, keepdims=True)
             + jnp.sum(e1, axis=1, keepdims=True)
             + jnp.sum(e0, axis=1, keepdims=True)
         )
-        mixed = jnp.dot(e2.astype(jnp.bfloat16), v2_ref[...], preferred_element_type=jnp.float32)
-        mixed = mixed + jnp.dot(e1.astype(jnp.bfloat16), v1_ref[...], preferred_element_type=jnp.float32)
-        mixed = mixed + jnp.dot(e0.astype(jnp.bfloat16), v0_ref[...], preferred_element_type=jnp.float32)
-        o_ref[...] = (mixed / total).astype(o_ref.dtype)
+        mixed = jnp.dot(e2.astype(jnp.bfloat16), v2_ref[:, lanes], preferred_element_type=jnp.float32)
+        mixed = mixed + jnp.dot(e1.astype(jnp.bfloat16), v1_ref[:, lanes], preferred_element_type=jnp.float32)
+        mixed = mixed + jnp.dot(
+            e0.astype(jnp.bfloat16), v0_ref[:own_rows, lanes], preferred_element_type=jnp.float32
+        )
+        o_ref[:, lanes] = (mixed / total).astype(o_ref.dtype)
 
-    @pl.when(seg >= MEM)
+    def run(masked, own_rows):
+        for head in range(q_ref.shape[1] // HD):
+            one_head(slice(head * HD, (head + 1) * HD), masked, own_rows)
+
+    early = first_row + count <= count
+
+    @pl.when(early)
     def _():
-        plain = lambda s, top: jnp.exp(s - top)
-        finish(scores_of(k2_ref), scores_of(k1_ref), plain, plain)
+        run(True, count)
 
-    @pl.when(seg < MEM)
+    @pl.when(jnp.logical_not(early))
     def _():
-        ok2 = col < jnp.where(seg >= 2, seg_rows, 0)
-        ok1 = col < jnp.where(seg >= 1, seg_rows, 0)
-        s2 = jnp.where(ok2, scores_of(k2_ref), low)
-        s1 = jnp.where(ok1, scores_of(k1_ref), low)
-        finish(
-            s2,
-            s1,
-            lambda s, top: jnp.where(ok2, jnp.exp(s - top), 0.0),
-            lambda s, top: jnp.where(ok1, jnp.exp(s - top), 0.0),
-        )
+        run(True, seg_rows)
 
 
 def attend(seg_number, first_row, query_rows, keys, values, head_lo, head_count):
     count = query_rows.shape[0]
     seg_rows = keys[0].shape[0]
-    q_spec = pl.BlockSpec((count, HD), lambda h, scalars: (0, h + head_lo))
-    kv_spec = pl.BlockSpec((seg_rows, HD), lambda h, scalars: (0, h + head_lo))
-    o_spec = pl.BlockSpec((count, HD), lambda h, scalars: (0, h))
+    step = 1
+    width = step * HD
+    q_spec = pl.BlockSpec((count, width), lambda h, scalars: (0, h + head_lo // step))
+    kv_spec = pl.BlockSpec((seg_rows, width), lambda h, scalars: (0, h + head_lo // step))
+    o_spec = pl.BlockSpec((count, width), lambda h, scalars: (0, h))
     grid_spec = pltpu.PrefetchScalarGridSpec(
         num_scalar_prefetch=1,
-        grid=(head_count,),
+        grid=(head_count // step,),
         in_specs=[q_spec] + [kv_spec] * 6,
         out_specs=o_spec,
     )
@@ -169,8 +181,9 @@
     mine_rows = attend(seg_number, half_number * tok_rows, mine_of(queries), keys, values, 0, heads)
     query_got, mine_rows = lax.optimization_barrier((query_got, mine_rows))
     got = []
-    for head_lo in range(0, heads, heads // 2):
-        their_rows = attend(seg_number, other_half * tok_rows, query_got, keys, values, head_lo, heads // 2)
+    lead = heads - heads // 4
+    for head_lo, head_count in ((0, lead), (lead, heads - lead)):
+        their_rows = attend(seg_number, other_half * tok_rows, query_got, keys, values, head_lo, head_count)
         got.append(swap_halves(their_rows))
     rows_got = jnp.concatenate(got, axis=1)
     return in_order(first_is_mine, mine_rows, rows_got, 1)

time: 219 us -> 215 us (0.982)
  Pallas kernels: 51.4 us -> 46.8 us
    pallas_call x3, Pallas kernels: 51.4 us -> 46.8 us  [attend(): pl.pallas_call(attention_kernel, grid_spec=grid_spec, out_shape=jax.Shape...]
  transfers between devices with their start and end apart: 13 -> 13, of which waited for: 6 -> 7; matrix products, arithmetic and copies ran while one was open for 5% -> 6% of each run, Pallas kernels for 17% -> 13%
where the time goes in v6:
time: 215 us; the launch traced here: 214 us
  waiting for transfers between devices  115 us (53%)
  Pallas kernels  46.8 us (22%)
  starting transfers between devices  24.3 us (11%)
  other arithmetic  17 us (8%)
  matrix products  6.85 us (3%)
  local copies, waits for them, and re-layouts  3.34 us (2%)
    ppermute x5, waiting for transfers between devices, swap_halves(): return lax.ppermute(value, 'fsdp', [(0, 1), (1, 0)])  57.4 us
    ppermute x2, waiting for transfers between devices, from_behind(): lax.ppermute(value, axis, [(source, source + steps) for source in range(l...  56.7 us
    pallas_call x3, Pallas kernels, attend(): pl.pallas_call(attention_kernel, grid_spec=grid_spec, out_shape=jax.Shape...  46.8 us
    select_n x3, other arithmetic, in_order(): lead = jnp.where(first_is_mine, mine, other)  5.88 us
    ppermute x2, starting transfers between devices, from_behind(): lax.ppermute(value, axis, [(source, source + steps) for source in range(l...  5.85 us
    ppermute x2, starting transfers between devices, shifted(): even_two = lax.ppermute(own, 'seg', even_pairs)  5.74 us
    ppermute x5, starting transfers between devices, swap_halves(): return lax.ppermute(value, 'fsdp', [(0, 1), (1, 0)])  5.67 us
    select_n x2, other arithmetic, shifted(): return (jnp.where(is_key_core, even_two, odd_two), one)  5.46 us
  transfers between devices with their start and end apart: 13, of which 7 were waited for; matrix products, arithmetic and copies ran while one was open for 6% of the time, Pallas kernels for 13%

profile of v6, /device:TPU:24, one launch (start us, length us, event | category | flops | bytes accessed | tf_op | source)
XLA Modules:
  0.0 213.8 jit_solution(16174694106054397503)
XLA Ops:
  0.0 3.2 %dynamic-slice_select_fusion = bf16[1024,1024]{1,0:T(8,128)(2,1)S(1)} fusion(bf16[1024,2048]{1,0:T(8,128)(2,1)} %param.7, s32[]{:T(128)S(6)} %select_n.88, bf16[1024,2048]{1,0:T(8,128)(2,1)} %param.6, pred[]{:T(512)S(6)} %eq.9), kind=kLoop, calls=%fused_computation.9 | loop fusion | flops 1048576 | bytes 6291461 | tf_op jit(solution)/shard_map/jit(_where)/select_n | solution.py:139
  3.2 0.2 fusion.16
  3.4 1.6 collective-permute-start.1
  4.9 2.1 collective-permute-start.2
  7.0 0.6 collective-permute-start
  7.6 21.9 %collective-permute-done.1 = bf16[1024,512]{1,0:T(8,128)(2,1)S(1)} collective-permute-done((bf16[1024,512]{1,0:T(8,128)(2,1)S(1)}, bf16[1024,512]{1,0:T(8,128)(2,1)S(1)}, u32[]{:S(2)}, u32[]{:S(2)}) %collective-permute-start.1) | collective-permute-done | bytes 1048608 | tf_op jit(solution)/shard_map/ppermute | solution.py:23
  29.5 0.1 constant_dynamic-update-slice_fusion.1
  29.6 1.1 collective-permute-done.2
  30.8 0.1 constant_dynamic-update-slice_fusion
  30.9 0.1 collective-permute-start.3
  31.0 0.0 copy-start.3
  31.0 2.8 %constant_dynamic-slice_fusion = (bf16[384,1024]{1,0:T(8,128)(2,1)}, bf16[384,1024]{1,0:T(8,128)(2,1)}) fusion(bf16[384,2048]{1,0:T(8,128)(2,1)} %param.5, s32[]{:T(128)S(6)} %select_n.93, s32[]{:T(128)S(6)} %select_n.88), kind=kLoop, calls=%fused_computation.29 | loop fusion | bytes 3145736 | tf_op jit(solution)/shard_map/dynamic_slice | solution.py:134
  33.8 0.0 copy-start.2
  33.8 28.3 %collective-permute-done = bf16[384,2048]{1,0:T(8,128)(2,1)} collective-permute-done((bf16[384,2048]{1,0:T(8,128)(2,1)}, bf16[384,2048]{1,0:T(8,128)(2,1)}, u32[]{:S(2)}, u32[]{:S(2)}) %collective-permute-start) | collective-permute-done | bytes 1572896 | tf_op jit(solution)/shard_map/ppermute | solution.py:23
  62.2 2.1 broadcast_select_fusion.9
  64.2 0.0 collective-permute-done.3
  64.3 0.0 copy-done.3
  64.3 0.0 copy-done.2
  64.3 3.7 %broadcast_select_fusion.3 = (bf16[1024,1024]{1,0:T(8,128)(2,1)S(1)}, bf16[1024,1024]{1,0:T(8,128)(2,1)S(1)}, bf16[1024,1024]{1,0:T(8,128)(2,1)S(1)}, bf16[1024,1024]{1,0:T(8,128)(2,1)S(1)}) fusion(pred[]{:T(512)S(6)} %eq.8, bf16[1024,2048]{1,0:T(8,128)(2,1)S(1)} %copy-done.2, s32[]{:T(128)S(6)} %select_n.93, bf16[1024,1024]{1,0:T(8,128)(2,1)} %collective-permute-done.3, ...), kind=kLoop, calls=%fused_computation.13 | loop fusion | flops 6291456 | bytes 16777222 | tf_op jit(solution)/shard_map/jit(_where)/select_n | solution.py:27
  68.0 3.4 %fusion.8.v0_ref = bf16[768,1024]{1,0:T(8,128)(2,1)S(1)} fusion(bf16[1024,1024]{1,0:T(8,128)(2,1)S(1)} %get-tuple-element.16, bf16[1024,1024]{1,0:T(8,128)(2,1)S(1)} %get-tuple-element.15, bf16[384,2048]{1,0:T(8,128)(2,1)S(1)} %get-tuple-element.22, bf16[384,2048]{1,0:T(8,128)(2,1)S(1)} %get-tuple-element.21), kind=kOutput, calls=%fused_computation.16 | convolution fusion | flops 3236691968 | bytes 8912896 | tf_op jit(solution)/shard_map/dot_general | solution.py:160
  71.4 0.0 copy-start
  71.4 3.4 %fusion.11.k0_ref = bf16[768,1024]{1,0:T(8,128)(2,1)S(1)} fusion(bf16[1024,1024]{1,0:T(8,128)(2,1)S(1)} %get-tuple-element.19, bf16[1024,1024]{1,0:T(8,128)(2,1)S(1)} %get-tuple-element.20, bf16[384,2048]{1,0:T(8,128)(2,1)S(1)} %get-tuple-element.22, bf16[384,2048]{1,0:T(8,128)(2,1)S(1)} %get-tuple-element.21), kind=kOutput, calls=%fused_computation.17 | convolution fusion | flops 3236691968 | bytes 8912896 | tf_op jit(solution)/shard_map/dot_general | solution.py:159
  74.8 0.0 copy-start.1
  74.9 1.9 collective-permute-start.9
  76.8 3.9 %collective-permute-start.6 = (bf16[768,1024]{1,0:T(8,128)(2,1)S(1)}, bf16[768,1024]{1,0:T(8,128)(2,1)}, u32[]{:S(2)}, u32[]{:S(2)}) collective-permute-start(bf16[768,1024]{1,0:T(8,128)(2,1)S(1)} %fusion.11.k0_ref), channel_id=1, source_target_pairs={{0,2},{2,4},{4,6},{6,8},{8,10},{10,12},{12,14},{14,16},{16,18},{18... | collective-permute-start | bytes 4718600 | tf_op jit(solution)/shard_map/ppermute | solution.py:19
  80.7 0.0 copy-done
  80.7 3.8 %collective-permute-start.8 = (bf16[768,1024]{1,0:T(8,128)(2,1)S(1)}, bf16[768,1024]{1,0:T(8,128)(2,1)}, u32[]{:S(2)}, u32[]{:S(2)}) collective-permute-start(bf16[768,1024]{1,0:T(8,128)(2,1)S(1)} %fusion.8.v0_ref), channel_id=1, source_target_pairs={{0,4},{4,8},{8,12},{12,16},{16,20},{20,24},{24,28},{28,32},{32,36}... | collective-permute-start | bytes 4718600 | tf_op jit(solution)/shard_map/ppermute | solution.py:171
  84.6 28.7 %collective-permute-done.9.v1_ref = bf16[768,1024]{1,0:T(8,128)(2,1)} collective-permute-done((bf16[768,1024]{1,0:T(8,128)(2,1)S(1)}, bf16[768,1024]{1,0:T(8,128)(2,1)}, u32[]{:S(2)}, u32[]{:S(2)}) %collective-permute-start.9) | collective-permute-done | bytes 1572896 | tf_op jit(solution)/shard_map/ppermute | solution.py:19
  113.3 2.5 %collective-permute-start.10 = (bf16[768,1024]{1,0:T(8,128)(2,1)}, bf16[768,1024]{1,0:T(8,128)(2,1)}, u32[]{:S(2)}, u32[]{:S(2)}) collective-permute-start(bf16[768,1024]{1,0:T(8,128)(2,1)} %collective-permute-done.9.v1_ref), channel_id=1, source_target_pairs={{0,2},{4,6},{8,10},{12,14},{16,18},{20,22},{24,26},{28,30},{32,34}... | collective-permute-start | bytes 4718600 | tf_op jit(solution)/shard_map/ppermute | solution.py:172
  115.7 1.9 collective-permute-start.5
  117.7 28.0 %collective-permute-done.6.k1_ref = bf16[768,1024]{1,0:T(8,128)(2,1)} collective-permute-done((bf16[768,1024]{1,0:T(8,128)(2,1)S(1)}, bf16[768,1024]{1,0:T(8,128)(2,1)}, u32[]{:S(2)}, u32[]{:S(2)}) %collective-permute-start.6) | collective-permute-done | bytes 1572896 | tf_op jit(solution)/shard_map/ppermute | solution.py:19
  145.7 2.4 %collective-permute-start.7 = (bf16[768,1024]{1,0:T(8,128)(2,1)}, bf16[768,1024]{1,0:T(8,128)(2,1)}, u32[]{:S(2)}, u32[]{:S(2)}) collective-permute-start(bf16[768,1024]{1,0:T(8,128)(2,1)} %collective-permute-done.6.k1_ref), channel_id=1, source_target_pairs={{0,2},{4,6},{8,10},{12,14},{16,18},{20,22},{24,26},{28,30},{32,34}... | collective-permute-start | bytes 4718600 | tf_op jit(solution)/shard_map/ppermute | solution.py:172
  148.1 0.7 pad_add_fusion.seg_ref
  148.8 1.1 collective-permute-start.4
  149.9 0.6 pad_add_fusion.1.seg_ref
  150.5 0.0 collective-permute-done.8
  150.5 0.0 collective-permute-done.10
  150.5 2.7 %broadcast_select_fusion.6.v2_ref = bf16[768,1024]{1,0:T(8,128)(2,1)} fusion(bf16[768,1024]{1,0:T(8,128)(2,1)} %collective-permute-done.8, bf16[768,1024]{1,0:T(8,128)(2,1)} %collective-permute-done.10, pred[]{:T(512)S(6)} %eq.9), kind=kLoop, calls=%fused_computation.19 | loop fusion | flops 786432 | bytes 4718593 | tf_op jit(solution)/shard_map/jit(_where)/select_n | solution.py:173
  153.2 0.0 copy-done.1
  153.2 0.0 collective-permute-done.5
  153.2 0.0 collective-permute-done.7
  153.2 2.7 %broadcast_select_fusion.7.k2_ref = bf16[768,1024]{1,0:T(8,128)(2,1)} fusion(bf16[768,1024]{1,0:T(8,128)(2,1)} %collective-permute-done.5, bf16[768,1024]{1,0:T(8,128)(2,1)} %collective-permute-done.7, pred[]{:T(512)S(6)} %eq.9), kind=kLoop, calls=%fused_computation.20 | loop fusion | flops 786432 | bytes 4718593 | tf_op jit(solution)/shard_map/jit(_where)/select_n | solution.py:173
  155.9 19.1 %shard_map.46 = bf16[384,1024]{1,0:T(8,128)(2,1)} custom-call(s32[2]{0:T(128)} %pad_add_fusion.seg_ref, bf16[384,1024]{1,0:T(8,128)(2,1)} %get-tuple-element.27.q_ref, bf16[768,1024]{1,0:T(8,128)(2,1)} %broadcast_select_fusion.7.k2_ref, bf16[768,1024]{1,0:T(8,128)(2,1)} %collective-permute-done.6.k1_ref, bf16[768,1024]{1,0:T(8,128)(2,1)} %copy-done.1, ...), custom_call_target="tpu_custom_call" | custom-call | tf_op jit(solution)/shard_map/pallas_call | solution.py:111
  175.0 0.0 collective-permute-done.4.q_ref
  175.0 19.5 %shard_map.47 = bf16[384,768]{1,0:T(8,128)(2,1)} custom-call(s32[2]{0:T(128)} %pad_add_fusion.1.seg_ref, bf16[384,1024]{1,0:T(8,128)(2,1)} %collective-permute-done.4.q_ref, bf16[768,1024]{1,0:T(8,128)(2,1)} %broadcast_select_fusion.7.k2_ref, bf16[768,1024]{1,0:T(8,128)(2,1)} %collective-permute-done.6.k1_ref, bf16[768,1024]{1,0:T(8,128)(2,1)} %copy-done.1, ...), custom_call_target="tpu_custom_call" | custom-call | tf_op jit(solution)/shard_map/pallas_call | solution.py:111
  194.5 2.4 %collective-permute-start.11 = (bf16[384,768]{1,0:T(8,128)(2,1)}, bf16[384,768]{1,0:T(8,128)(2,1)S(1)}, u32[]{:S(2)}, u32[]{:S(2)}) collective-permute-start(bf16[384,768]{1,0:T(8,128)(2,1)} %shard_map.47), channel_id=1, source_target_pairs={{0,1},{1,0},{2,3},{3,2},{4,5},{5,4},{6,7},{7,6},{8,9},{9,8},{10,11... | collective-permute-start | bytes 1769480 | tf_op jit(solution)/shard_map/ppermute | solution.py:23
  196.9 8.3 %shard_map.48 = bf16[384,256]{1,0:T(8,128)(2,1)} custom-call(s32[2]{0:T(128)} %pad_add_fusion.1.seg_ref, bf16[384,1024]{1,0:T(8,128)(2,1)} %collective-permute-done.4.q_ref, bf16[768,1024]{1,0:T(8,128)(2,1)} %broadcast_select_fusion.7.k2_ref, bf16[768,1024]{1,0:T(8,128)(2,1)} %collective-permute-done.6.k1_ref, bf16[768,1024]{1,0:T(8,128)(2,1)} %copy-done.1, ...), custom_call_target="tpu_custom_call" | custom-call | tf_op jit(solution)/shard_map/pallas_call | solution.py:111
  205.1 0.0 copy-start.4
  205.1 0.0 collective-permute-start.12
  205.1 5.2 %collective-permute-done.11 = bf16[384,768]{1,0:T(8,128)(2,1)S(1)} collective-permute-done((bf16[384,768]{1,0:T(8,128)(2,1)}, bf16[384,768]{1,0:T(8,128)(2,1)S(1)}, u32[]{:S(2)}, u32[]{:S(2)}) %collective-permute-start.11) | collective-permute-done | bytes 589856 | tf_op jit(solution)/shard_map/ppermute | solution.py:23
  210.4 0.1 constant_dynamic-update-slice_fusion.3
  210.4 2.0 collective-permute-done.12
  212.5 0.0 copy-done.4
  212.5 0.1 broadcast_select_fusion.11
  212.6 1.2 pad_maximum_fusion.7
  (1 shorter events, 0.0 us)
Async XLA Ops:
  3.4 26.1 %collective-permute-start.1 = (bf16[1024,512]{1,0:T(8,128)(2,1)S(1)}, bf16[1024,512]{1,0:T(8,128)(2,1)S(1)}, u32[]{:S(2)}, u32[]{:S(2)}) collective-permute-start(bf16[1024,512]{1,0:T(8,128)(2,1)S(1)} %get-tuple-element.24), channel_id=1, source_target_pairs={{0,1},{1,0},{2,3},{3,2},{4,5},{5,4},{6,7},{7,6},{8,9},{9,8},{10,11... | collective-permute-start | bytes 3145736 | tf_op jit(solution)/shard_map/ppermute | solution.py:23
  4.9 25.8 %collective-permute-start.2 = (bf16[1024,512]{1,0:T(8,128)(2,1)S(1)}, bf16[1024,512]{1,0:T(8,128)(2,1)S(1)}, u32[]{:S(2)}, u32[]{:S(2)}) collective-permute-start(bf16[1024,512]{1,0:T(8,128)(2,1)S(1)} %get-tuple-element.23), channel_id=1, source_target_pairs={{33,0},{32,1},{35,2},{34,3},{37,4},{36,5},{39,6},{38,7},{41,8},{40... | collective-permute-start | bytes 3145736 | tf_op jit(solution)/shard_map/ppermute | solution.py:146
  7.0 55.1 %collective-permute-start = (bf16[384,2048]{1,0:T(8,128)(2,1)}, bf16[384,2048]{1,0:T(8,128)(2,1)}, u32[]{:S(2)}, u32[]{:S(2)}) collective-permute-start(bf16[384,2048]{1,0:T(8,128)(2,1)} %param.4), channel_id=1, source_target_pairs={{0,1},{1,0},{2,3},{3,2},{4,5},{5,4},{6,7},{7,6},{8,9},{9,8},{10,11... | collective-permute-start | bytes 4718600 | tf_op jit(solution)/shard_map/ppermute | solution.py:23
  30.9 33.3 %collective-permute-start.3 = (bf16[1024,1024]{1,0:T(8,128)(2,1)S(1)}, bf16[1024,1024]{1,0:T(8,128)(2,1)}, u32[]{:S(2)}, u32[]{:S(2)}) collective-permute-start(bf16[1024,1024]{1,0:T(8,128)(2,1)S(1)} %constant_dynamic-update-slice_fusion), channel_id=1, source_target_pairs={{0,2},{2,0},{4,6},{6,4},{8,10},{10,8},{12,14},{14,12},{16,18},{18,... | collective-permute-start | bytes 6291464 | tf_op jit(solution)/shard_map/ppermute | solution.py:149
  31.0 33.2 %copy-start.3 = (bf16[1024,2048]{1,0:T(8,128)(2,1)S(1)}, bf16[1024,2048]{1,0:T(8,128)(2,1)}, u32[]{:S(2)}) copy-start(bf16[1024,2048]{1,0:T(8,128)(2,1)} %param.6) | copy-start | bytes 12582916
  33.8 30.4 %copy-start.2 = (bf16[1024,2048]{1,0:T(8,128)(2,1)S(1)}, bf16[1024,2048]{1,0:T(8,128)(2,1)}, u32[]{:S(2)}) copy-start(bf16[1024,2048]{1,0:T(8,128)(2,1)} %param.7) | copy-start | bytes 12582916
  71.4 9.3 %copy-start = (bf16[768,1024]{1,0:T(8,128)(2,1)}, bf16[768,1024]{1,0:T(8,128)(2,1)S(1)}, u32[]{:S(2)}) copy-start(bf16[768,1024]{1,0:T(8,128)(2,1)S(1)} %fusion.8.v0_ref) | copy-start | bytes 4718596
  74.8 78.4 %copy-start.1 = (bf16[768,1024]{1,0:T(8,128)(2,1)}, bf16[768,1024]{1,0:T(8,128)(2,1)S(1)}, u32[]{:S(2)}) copy-start(bf16[768,1024]{1,0:T(8,128)(2,1)S(1)} %fusion.11.k0_ref) | copy-start | bytes 4718596
  74.9 38.4 %collective-permute-start.9 = (bf16[768,1024]{1,0:T(8,128)(2,1)S(1)}, bf16[768,1024]{1,0:T(8,128)(2,1)}, u32[]{:S(2)}, u32[]{:S(2)}) collective-permute-start(bf16[768,1024]{1,0:T(8,128)(2,1)S(1)} %fusion.8.v0_ref), channel_id=1, source_target_pairs={{0,2},{2,4},{4,6},{6,8},{8,10},{10,12},{12,14},{14,16},{16,18},{18... | collective-permute-start | bytes 4718600 | tf_op jit(solution)/shard_map/ppermute | solution.py:19
  76.8 68.9 %collective-permute-start.6 = (bf16[768,1024]{1,0:T(8,128)(2,1)S(1)}, bf16[768,1024]{1,0:T(8,128)(2,1)}, u32[]{:S(2)}, u32[]{:S(2)}) collective-permute-start(bf16[768,1024]{1,0:T(8,128)(2,1)S(1)} %fusion.11.k0_ref), channel_id=1, source_target_pairs={{0,2},{2,4},{4,6},{6,8},{8,10},{10,12},{12,14},{14,16},{16,18},{18... | collective-permute-start | bytes 4718600 | tf_op jit(solution)/shard_map/ppermute | solution.py:19
  80.7 69.7 %collective-permute-start.8 = (bf16[768,1024]{1,0:T(8,128)(2,1)S(1)}, bf16[768,1024]{1,0:T(8,128)(2,1)}, u32[]{:S(2)}, u32[]{:S(2)}) collective-permute-start(bf16[768,1024]{1,0:T(8,128)(2,1)S(1)} %fusion.8.v0_ref), channel_id=1, source_target_pairs={{0,4},{4,8},{8,12},{12,16},{16,20},{20,24},{24,28},{28,32},{32,36}... | collective-permute-start | bytes 4718600 | tf_op jit(solution)/shard_map/ppermute | solution.py:171
  113.3 37.2 %collective-permute-start.10 = (bf16[768,1024]{1,0:T(8,128)(2,1)}, bf16[768,1024]{1,0:T(8,128)(2,1)}, u32[]{:S(2)}, u32[]{:S(2)}) collective-permute-start(bf16[768,1024]{1,0:T(8,128)(2,1)} %collective-permute-done.9.v1_ref), channel_id=1, source_target_pairs={{0,2},{4,6},{8,10},{12,14},{16,18},{20,22},{24,26},{28,30},{32,34}... | collective-permute-start | bytes 4718600 | tf_op jit(solution)/shard_map/ppermute | solution.py:172
  115.7 37.5 %collective-permute-start.5 = (bf16[768,1024]{1,0:T(8,128)(2,1)S(1)}, bf16[768,1024]{1,0:T(8,128)(2,1)}, u32[]{:S(2)}, u32[]{:S(2)}) collective-permute-start(bf16[768,1024]{1,0:T(8,128)(2,1)S(1)} %fusion.11.k0_ref), channel_id=1, source_target_pairs={{0,4},{4,8},{8,12},{12,16},{16,20},{20,24},{24,28},{28,32},{32,36}... | collective-permute-start | bytes 4718600 | tf_op jit(solution)/shard_map/ppermute | solution.py:171
  145.7 7.5 %collective-permute-start.7 = (bf16[768,1024]{1,0:T(8,128)(2,1)}, bf16[768,1024]{1,0:T(8,128)(2,1)}, u32[]{:S(2)}, u32[]{:S(2)}) collective-permute-start(bf16[768,1024]{1,0:T(8,128)(2,1)} %collective-permute-done.6.k1_ref), channel_id=1, source_target_pairs={{0,2},{4,6},{8,10},{12,14},{16,18},{20,22},{24,26},{28,30},{32,34}... | collective-permute-start | bytes 4718600 | tf_op jit(solution)/shard_map/ppermute | solution.py:172
  148.8 26.2 %collective-permute-start.4 = (bf16[384,1024]{1,0:T(8,128)(2,1)}, bf16[384,1024]{1,0:T(8,128)(2,1)}, u32[]{:S(2)}, u32[]{:S(2)}) collective-permute-start(bf16[384,1024]{1,0:T(8,128)(2,1)} %get-tuple-element.10), channel_id=1, source_target_pairs={{0,1},{1,0},{2,3},{3,2},{4,5},{5,4},{6,7},{7,6},{8,9},{9,8},{10,11... | collective-permute-start | bytes 2359304 | tf_op jit(solution)/shard_map/ppermute | solution.py:23
  194.5 15.9 %collective-permute-start.11 = (bf16[384,768]{1,0:T(8,128)(2,1)}, bf16[384,768]{1,0:T(8,128)(2,1)S(1)}, u32[]{:S(2)}, u32[]{:S(2)}) collective-permute-start(bf16[384,768]{1,0:T(8,128)(2,1)} %shard_map.47), channel_id=1, source_target_pairs={{0,1},{1,0},{2,3},{3,2},{4,5},{5,4},{6,7},{7,6},{8,9},{9,8},{10,11... | collective-permute-start | bytes 1769480 | tf_op jit(solution)/shard_map/ppermute | solution.py:23
  205.1 7.4 %copy-start.4 = (bf16[384,1024]{1,0:T(8,128)(2,1)S(1)}, bf16[384,1024]{1,0:T(8,128)(2,1)}, u32[]{:S(2)}) copy-start(bf16[384,1024]{1,0:T(8,128)(2,1)} %shard_map.46) | copy-start | bytes 2359300
  205.1 7.3 %collective-permute-start.12 = (bf16[384,256]{1,0:T(8,128)(2,1)}, bf16[384,256]{1,0:T(8,128)(2,1)S(1)}, u32[]{:S(2)}, u32[]{:S(2)}) collective-permute-start(bf16[384,256]{1,0:T(8,128)(2,1)} %shard_map.48), channel_id=1, source_target_pairs={{0,1},{1,0},{2,3},{3,2},{4,5},{5,4},{6,7},{7,6},{8,9},{9,8},{10,11... | collective-permute-start | bytes 589832 | tf_op jit(solution)/shard_map/ppermute | solution.py:23

commit v7 on v6

--- a/solution.py
+++ b/solution.py
@@ -178,13 +178,17 @@
     values = (value_two, value_one, own_value)
 
     heads = cols // HD
-    mine_rows = attend(seg_number, half_number * tok_rows, mine_of(queries), keys, values, 0, heads)
-    query_got, mine_rows = lax.optimization_barrier((query_got, mine_rows))
+    lead = heads - heads // 4
+    mine_q = mine_of(queries)
+    mine_lead = attend(seg_number, half_number * tok_rows, mine_q, keys, values, 0, lead)
+    query_got, mine_lead = lax.optimization_barrier((query_got, mine_lead))
     got = []
-    lead = heads - heads // 4
-    for head_lo, head_count in ((0, lead), (lead, heads - lead)):
-        their_rows = attend(seg_number, other_half * tok_rows, query_got, keys, values, head_lo, head_count)
+    for head_lo in range(0, heads, heads // 2):
+        their_rows = attend(seg_number, other_half * tok_rows, query_got, keys, values, head_lo, heads // 2)
         got.append(swap_halves(their_rows))
+    mine_q, their_rows = lax.optimization_barrier((mine_q, their_rows))
+    mine_tail = attend(seg_number, half_number * tok_rows, mine_q, keys, values, lead, heads - lead)
+    mine_rows = jnp.concatenate([mine_lead, mine_tail], axis=1)
     rows_got = jnp.concatenate(got, axis=1)
     return in_order(first_is_mine, mine_rows, rows_got, 1)
 

time: 215 us -> 213 us (level)
  waiting for transfers between devices: 115 us -> 110 us
  Pallas kernels: 46.8 us -> 49.6 us
    ppermute x5, waiting for transfers between devices: 57.4 us -> 51.8 us  [swap_halves(): return lax.ppermute(value, 'fsdp', [(0, 1), (1, 0)])]
    pallas_call x3 -> x4, Pallas kernels: 46.8 us -> 49.6 us  [attend(): pl.pallas_call(attention_kernel, grid_spec=grid_spec, out_shape=jax.Shape...]
  transfers between devices with their start and end apart: 13 -> 13, of which waited for: 7 -> 6; matrix products, arithmetic and copies ran while one was open for 6% -> 6% of each run, Pallas kernels for 13% -> 17%
where the time goes in v7:
time: 213 us; the launch traced here: 212 us
  waiting for transfers between devices  110 us (52%)
  Pallas kernels  49.6 us (23%)
  starting transfers between devices  24.3 us (11%)
  other arithmetic  18.2 us (9%)
  matrix products  6.85 us (3%)
  local copies, waits for them, and re-layouts  3.34 us (2%)
    ppermute x2, waiting for transfers between devices, from_behind(): lax.ppermute(value, axis, [(source, source + steps) for source in range(l...  56.7 us
    ppermute x5, waiting for transfers between devices, swap_halves(): return lax.ppermute(value, 'fsdp', [(0, 1), (1, 0)])  51.8 us
    pallas_call x4, Pallas kernels, attend(): pl.pallas_call(attention_kernel, grid_spec=grid_spec, out_shape=jax.Shape...  49.6 us
    select_n x3, other arithmetic, in_order(): lead = jnp.where(first_is_mine, mine, other)  7.07 us
    ppermute x2, starting transfers between devices, from_behind(): lax.ppermute(value, axis, [(source, source + steps) for source in range(l...  5.85 us
    ppermute x2, starting transfers between devices, shifted(): even_two = lax.ppermute(own, 'seg', even_pairs)  5.74 us
    ppermute x5, starting transfers between devices, swap_halves(): return lax.ppermute(value, 'fsdp', [(0, 1), (1, 0)])  5.67 us
    select_n x2, other arithmetic, shifted(): return (jnp.where(is_key_core, even_two, odd_two), one)  5.46 us
  transfers between devices with their start and end apart: 13, of which 6 were waited for; matrix products, arithmetic and copies ran while one was open for 6% of the time, Pallas kernels for 17%

profile of v7, /device:TPU:24, one launch (start us, length us, event | category | flops | bytes accessed | tf_op | source)
XLA Modules:
  0.0 212.3 jit_solution(2469396701168252490)
XLA Ops:
  0.0 3.2 %dynamic-slice_select_fusion = bf16[1024,1024]{1,0:T(8,128)(2,1)S(1)} fusion(bf16[1024,2048]{1,0:T(8,128)(2,1)} %param.7, s32[]{:T(128)S(6)} %select_n.88, bf16[1024,2048]{1,0:T(8,128)(2,1)} %param.6, pred[]{:T(512)S(6)} %eq.9), kind=kLoop, calls=%fused_computation.9 | loop fusion | flops 1048576 | bytes 6291461 | tf_op jit(solution)/shard_map/jit(_where)/select_n | solution.py:139
  3.2 0.2 fusion.16
  3.4 1.6 collective-permute-start.1
  4.9 2.1 collective-permute-start.2
  7.0 0.6 collective-permute-start
  7.6 21.9 %collective-permute-done.1 = bf16[1024,512]{1,0:T(8,128)(2,1)S(1)} collective-permute-done((bf16[1024,512]{1,0:T(8,128)(2,1)S(1)}, bf16[1024,512]{1,0:T(8,128)(2,1)S(1)}, u32[]{:S(2)}, u32[]{:S(2)}) %collective-permute-start.1) | collective-permute-done | bytes 1048608 | tf_op jit(solution)/shard_map/ppermute | solution.py:23
  29.5 0.1 constant_dynamic-update-slice_fusion.1
  29.6 1.1 collective-permute-done.2
  30.8 0.1 constant_dynamic-update-slice_fusion
  30.9 0.1 collective-permute-start.3
  31.0 0.0 copy-start.3
  31.0 2.8 %constant_dynamic-slice_fusion = (bf16[384,1024]{1,0:T(8,128)(2,1)}, bf16[384,1024]{1,0:T(8,128)(2,1)}) fusion(bf16[384,2048]{1,0:T(8,128)(2,1)} %param.5, s32[]{:T(128)S(6)} %select_n.93, s32[]{:T(128)S(6)} %select_n.88), kind=kLoop, calls=%fused_computation.30 | loop fusion | bytes 3145736 | tf_op jit(solution)/shard_map/dynamic_slice | solution.py:134
  33.8 0.0 copy-start.2
  33.8 28.3 %collective-permute-done = bf16[384,2048]{1,0:T(8,128)(2,1)} collective-permute-done((bf16[384,2048]{1,0:T(8,128)(2,1)}, bf16[384,2048]{1,0:T(8,128)(2,1)}, u32[]{:S(2)}, u32[]{:S(2)}) %collective-permute-start) | collective-permute-done | bytes 1572896 | tf_op jit(solution)/shard_map/ppermute | solution.py:23
  62.2 2.1 broadcast_select_fusion.9
  64.2 0.0 collective-permute-done.3
  64.3 0.0 copy-done.3
  64.3 0.0 copy-done.2
  64.3 3.7 %broadcast_select_fusion.3 = (bf16[1024,1024]{1,0:T(8,128)(2,1)S(1)}, bf16[1024,1024]{1,0:T(8,128)(2,1)S(1)}, bf16[1024,1024]{1,0:T(8,128)(2,1)S(1)}, bf16[1024,1024]{1,0:T(8,128)(2,1)S(1)}) fusion(pred[]{:T(512)S(6)} %eq.8, bf16[1024,2048]{1,0:T(8,128)(2,1)S(1)} %copy-done.2, s32[]{:T(128)S(6)} %select_n.93, bf16[1024,1024]{1,0:T(8,128)(2,1)} %collective-permute-done.3, ...), kind=kLoop, calls=%fused_computation.13 | loop fusion | flops 6291456 | bytes 16777222 | tf_op jit(solution)/shard_map/jit(_where)/select_n | solution.py:27
  68.0 3.4 %fusion.8.v0_ref = bf16[768,1024]{1,0:T(8,128)(2,1)S(1)} fusion(bf16[1024,1024]{1,0:T(8,128)(2,1)S(1)} %get-tuple-element.18, bf16[1024,1024]{1,0:T(8,128)(2,1)S(1)} %get-tuple-element.17, bf16[384,2048]{1,0:T(8,128)(2,1)S(1)} %get-tuple-element.24, bf16[384,2048]{1,0:T(8,128)(2,1)S(1)} %get-tuple-element.23), kind=kOutput, calls=%fused_computation.16 | convolution fusion | flops 3236691968 | bytes 8912896 | tf_op jit(solution)/shard_map/dot_general | solution.py:160
  71.4 0.0 copy-start
  71.4 3.4 %fusion.11.k0_ref = bf16[768,1024]{1,0:T(8,128)(2,1)S(1)} fusion(bf16[1024,1024]{1,0:T(8,128)(2,1)S(1)} %get-tuple-element.21, bf16[1024,1024]{1,0:T(8,128)(2,1)S(1)} %get-tuple-element.22, bf16[384,2048]{1,0:T(8,128)(2,1)S(1)} %get-tuple-element.24, bf16[384,2048]{1,0:T(8,128)(2,1)S(1)} %get-tuple-element.23), kind=kOutput, calls=%fused_computation.17 | convolution fusion | flops 3236691968 | bytes 8912896 | tf_op jit(solution)/shard_map/dot_general | solution.py:159
  74.8 0.0 copy-start.1
  74.9 1.9 collective-permute-start.9
  76.8 3.9 %collective-permute-start.6 = (bf16[768,1024]{1,0:T(8,128)(2,1)S(1)}, bf16[768,1024]{1,0:T(8,128)(2,1)}, u32[]{:S(2)}, u32[]{:S(2)}) collective-permute-start(bf16[768,1024]{1,0:T(8,128)(2,1)S(1)} %fusion.11.k0_ref), channel_id=1, source_target_pairs={{0,2},{2,4},{4,6},{6,8},{8,10},{10,12},{12,14},{14,16},{16,18},{18... | collective-permute-start | bytes 4718600 | tf_op jit(solution)/shard_map/ppermute | solution.py:19
  80.7 0.0 copy-done
  80.7 3.8 %collective-permute-start.8 = (bf16[768,1024]{1,0:T(8,128)(2,1)S(1)}, bf16[768,1024]{1,0:T(8,128)(2,1)}, u32[]{:S(2)}, u32[]{:S(2)}) collective-permute-start(bf16[768,1024]{1,0:T(8,128)(2,1)S(1)} %fusion.8.v0_ref), channel_id=1, source_target_pairs={{0,4},{4,8},{8,12},{12,16},{16,20},{20,24},{24,28},{28,32},{32,36}... | collective-permute-start | bytes 4718600 | tf_op jit(solution)/shard_map/ppermute | solution.py:171
  84.6 28.7 %collective-permute-done.9.v1_ref = bf16[768,1024]{1,0:T(8,128)(2,1)} collective-permute-done((bf16[768,1024]{1,0:T(8,128)(2,1)S(1)}, bf16[768,1024]{1,0:T(8,128)(2,1)}, u32[]{:S(2)}, u32[]{:S(2)}) %collective-permute-start.9) | collective-permute-done | bytes 1572896 | tf_op jit(solution)/shard_map/ppermute | solution.py:19
  113.3 2.5 %collective-permute-start.10 = (bf16[768,1024]{1,0:T(8,128)(2,1)}, bf16[768,1024]{1,0:T(8,128)(2,1)}, u32[]{:S(2)}, u32[]{:S(2)}) collective-permute-start(bf16[768,1024]{1,0:T(8,128)(2,1)} %collective-permute-done.9.v1_ref), channel_id=1, source_target_pairs={{0,2},{4,6},{8,10},{12,14},{16,18},{20,22},{24,26},{28,30},{32,34}... | collective-permute-start | bytes 4718600 | tf_op jit(solution)/shard_map/ppermute | solution.py:172
  115.7 1.9 collective-permute-start.5
  117.7 28.0 %collective-permute-done.6.k1_ref = bf16[768,1024]{1,0:T(8,128)(2,1)} collective-permute-done((bf16[768,1024]{1,0:T(8,128)(2,1)S(1)}, bf16[768,1024]{1,0:T(8,128)(2,1)}, u32[]{:S(2)}, u32[]{:S(2)}) %collective-permute-start.6) | collective-permute-done | bytes 1572896 | tf_op jit(solution)/shard_map/ppermute | solution.py:19
  145.7 2.4 %collective-permute-start.7 = (bf16[768,1024]{1,0:T(8,128)(2,1)}, bf16[768,1024]{1,0:T(8,128)(2,1)}, u32[]{:S(2)}, u32[]{:S(2)}) collective-permute-start(bf16[768,1024]{1,0:T(8,128)(2,1)} %collective-permute-done.6.k1_ref), channel_id=1, source_target_pairs={{0,2},{4,6},{8,10},{12,14},{16,18},{20,22},{24,26},{28,30},{32,34}... | collective-permute-start | bytes 4718600 | tf_op jit(solution)/shard_map/ppermute | solution.py:172
  148.1 0.6 pad_add_fusion.seg_ref
  148.7 1.1 collective-permute-start.4
  149.8 0.7 pad_add_fusion.1.seg_ref
  150.5 0.0 collective-permute-done.8
  150.5 0.0 collective-permute-done.10
  150.5 2.7 %broadcast_select_fusion.6.v2_ref = bf16[768,1024]{1,0:T(8,128)(2,1)} fusion(bf16[768,1024]{1,0:T(8,128)(2,1)} %collective-permute-done.8, bf16[768,1024]{1,0:T(8,128)(2,1)} %collective-permute-done.10, pred[]{:T(512)S(6)} %eq.9), kind=kLoop, calls=%fused_computation.19 | loop fusion | flops 786432 | bytes 4718593 | tf_op jit(solution)/shard_map/jit(_where)/select_n | solution.py:173
  153.2 0.0 copy-done.1
  153.2 0.0 collective-permute-done.5
  153.2 0.0 collective-permute-done.7
  153.2 2.7 %broadcast_select_fusion.7.k2_ref = bf16[768,1024]{1,0:T(8,128)(2,1)} fusion(bf16[768,1024]{1,0:T(8,128)(2,1)} %collective-permute-done.5, bf16[768,1024]{1,0:T(8,128)(2,1)} %collective-permute-done.7, pred[]{:T(512)S(6)} %eq.9), kind=kLoop, calls=%fused_computation.20 | loop fusion | flops 786432 | bytes 4718593 | tf_op jit(solution)/shard_map/jit(_where)/select_n | solution.py:173
  155.9 15.0 %shard_map.46 = bf16[384,768]{1,0:T(8,128)(2,1)} custom-call(s32[2]{0:T(128)} %pad_add_fusion.seg_ref, bf16[384,1024]{1,0:T(8,128)(2,1)} %get-tuple-element.16.q_ref, bf16[768,1024]{1,0:T(8,128)(2,1)} %broadcast_select_fusion.7.k2_ref, bf16[768,1024]{1,0:T(8,128)(2,1)} %collective-permute-done.6.k1_ref, bf16[768,1024]{1,0:T(8,128)(2,1)} %copy-done.1, ...), custom_call_target="tpu_custom_call" | custom-call | tf_op jit(solution)/shard_map/pallas_call | solution.py:111
  170.9 0.0 collective-permute-done.4.q_ref
  170.9 13.9 %shard_map.49 = bf16[384,512]{1,0:T(8,128)(2,1)} custom-call(s32[2]{0:T(128)} %pad_add_fusion.1.seg_ref, bf16[384,1024]{1,0:T(8,128)(2,1)} %collective-permute-done.4.q_ref, bf16[768,1024]{1,0:T(8,128)(2,1)} %broadcast_select_fusion.7.k2_ref, bf16[768,1024]{1,0:T(8,128)(2,1)} %collective-permute-done.6.k1_ref, bf16[768,1024]{1,0:T(8,128)(2,1)} %copy-done.1, ...), custom_call_target="tpu_custom_call" | custom-call | tf_op jit(solution)/shard_map/pallas_call | solution.py:111
  184.8 2.4 %collective-permute-start.11 = (bf16[384,512]{1,0:T(8,128)(2,1)}, bf16[384,512]{1,0:T(8,128)(2,1)S(1)}, u32[]{:S(2)}, u32[]{:S(2)}) collective-permute-start(bf16[384,512]{1,0:T(8,128)(2,1)} %shard_map.49), channel_id=1, source_target_pairs={{0,1},{1,0},{2,3},{3,2},{4,5},{5,4},{6,7},{7,6},{8,9},{9,8},{10,11... | collective-permute-start | bytes 1179656 | tf_op jit(solution)/shard_map/ppermute | solution.py:23
  187.2 13.9 %shard_map.47 = bf16[384,512]{1,0:T(8,128)(2,1)} custom-call(s32[2]{0:T(128)} %pad_add_fusion.1.seg_ref, bf16[384,1024]{1,0:T(8,128)(2,1)} %collective-permute-done.4.q_ref, bf16[768,1024]{1,0:T(8,128)(2,1)} %broadcast_select_fusion.7.k2_ref, bf16[768,1024]{1,0:T(8,128)(2,1)} %collective-permute-done.6.k1_ref, bf16[768,1024]{1,0:T(8,128)(2,1)} %copy-done.1, ...), custom_call_target="tpu_custom_call" | custom-call | tf_op jit(solution)/shard_map/pallas_call | solution.py:111
  201.1 0.0 copy-start.4
  201.1 0.0 collective-permute-start.12
  201.1 6.9 %shard_map.48 = bf16[384,256]{1,0:T(8,128)(2,1)} custom-call(s32[2]{0:T(128)} %pad_add_fusion.seg_ref, bf16[384,1024]{1,0:T(8,128)(2,1)} %get-tuple-element.16.q_ref, bf16[768,1024]{1,0:T(8,128)(2,1)} %broadcast_select_fusion.7.k2_ref, bf16[768,1024]{1,0:T(8,128)(2,1)} %collective-permute-done.6.k1_ref, bf16[768,1024]{1,0:T(8,128)(2,1)} %copy-done.1, ...), custom_call_target="tpu_custom_call" | custom-call | tf_op jit(solution)/shard_map/pallas_call | solution.py:111
  208.0 0.0 collective-permute-done.11
  208.0 1.7 collective-permute-done.12
  209.7 0.0 copy-done.4
  209.8 1.3 broadcast_select_fusion.11
  211.1 1.2 pad_maximum_fusion.7
  (2 shorter events, 0.1 us)
Async XLA Ops:
  3.4 26.1 %collective-permute-start.1 = (bf16[1024,512]{1,0:T(8,128)(2,1)S(1)}, bf16[1024,512]{1,0:T(8,128)(2,1)S(1)}, u32[]{:S(2)}, u32[]{:S(2)}) collective-permute-start(bf16[1024,512]{1,0:T(8,128)(2,1)S(1)} %get-tuple-element.26), channel_id=1, source_target_pairs={{0,1},{1,0},{2,3},{3,2},{4,5},{5,4},{6,7},{7,6},{8,9},{9,8},{10,11... | collective-permute-start | bytes 3145736 | tf_op jit(solution)/shard_map/ppermute | solution.py:23
  4.9 25.8 %collective-permute-start.2 = (bf16[1024,512]{1,0:T(8,128)(2,1)S(1)}, bf16[1024,512]{1,0:T(8,128)(2,1)S(1)}, u32[]{:S(2)}, u32[]{:S(2)}) collective-permute-start(bf16[1024,512]{1,0:T(8,128)(2,1)S(1)} %get-tuple-element.25), channel_id=1, source_target_pairs={{33,0},{32,1},{35,2},{34,3},{37,4},{36,5},{39,6},{38,7},{41,8},{40... | collective-permute-start | bytes 3145736 | tf_op jit(solution)/shard_map/ppermute | solution.py:146
  7.0 55.1 %collective-permute-start = (bf16[384,2048]{1,0:T(8,128)(2,1)}, bf16[384,2048]{1,0:T(8,128)(2,1)}, u32[]{:S(2)}, u32[]{:S(2)}) collective-permute-start(bf16[384,2048]{1,0:T(8,128)(2,1)} %param.4), channel_id=1, source_target_pairs={{0,1},{1,0},{2,3},{3,2},{4,5},{5,4},{6,7},{7,6},{8,9},{9,8},{10,11... | collective-permute-start | bytes 4718600 | tf_op jit(solution)/shard_map/ppermute | solution.py:23
  30.9 33.3 %collective-permute-start.3 = (bf16[1024,1024]{1,0:T(8,128)(2,1)S(1)}, bf16[1024,1024]{1,0:T(8,128)(2,1)}, u32[]{:S(2)}, u32[]{:S(2)}) collective-permute-start(bf16[1024,1024]{1,0:T(8,128)(2,1)S(1)} %constant_dynamic-update-slice_fusion), channel_id=1, source_target_pairs={{0,2},{2,0},{4,6},{6,4},{8,10},{10,8},{12,14},{14,12},{16,18},{18,... | collective-permute-start | bytes 6291464 | tf_op jit(solution)/shard_map/ppermute | solution.py:149
  31.0 33.2 %copy-start.3 = (bf16[1024,2048]{1,0:T(8,128)(2,1)S(1)}, bf16[1024,2048]{1,0:T(8,128)(2,1)}, u32[]{:S(2)}) copy-start(bf16[1024,2048]{1,0:T(8,128)(2,1)} %param.6) | copy-start | bytes 12582916
  33.8 30.4 %copy-start.2 = (bf16[1024,2048]{1,0:T(8,128)(2,1)S(1)}, bf16[1024,2048]{1,0:T(8,128)(2,1)}, u32[]{:S(2)}) copy-start(bf16[1024,2048]{1,0:T(8,128)(2,1)} %param.7) | copy-start | bytes 12582916
  71.4 9.3 %copy-start = (bf16[768,1024]{1,0:T(8,128)(2,1)}, bf16[768,1024]{1,0:T(8,128)(2,1)S(1)}, u32[]{:S(2)}) copy-start(bf16[768,1024]{1,0:T(8,128)(2,1)S(1)} %fusion.8.v0_ref) | copy-start | bytes 4718596
  74.8 78.4 %copy-start.1 = (bf16[768,1024]{1,0:T(8,128)(2,1)}, bf16[768,1024]{1,0:T(8,128)(2,1)S(1)}, u32[]{:S(2)}) copy-start(bf16[768,1024]{1,0:T(8,128)(2,1)S(1)} %fusion.11.k0_ref) | copy-start | bytes 4718596
  74.9 38.4 %collective-permute-start.9 = (bf16[768,1024]{1,0:T(8,128)(2,1)S(1)}, bf16[768,1024]{1,0:T(8,128)(2,1)}, u32[]{:S(2)}, u32[]{:S(2)}) collective-permute-start(bf16[768,1024]{1,0:T(8,128)(2,1)S(1)} %fusion.8.v0_ref), channel_id=1, source_target_pairs={{0,2},{2,4},{4,6},{6,8},{8,10},{10,12},{12,14},{14,16},{16,18},{18... | collective-permute-start | bytes 4718600 | tf_op jit(solution)/shard_map/ppermute | solution.py:19
  76.8 68.9 %collective-permute-start.6 = (bf16[768,1024]{1,0:T(8,128)(2,1)S(1)}, bf16[768,1024]{1,0:T(8,128)(2,1)}, u32[]{:S(2)}, u32[]{:S(2)}) collective-permute-start(bf16[768,1024]{1,0:T(8,128)(2,1)S(1)} %fusion.11.k0_ref), channel_id=1, source_target_pairs={{0,2},{2,4},{4,6},{6,8},{8,10},{10,12},{12,14},{14,16},{16,18},{18... | collective-permute-start | bytes 4718600 | tf_op jit(solution)/shard_map/ppermute | solution.py:19
  80.7 69.7 %collective-permute-start.8 = (bf16[768,1024]{1,0:T(8,128)(2,1)S(1)}, bf16[768,1024]{1,0:T(8,128)(2,1)}, u32[]{:S(2)}, u32[]{:S(2)}) collective-permute-start(bf16[768,1024]{1,0:T(8,128)(2,1)S(1)} %fusion.8.v0_ref), channel_id=1, source_target_pairs={{0,4},{4,8},{8,12},{12,16},{16,20},{20,24},{24,28},{28,32},{32,36}... | collective-permute-start | bytes 4718600 | tf_op jit(solution)/shard_map/ppermute | solution.py:171
  113.3 37.2 %collective-permute-start.10 = (bf16[768,1024]{1,0:T(8,128)(2,1)}, bf16[768,1024]{1,0:T(8,128)(2,1)}, u32[]{:S(2)}, u32[]{:S(2)}) collective-permute-start(bf16[768,1024]{1,0:T(8,128)(2,1)} %collective-permute-done.9.v1_ref), channel_id=1, source_target_pairs={{0,2},{4,6},{8,10},{12,14},{16,18},{20,22},{24,26},{28,30},{32,34}... | collective-permute-start | bytes 4718600 | tf_op jit(solution)/shard_map/ppermute | solution.py:172
  115.7 37.5 %collective-permute-start.5 = (bf16[768,1024]{1,0:T(8,128)(2,1)S(1)}, bf16[768,1024]{1,0:T(8,128)(2,1)}, u32[]{:S(2)}, u32[]{:S(2)}) collective-permute-start(bf16[768,1024]{1,0:T(8,128)(2,1)S(1)} %fusion.11.k0_ref), channel_id=1, source_target_pairs={{0,4},{4,8},{8,12},{12,16},{16,20},{20,24},{24,28},{28,32},{32,36}... | collective-permute-start | bytes 4718600 | tf_op jit(solution)/shard_map/ppermute | solution.py:171
  145.7 7.5 %collective-permute-start.7 = (bf16[768,1024]{1,0:T(8,128)(2,1)}, bf16[768,1024]{1,0:T(8,128)(2,1)}, u32[]{:S(2)}, u32[]{:S(2)}) collective-permute-start(bf16[768,1024]{1,0:T(8,128)(2,1)} %collective-permute-done.6.k1_ref), channel_id=1, source_target_pairs={{0,2},{4,6},{8,10},{12,14},{16,18},{20,22},{24,26},{28,30},{32,34}... | collective-permute-start | bytes 4718600 | tf_op jit(solution)/shard_map/ppermute | solution.py:172
  148.7 22.2 %collective-permute-start.4 = (bf16[384,1024]{1,0:T(8,128)(2,1)}, bf16[384,1024]{1,0:T(8,128)(2,1)}, u32[]{:S(2)}, u32[]{:S(2)}) collective-permute-start(bf16[384,1024]{1,0:T(8,128)(2,1)} %get-tuple-element.11), channel_id=1, source_target_pairs={{0,1},{1,0},{2,3},{3,2},{4,5},{5,4},{6,7},{7,6},{8,9},{9,8},{10,11... | collective-permute-start | bytes 2359304 | tf_op jit(solution)/shard_map/ppermute | solution.py:23
  184.8 23.2 %collective-permute-start.11 = (bf16[384,512]{1,0:T(8,128)(2,1)}, bf16[384,512]{1,0:T(8,128)(2,1)S(1)}, u32[]{:S(2)}, u32[]{:S(2)}) collective-permute-start(bf16[384,512]{1,0:T(8,128)(2,1)} %shard_map.49), channel_id=1, source_target_pairs={{0,1},{1,0},{2,3},{3,2},{4,5},{5,4},{6,7},{7,6},{8,9},{9,8},{10,11... | collective-permute-start | bytes 1179656 | tf_op jit(solution)/shard_map/ppermute | solution.py:23
  201.1 8.7 %copy-start.4 = (bf16[384,768]{1,0:T(8,128)(2,1)S(1)}, bf16[384,768]{1,0:T(8,128)(2,1)}, u32[]{:S(2)}) copy-start(bf16[384,768]{1,0:T(8,128)(2,1)} %shard_map.46) | copy-start | bytes 1769476
  201.1 8.6 %collective-permute-start.12 = (bf16[384,512]{1,0:T(8,128)(2,1)}, bf16[384,512]{1,0:T(8,128)(2,1)S(1)}, u32[]{:S(2)}, u32[]{:S(2)}) collective-permute-start(bf16[384,512]{1,0:T(8,128)(2,1)} %shard_map.47), channel_id=1, source_target_pairs={{0,1},{1,0},{2,3},{3,2},{4,5},{5,4},{6,7},{7,6},{8,9},{9,8},{10,11... | collective-permute-start | bytes 1179656 | tf_op jit(solution)/shard_map/ppermute | solution.py:23

commit v8 on v7

--- a/solution.py
+++ b/solution.py
@@ -29,9 +29,12 @@
     return jnp.concatenate([lead, tail], axis=axis)
 
 
-def attention_kernel(seg_ref, q_ref, k2_ref, k1_ref, k0_ref, v2_ref, v1_ref, v0_ref, o_ref):
+def attention_kernel(
+    seg_ref, q_ref, k2e_ref, k2o_ref, k1_ref, k0_ref, v2e_ref, v2o_ref, v1_ref, v0_ref, o_ref
+):
     seg = seg_ref[0]
     first_row = seg_ref[1]
+    even = seg_ref[2]
     count = q_ref.shape[0]
     seg_rows = k0_ref.shape[0]
     dims = (((1,), (1,)), ((), ()))
@@ -48,7 +51,8 @@
         own_row = lax.broadcasted_iota(jnp.int32, (count, own_rows), 0) + first_row
         causal = own_col <= own_row
         s0 = jnp.where(causal, scores_of(k0_ref[:own_rows, lanes]), low)
-        s2 = scores_of(k2_ref[:, lanes])
+        pick = lax.broadcasted_iota(jnp.int32, (seg_rows, HD), 0) < even * seg_rows
+        s2 = scores_of(jnp.where(pick, k2e_ref[:, lanes], k2o_ref[:, lanes]))
         s1 = scores_of(k1_ref[:, lanes])
         if masked:
             col = lax.broadcasted_iota(jnp.int32, (count, seg_rows), 1)
@@ -71,7 +75,8 @@
             + jnp.sum(e1, axis=1, keepdims=True)
             + jnp.sum(e0, axis=1, keepdims=True)
         )
-        mixed = jnp.dot(e2.astype(jnp.bfloat16), v2_ref[:, lanes], preferred_element_type=jnp.float32)
+        value2 = jnp.where(pick, v2e_ref[:, lanes], v2o_ref[:, lanes])
+        mixed = jnp.dot(e2.astype(jnp.bfloat16), value2, preferred_element_type=jnp.float32)
         mixed = mixed + jnp.dot(e1.astype(jnp.bfloat16), v1_ref[:, lanes], preferred_element_type=jnp.float32)
         mixed = mixed + jnp.dot(
             e0.astype(jnp.bfloat16), v0_ref[:own_rows, lanes], preferred_element_type=jnp.float32
@@ -100,14 +105,18 @@
     width = step * HD
     q_spec = pl.BlockSpec((count, width), lambda h, scalars: (0, h + head_lo // step))
     kv_spec = pl.BlockSpec((seg_rows, width), lambda h, scalars: (0, h + head_lo // step))
+    even_spec = pl.BlockSpec((seg_rows, width), lambda h, scalars: (0, (h + head_lo // step) * scalars[2]))
+    odd_spec = pl.BlockSpec((seg_rows, width), lambda h, scalars: (0, (h + head_lo // step) * (1 - scalars[2])))
     o_spec = pl.BlockSpec((count, width), lambda h, scalars: (0, h))
+    mem_specs = [even_spec, odd_spec, kv_spec, kv_spec]
     grid_spec = pltpu.PrefetchScalarGridSpec(
         num_scalar_prefetch=1,
         grid=(head_count // step,),
-        in_specs=[q_spec] + [kv_spec] * 6,
+        in_specs=[q_spec] + mem_specs + mem_specs,
         out_specs=o_spec,
     )
-    scalars = jnp.stack([seg_number, first_row]).astype(jnp.int32)
+    even = (seg_number % 2 == 0).astype(jnp.int32)
+    scalars = jnp.stack([seg_number, first_row, even]).astype(jnp.int32)
     return pl.pallas_call(
         attention_kernel,
         grid_spec=grid_spec,
@@ -122,7 +131,7 @@
     halves = lax.axis_size("fsdp")
     segs = lax.axis_size("seg")
     cols = width // halves
-    piece = cols // 2
+    piece = cols // 8
     half_number = lax.axis_index("fsdp")
     seg_number = lax.axis_index("seg")
     other_half = 1 - half_number
@@ -170,12 +179,12 @@
         one = from_behind(own, "seg", 1)
         even_two = lax.ppermute(own, "seg", even_pairs)
         odd_two = lax.ppermute(one, "seg", forward_pairs)
-        return jnp.where(is_key_core, even_two, odd_two), one
+        return (even_two, odd_two), one
 
     key_two, key_one = shifted(own_key)
     value_two, value_one = shifted(own_value)
-    keys = (key_two, key_one, own_key)
-    values = (value_two, value_one, own_value)
+    keys = (*key_two, key_one, own_key)
+    values = (*value_two, value_one, own_value)
 
     heads = cols // HD
     lead = heads - heads // 4

time: 213 us -> 203 us (0.953)
  waiting for transfers between devices: 110 us -> 98.8 us
  other arithmetic: 18.2 us -> 12.9 us
  starting transfers between devices: 24.3 us -> 28.6 us
    ppermute x5, waiting for transfers between devices: 51.8 us -> 11.3 us  [swap_halves(): return lax.ppermute(value, 'fsdp', [(0, 1), (1, 0)])]
    ppermute x1, waiting for transfers between devices: 1.13 us -> 30.8 us  [body(): right_got = lax.ppermute(served[:, piece:], ('seg', 'fsdp'), wrap_pairs)]
    select_n x2 -> x0, other arithmetic: 5.46 us -> none  [shifted(): return (jnp.where(is_key_core, even_two, odd_two), one)]
  transfers between devices with their start and end apart: 13 -> 13, of which waited for: 6 -> 5; matrix products, arithmetic and copies ran while one was open for 6% -> 3% of each run, Pallas kernels for 17% -> 18%
where the time goes in v8:
time: 203 us
  waiting for transfers between devices  98.8 us (49%)
  Pallas kernels  51 us (25%)
  starting transfers between devices  28.6 us (14%)
  other arithmetic  12.9 us (6%)
  matrix products  6.85 us (3%)
  local copies, waits for them, and re-layouts  4.4 us (2%)
    ppermute x2, waiting for transfers between devices, from_behind(): lax.ppermute(value, axis, [(source, source + steps) for source in range(l...  56.7 us
    pallas_call x4, Pallas kernels, attend(): pl.pallas_call(attention_kernel, grid_spec=grid_spec, out_shape=jax.Shape...  51 us
    ppermute x1, waiting for transfers between devices, body(): right_got = lax.ppermute(served[:, piece:], ('seg', 'fsdp'), wrap_pairs)  30.8 us
    ppermute x5, waiting for transfers between devices, swap_halves(): return lax.ppermute(value, 'fsdp', [(0, 1), (1, 0)])  11.3 us
    ppermute x2, starting transfers between devices, shifted(): even_two = lax.ppermute(own, 'seg', even_pairs)  7.65 us
    select_n x3, other arithmetic, in_order(): lead = jnp.where(first_is_mine, mine, other)  7.2 us
    ppermute x5, starting transfers between devices, swap_halves(): return lax.ppermute(value, 'fsdp', [(0, 1), (1, 0)])  7.15 us
    ppermute x2, starting transfers between devices, from_behind(): lax.ppermute(value, axis, [(source, source + steps) for source in range(l...  5.85 us
  transfers between devices with their start and end apart: 13, of which 5 were waited for; matrix products, arithmetic and copies ran while one was open for 3% of the time, Pallas kernels for 18%

profile of v8, /device:TPU:24, one launch (start us, length us, event | category | flops | bytes accessed | tf_op | source)
XLA Modules:
  0.0 202.7 jit_solution(13822286668189207744)
XLA Ops:
  0.0 3.2 %dynamic-slice_select_fusion = bf16[1024,1024]{1,0:T(8,128)(2,1)S(1)} fusion(bf16[1024,2048]{1,0:T(8,128)(2,1)} %param.7, s32[]{:T(128)S(6)} %select_n.84, bf16[1024,2048]{1,0:T(8,128)(2,1)} %param.6, pred[]{:T(512)S(6)} %eq.17), kind=kLoop, calls=%fused_computation.9 | loop fusion | flops 1048576 | bytes 6291461 | tf_op jit(solution)/shard_map/jit(_where)/select_n | solution.py:148
  3.2 0.2 slice.9
  3.4 2.8 %collective-permute-start.2 = (bf16[1024,896]{1,0:T(8,128)(2,1)S(1)}, bf16[1024,896]{1,0:T(8,128)(2,1)S(1)}, u32[]{:S(2)}, u32[]{:S(2)}) collective-permute-start(bf16[1024,896]{1,0:T(8,128)(2,1)S(1)} %slice.9), channel_id=1, source_target_pairs={{33,0},{32,1},{35,2},{34,3},{37,4},{36,5},{39,6},{38,7},{41,8},{40... | collective-permute-start | bytes 5505032 | tf_op jit(solution)/shard_map/ppermute | solution.py:155
  6.2 0.1 slice.8
  6.3 0.3 collective-permute-start.1
  6.6 1.8 collective-permute-start
  8.4 7.1 %collective-permute-done.1 = bf16[1024,128]{1,0:T(8,128)(2,1)S(1)} collective-permute-done((bf16[1024,128]{1,0:T(8,128)(2,1)S(1)}, bf16[1024,128]{1,0:T(8,128)(2,1)S(1)}, u32[]{:S(2)}, u32[]{:S(2)}) %collective-permute-start.1) | collective-permute-done | bytes 262176 | tf_op jit(solution)/shard_map/ppermute | solution.py:23
  15.5 0.1 constant_dynamic-update-slice_fusion.1
  15.6 30.8 %collective-permute-done.2 = bf16[1024,896]{1,0:T(8,128)(2,1)S(1)} collective-permute-done((bf16[1024,896]{1,0:T(8,128)(2,1)S(1)}, bf16[1024,896]{1,0:T(8,128)(2,1)S(1)}, u32[]{:S(2)}, u32[]{:S(2)}) %collective-permute-start.2) | collective-permute-done | bytes 1835040 | tf_op jit(solution)/shard_map/ppermute | solution.py:155
  46.4 0.3 constant_dynamic-update-slice_fusion
  46.7 0.1 collective-permute-start.3
  46.8 0.0 copy-start.3
  46.9 2.8 %constant_dynamic-slice_fusion = (bf16[384,1024]{1,0:T(8,128)(2,1)}, bf16[384,1024]{1,0:T(8,128)(2,1)}) fusion(bf16[384,2048]{1,0:T(8,128)(2,1)} %param.5, s32[]{:T(128)S(6)} %select_n.89, s32[]{:T(128)S(6)} %select_n.84), kind=kLoop, calls=%fused_computation.28 | loop fusion | bytes 3145736 | tf_op jit(solution)/shard_map/dynamic_slice | solution.py:143
  49.7 0.0 copy-start.2
  49.7 0.0 collective-permute-done
  49.7 2.2 %broadcast_select_fusion.7 = (bf16[384,2048]{1,0:T(8,128)(2,1)S(1)}, bf16[384,2048]{1,0:T(8,128)(2,1)S(1)}) fusion(bf16[384,2048]{1,0:T(8,128)(2,1)} %param.4, bf16[384,2048]{1,0:T(8,128)(2,1)} %collective-permute-done, pred[]{:T(512)S(6)} %eq.16), kind=kLoop, calls=%fused_computation.20 | loop fusion | flops 1572864 | bytes 6291457 | tf_op jit(solution)/shard_map/jit(_where)/select_n | solution.py:27
  51.9 0.0 collective-permute-done.3
  51.9 0.0 copy-done.3
  51.9 0.9 copy-done.2
  52.8 3.7 %broadcast_select_fusion.3 = (bf16[1024,1024]{1,0:T(8,128)(2,1)S(1)}, bf16[1024,1024]{1,0:T(8,128)(2,1)S(1)}, bf16[1024,1024]{1,0:T(8,128)(2,1)S(1)}, bf16[1024,1024]{1,0:T(8,128)(2,1)S(1)}) fusion(pred[]{:T(512)S(6)} %eq.16, bf16[1024,2048]{1,0:T(8,128)(2,1)S(1)} %copy-done.2, s32[]{:T(128)S(6)} %select_n.89, bf16[1024,1024]{1,0:T(8,128)(2,1)} %collective-permute-done.3, ...), kind=kLoop, calls=%fused_computation.13 | loop fusion | flops 6291456 | bytes 16777222 | tf_op jit(solution)/shard_map/jit(_where)/select_n | solution.py:27
  56.5 3.4 %fusion.8.v0_ref = bf16[768,1024]{1,0:T(8,128)(2,1)S(1)} fusion(bf16[1024,1024]{1,0:T(8,128)(2,1)S(1)} %get-tuple-element.18, bf16[1024,1024]{1,0:T(8,128)(2,1)S(1)} %get-tuple-element.17, bf16[384,2048]{1,0:T(8,128)(2,1)S(1)} %get-tuple-element.24, bf16[384,2048]{1,0:T(8,128)(2,1)S(1)} %get-tuple-element.23), kind=kOutput, calls=%fused_computation.16 | convolution fusion | flops 3236691968 | bytes 8912896 | tf_op jit(solution)/shard_map/dot_general | solution.py:169
  59.9 0.0 copy-start
  59.9 3.4 %fusion.11.k0_ref = bf16[768,1024]{1,0:T(8,128)(2,1)S(1)} fusion(bf16[1024,1024]{1,0:T(8,128)(2,1)S(1)} %get-tuple-element.21, bf16[1024,1024]{1,0:T(8,128)(2,1)S(1)} %get-tuple-element.22, bf16[384,2048]{1,0:T(8,128)(2,1)S(1)} %get-tuple-element.24, bf16[384,2048]{1,0:T(8,128)(2,1)S(1)} %get-tuple-element.23), kind=kOutput, calls=%fused_computation.17 | convolution fusion | flops 3236691968 | bytes 8912896 | tf_op jit(solution)/shard_map/dot_general | solution.py:168
  63.4 0.0 copy-start.1
  63.4 2.4 %collective-permute-start.9 = (bf16[768,1024]{1,0:T(8,128)(2,1)S(1)}, bf16[768,1024]{1,0:T(8,128)(2,1)}, u32[]{:S(2)}, u32[]{:S(2)}) collective-permute-start(bf16[768,1024]{1,0:T(8,128)(2,1)S(1)} %fusion.8.v0_ref), channel_id=1, source_target_pairs={{0,2},{2,4},{4,6},{6,8},{8,10},{10,12},{12,14},{14,16},{16,18},{18... | collective-permute-start | bytes 4718600 | tf_op jit(solution)/shard_map/ppermute | solution.py:19
  65.8 3.5 %collective-permute-start.6 = (bf16[768,1024]{1,0:T(8,128)(2,1)S(1)}, bf16[768,1024]{1,0:T(8,128)(2,1)}, u32[]{:S(2)}, u32[]{:S(2)}) collective-permute-start(bf16[768,1024]{1,0:T(8,128)(2,1)S(1)} %fusion.11.k0_ref), channel_id=1, source_target_pairs={{0,2},{2,4},{4,6},{6,8},{8,10},{10,12},{12,14},{14,16},{16,18},{18... | collective-permute-start | bytes 4718600 | tf_op jit(solution)/shard_map/ppermute | solution.py:19
  69.2 3.8 %collective-permute-start.5 = (bf16[768,1024]{1,0:T(8,128)(2,1)S(1)}, bf16[768,1024]{1,0:T(8,128)(2,1)}, u32[]{:S(2)}, u32[]{:S(2)}) collective-permute-start(bf16[768,1024]{1,0:T(8,128)(2,1)S(1)} %fusion.11.k0_ref), channel_id=1, source_target_pairs={{0,4},{4,8},{8,12},{12,16},{16,20},{20,24},{24,28},{28,32},{32,36}... | collective-permute-start | bytes 4718600 | tf_op jit(solution)/shard_map/ppermute | solution.py:180
  73.1 0.0 copy-done
  73.1 3.8 %collective-permute-start.8 = (bf16[768,1024]{1,0:T(8,128)(2,1)S(1)}, bf16[768,1024]{1,0:T(8,128)(2,1)}, u32[]{:S(2)}, u32[]{:S(2)}) collective-permute-start(bf16[768,1024]{1,0:T(8,128)(2,1)S(1)} %fusion.8.v0_ref), channel_id=1, source_target_pairs={{0,4},{4,8},{8,12},{12,16},{16,20},{20,24},{24,28},{28,32},{32,36}... | collective-permute-start | bytes 4718600 | tf_op jit(solution)/shard_map/ppermute | solution.py:180
  76.9 25.5 %collective-permute-done.9.v1_ref = bf16[768,1024]{1,0:T(8,128)(2,1)} collective-permute-done((bf16[768,1024]{1,0:T(8,128)(2,1)S(1)}, bf16[768,1024]{1,0:T(8,128)(2,1)}, u32[]{:S(2)}, u32[]{:S(2)}) %collective-permute-start.9) | collective-permute-done | bytes 1572896 | tf_op jit(solution)/shard_map/ppermute | solution.py:19
  102.4 2.5 %collective-permute-start.10 = (bf16[768,1024]{1,0:T(8,128)(2,1)}, bf16[768,1024]{1,0:T(8,128)(2,1)}, u32[]{:S(2)}, u32[]{:S(2)}) collective-permute-start(bf16[768,1024]{1,0:T(8,128)(2,1)} %collective-permute-done.9.v1_ref), channel_id=1, source_target_pairs={{0,2},{4,6},{8,10},{12,14},{16,18},{20,22},{24,26},{28,30},{32,34}... | collective-permute-start | bytes 4718600 | tf_op jit(solution)/shard_map/ppermute | solution.py:181
  104.9 31.2 %collective-permute-done.6.k1_ref = bf16[768,1024]{1,0:T(8,128)(2,1)} collective-permute-done((bf16[768,1024]{1,0:T(8,128)(2,1)S(1)}, bf16[768,1024]{1,0:T(8,128)(2,1)}, u32[]{:S(2)}, u32[]{:S(2)}) %collective-permute-start.6) | collective-permute-done | bytes 1572896 | tf_op jit(solution)/shard_map/ppermute | solution.py:19
  136.1 2.4 %collective-permute-start.7 = (bf16[768,1024]{1,0:T(8,128)(2,1)}, bf16[768,1024]{1,0:T(8,128)(2,1)}, u32[]{:S(2)}, u32[]{:S(2)}) collective-permute-start(bf16[768,1024]{1,0:T(8,128)(2,1)} %collective-permute-done.6.k1_ref), channel_id=1, source_target_pairs={{0,2},{4,6},{8,10},{12,14},{16,18},{20,22},{24,26},{28,30},{32,34}... | collective-permute-start | bytes 4718600 | tf_op jit(solution)/shard_map/ppermute | solution.py:181
  138.6 2.6 %collective-permute-start.4 = (bf16[384,1024]{1,0:T(8,128)(2,1)}, bf16[384,1024]{1,0:T(8,128)(2,1)}, u32[]{:S(2)}, u32[]{:S(2)}) collective-permute-start(bf16[384,1024]{1,0:T(8,128)(2,1)} %get-tuple-element.11), channel_id=1, source_target_pairs={{0,1},{1,0},{2,3},{3,2},{4,5},{5,4},{6,7},{7,6},{8,9},{9,8},{10,11... | collective-permute-start | bytes 2359304 | tf_op jit(solution)/shard_map/ppermute | solution.py:23
  141.2 0.7 add_add_fusion.seg_ref
  141.9 0.7 add_add_fusion.1.seg_ref
  142.5 0.0 collective-permute-done.5.k2e_ref
  142.5 0.0 collective-permute-done.8.v2e_ref
  142.5 0.0 collective-permute-done.10.v2o_ref
  142.6 0.0 collective-permute-done.7.k2o_ref
  142.6 0.0 copy-done.1
  142.6 15.4 %shard_map.46 = bf16[384,768]{1,0:T(8,128)(2,1)} custom-call(s32[3]{0:T(128)} %add_add_fusion.seg_ref, bf16[384,1024]{1,0:T(8,128)(2,1)} %get-tuple-element.16.q_ref, bf16[768,1024]{1,0:T(8,128)(2,1)} %collective-permute-done.5.k2e_ref, bf16[768,1024]{1,0:T(8,128)(2,1)} %collective-permute-done.7.k2o_ref, bf16[768,1024]{1,0:T(8,128)(2,1)} %collective-permute-done.6.k1_ref, ...), custom_call_target="tpu_custom_call" | custom-call | tf_op jit(solution)/shard_map/pallas_call | solution.py:120
  158.0 0.0 collective-permute-done.4.q_ref
  158.0 14.2 %shard_map.49 = bf16[384,512]{1,0:T(8,128)(2,1)} custom-call(s32[3]{0:T(128)} %add_add_fusion.1.seg_ref, bf16[384,1024]{1,0:T(8,128)(2,1)} %collective-permute-done.4.q_ref, bf16[768,1024]{1,0:T(8,128)(2,1)} %collective-permute-done.5.k2e_ref, bf16[768,1024]{1,0:T(8,128)(2,1)} %collective-permute-done.7.k2o_ref, ...), custom_call_target="tpu_custom_call" | custom-call | tf_op jit(solution)/shard_map/pallas_call | solution.py:120
  172.2 2.3 %collective-permute-start.11 = (bf16[384,512]{1,0:T(8,128)(2,1)}, bf16[384,512]{1,0:T(8,128)(2,1)S(1)}, u32[]{:S(2)}, u32[]{:S(2)}) collective-permute-start(bf16[384,512]{1,0:T(8,128)(2,1)} %shard_map.49), channel_id=1, source_target_pairs={{0,1},{1,0},{2,3},{3,2},{4,5},{5,4},{6,7},{7,6},{8,9},{9,8},{10,11... | collective-permute-start | bytes 1179656 | tf_op jit(solution)/shard_map/ppermute | solution.py:23
  174.5 14.2 %shard_map.47 = bf16[384,512]{1,0:T(8,128)(2,1)} custom-call(s32[3]{0:T(128)} %add_add_fusion.1.seg_ref, bf16[384,1024]{1,0:T(8,128)(2,1)} %collective-permute-done.4.q_ref, bf16[768,1024]{1,0:T(8,128)(2,1)} %collective-permute-done.5.k2e_ref, bf16[768,1024]{1,0:T(8,128)(2,1)} %collective-permute-done.7.k2o_ref, ...), custom_call_target="tpu_custom_call" | custom-call | tf_op jit(solution)/shard_map/pallas_call | solution.py:120
  188.7 0.0 copy-start.4
  188.7 0.1 collective-permute-start.12
  188.8 7.1 %shard_map.48 = bf16[384,256]{1,0:T(8,128)(2,1)} custom-call(s32[3]{0:T(128)} %add_add_fusion.seg_ref, bf16[384,1024]{1,0:T(8,128)(2,1)} %get-tuple-element.16.q_ref, bf16[768,1024]{1,0:T(8,128)(2,1)} %collective-permute-done.5.k2e_ref, bf16[768,1024]{1,0:T(8,128)(2,1)} %collective-permute-done.7.k2o_ref, bf16[768,1024]{1,0:T(8,128)(2,1)} %collective-permute-done.6.k1_ref, ...), custom_call_target="tpu_custom_call" | custom-call | tf_op jit(solution)/shard_map/pallas_call | solution.py:120
  196.0 0.0 collective-permute-done.11
  196.0 4.1 %collective-permute-done.12 = bf16[384,512]{1,0:T(8,128)(2,1)S(1)} collective-permute-done((bf16[384,512]{1,0:T(8,128)(2,1)}, bf16[384,512]{1,0:T(8,128)(2,1)S(1)}, u32[]{:S(2)}, u32[]{:S(2)}) %collective-permute-start.12) | collective-permute-done | bytes 393248 | tf_op jit(solution)/shard_map/ppermute | solution.py:23
  200.2 0.0 copy-done.4
  200.2 1.3 broadcast_select_fusion.9
  201.5 1.2 pad_maximum_fusion.7
  (2 shorter events, 0.1 us)
Async XLA Ops:
  3.4 43.0 %collective-permute-start.2 = (bf16[1024,896]{1,0:T(8,128)(2,1)S(1)}, bf16[1024,896]{1,0:T(8,128)(2,1)S(1)}, u32[]{:S(2)}, u32[]{:S(2)}) collective-permute-start(bf16[1024,896]{1,0:T(8,128)(2,1)S(1)} %slice.9), channel_id=1, source_target_pairs={{33,0},{32,1},{35,2},{34,3},{37,4},{36,5},{39,6},{38,7},{41,8},{40... | collective-permute-start | bytes 5505032 | tf_op jit(solution)/shard_map/ppermute | solution.py:155
  6.3 9.3 %collective-permute-start.1 = (bf16[1024,128]{1,0:T(8,128)(2,1)S(1)}, bf16[1024,128]{1,0:T(8,128)(2,1)S(1)}, u32[]{:S(2)}, u32[]{:S(2)}) collective-permute-start(bf16[1024,128]{1,0:T(8,128)(2,1)S(1)} %slice.8), channel_id=1, source_target_pairs={{0,1},{1,0},{2,3},{3,2},{4,5},{5,4},{6,7},{7,6},{8,9},{9,8},{10,11... | collective-permute-start | bytes 786440 | tf_op jit(solution)/shard_map/ppermute | solution.py:23
  6.6 43.1 %collective-permute-start = (bf16[384,2048]{1,0:T(8,128)(2,1)}, bf16[384,2048]{1,0:T(8,128)(2,1)}, u32[]{:S(2)}, u32[]{:S(2)}) collective-permute-start(bf16[384,2048]{1,0:T(8,128)(2,1)} %param.4), channel_id=1, source_target_pairs={{0,1},{1,0},{2,3},{3,2},{4,5},{5,4},{6,7},{7,6},{8,9},{9,8},{10,11... | collective-permute-start | bytes 4718600 | tf_op jit(solution)/shard_map/ppermute | solution.py:23
  46.7 5.2 %collective-permute-start.3 = (bf16[1024,1024]{1,0:T(8,128)(2,1)S(1)}, bf16[1024,1024]{1,0:T(8,128)(2,1)}, u32[]{:S(2)}, u32[]{:S(2)}) collective-permute-start(bf16[1024,1024]{1,0:T(8,128)(2,1)S(1)} %constant_dynamic-update-slice_fusion), channel_id=1, source_target_pairs={{0,2},{2,0},{4,6},{6,4},{8,10},{10,8},{12,14},{14,12},{16,18},{18,... | collective-permute-start | bytes 6291464 | tf_op jit(solution)/shard_map/ppermute | solution.py:158
  46.8 5.1 %copy-start.3 = (bf16[1024,2048]{1,0:T(8,128)(2,1)S(1)}, bf16[1024,2048]{1,0:T(8,128)(2,1)}, u32[]{:S(2)}) copy-start(bf16[1024,2048]{1,0:T(8,128)(2,1)} %param.6) | copy-start | bytes 12582916
  49.7 3.1 %copy-start.2 = (bf16[1024,2048]{1,0:T(8,128)(2,1)S(1)}, bf16[1024,2048]{1,0:T(8,128)(2,1)}, u32[]{:S(2)}) copy-start(bf16[1024,2048]{1,0:T(8,128)(2,1)} %param.7) | copy-start | bytes 12582916
  59.9 13.2 %copy-start = (bf16[768,1024]{1,0:T(8,128)(2,1)}, bf16[768,1024]{1,0:T(8,128)(2,1)S(1)}, u32[]{:S(2)}) copy-start(bf16[768,1024]{1,0:T(8,128)(2,1)S(1)} %fusion.8.v0_ref) | copy-start | bytes 4718596
  63.4 79.2 %copy-start.1 = (bf16[768,1024]{1,0:T(8,128)(2,1)}, bf16[768,1024]{1,0:T(8,128)(2,1)S(1)}, u32[]{:S(2)}) copy-start(bf16[768,1024]{1,0:T(8,128)(2,1)S(1)} %fusion.11.k0_ref) | copy-start | bytes 4718596
  63.4 39.0 %collective-permute-start.9 = (bf16[768,1024]{1,0:T(8,128)(2,1)S(1)}, bf16[768,1024]{1,0:T(8,128)(2,1)}, u32[]{:S(2)}, u32[]{:S(2)}) collective-permute-start(bf16[768,1024]{1,0:T(8,128)(2,1)S(1)} %fusion.8.v0_ref), channel_id=1, source_target_pairs={{0,2},{2,4},{4,6},{6,8},{8,10},{10,12},{12,14},{14,16},{16,18},{18... | collective-permute-start | bytes 4718600 | tf_op jit(solution)/shard_map/ppermute | solution.py:19
  65.8 70.4 %collective-permute-start.6 = (bf16[768,1024]{1,0:T(8,128)(2,1)S(1)}, bf16[768,1024]{1,0:T(8,128)(2,1)}, u32[]{:S(2)}, u32[]{:S(2)}) collective-permute-start(bf16[768,1024]{1,0:T(8,128)(2,1)S(1)} %fusion.11.k0_ref), channel_id=1, source_target_pairs={{0,2},{2,4},{4,6},{6,8},{8,10},{10,12},{12,14},{14,16},{16,18},{18... | collective-permute-start | bytes 4718600 | tf_op jit(solution)/shard_map/ppermute | solution.py:19
  69.2 73.3 %collective-permute-start.5 = (bf16[768,1024]{1,0:T(8,128)(2,1)S(1)}, bf16[768,1024]{1,0:T(8,128)(2,1)}, u32[]{:S(2)}, u32[]{:S(2)}) collective-permute-start(bf16[768,1024]{1,0:T(8,128)(2,1)S(1)} %fusion.11.k0_ref), channel_id=1, source_target_pairs={{0,4},{4,8},{8,12},{12,16},{16,20},{20,24},{24,28},{28,32},{32,36}... | collective-permute-start | bytes 4718600 | tf_op jit(solution)/shard_map/ppermute | solution.py:180
  73.1 69.5 %collective-permute-start.8 = (bf16[768,1024]{1,0:T(8,128)(2,1)S(1)}, bf16[768,1024]{1,0:T(8,128)(2,1)}, u32[]{:S(2)}, u32[]{:S(2)}) collective-permute-start(bf16[768,1024]{1,0:T(8,128)(2,1)S(1)} %fusion.8.v0_ref), channel_id=1, source_target_pairs={{0,4},{4,8},{8,12},{12,16},{16,20},{20,24},{24,28},{28,32},{32,36}... | collective-permute-start | bytes 4718600 | tf_op jit(solution)/shard_map/ppermute | solution.py:180
  102.4 40.2 %collective-permute-start.10 = (bf16[768,1024]{1,0:T(8,128)(2,1)}, bf16[768,1024]{1,0:T(8,128)(2,1)}, u32[]{:S(2)}, u32[]{:S(2)}) collective-permute-start(bf16[768,1024]{1,0:T(8,128)(2,1)} %collective-permute-done.9.v1_ref), channel_id=1, source_target_pairs={{0,2},{4,6},{8,10},{12,14},{16,18},{20,22},{24,26},{28,30},{32,34}... | collective-permute-start | bytes 4718600 | tf_op jit(solution)/shard_map/ppermute | solution.py:181
  136.1 6.4 %collective-permute-start.7 = (bf16[768,1024]{1,0:T(8,128)(2,1)}, bf16[768,1024]{1,0:T(8,128)(2,1)}, u32[]{:S(2)}, u32[]{:S(2)}) collective-permute-start(bf16[768,1024]{1,0:T(8,128)(2,1)} %collective-permute-done.6.k1_ref), channel_id=1, source_target_pairs={{0,2},{4,6},{8,10},{12,14},{16,18},{20,22},{24,26},{28,30},{32,34}... | collective-permute-start | bytes 4718600 | tf_op jit(solution)/shard_map/ppermute | solution.py:181
  138.6 19.4 %collective-permute-start.4 = (bf16[384,1024]{1,0:T(8,128)(2,1)}, bf16[384,1024]{1,0:T(8,128)(2,1)}, u32[]{:S(2)}, u32[]{:S(2)}) collective-permute-start(bf16[384,1024]{1,0:T(8,128)(2,1)} %get-tuple-element.11), channel_id=1, source_target_pairs={{0,1},{1,0},{2,3},{3,2},{4,5},{5,4},{6,7},{7,6},{8,9},{9,8},{10,11... | collective-permute-start | bytes 2359304 | tf_op jit(solution)/shard_map/ppermute | solution.py:23
  172.2 23.8 %collective-permute-start.11 = (bf16[384,512]{1,0:T(8,128)(2,1)}, bf16[384,512]{1,0:T(8,128)(2,1)S(1)}, u32[]{:S(2)}, u32[]{:S(2)}) collective-permute-start(bf16[384,512]{1,0:T(8,128)(2,1)} %shard_map.49), channel_id=1, source_target_pairs={{0,1},{1,0},{2,3},{3,2},{4,5},{5,4},{6,7},{7,6},{8,9},{9,8},{10,11... | collective-permute-start | bytes 1179656 | tf_op jit(solution)/shard_map/ppermute | solution.py:23
  188.7 11.5 %copy-start.4 = (bf16[384,768]{1,0:T(8,128)(2,1)S(1)}, bf16[384,768]{1,0:T(8,128)(2,1)}, u32[]{:S(2)}) copy-start(bf16[384,768]{1,0:T(8,128)(2,1)} %shard_map.46) | copy-start | bytes 1769476
  188.7 11.4 %collective-permute-start.12 = (bf16[384,512]{1,0:T(8,128)(2,1)}, bf16[384,512]{1,0:T(8,128)(2,1)S(1)}, u32[]{:S(2)}, u32[]{:S(2)}) collective-permute-start(bf16[384,512]{1,0:T(8,128)(2,1)} %shard_map.47), channel_id=1, source_target_pairs={{0,1},{1,0},{2,3},{3,2},{4,5},{5,4},{6,7},{7,6},{8,9},{9,8},{10,11... | collective-permute-start | bytes 1179656 | tf_op jit(solution)/shard_map/ppermute | solution.py:23

commit v9 on v8

--- a/solution.py
+++ b/solution.py
@@ -47,10 +47,12 @@
             raw = lax.dot_general(query, key, dims, preferred_element_type=jnp.float32)
             return raw * HD ** (-0.5)
 
-        own_col = lax.broadcasted_iota(jnp.int32, (count, own_rows), 1)
-        own_row = lax.broadcasted_iota(jnp.int32, (count, own_rows), 0) + first_row
+        open_rows = own_rows - count
+        own_col = lax.broadcasted_iota(jnp.int32, (count, count), 1) + open_rows
+        own_row = lax.broadcasted_iota(jnp.int32, (count, count), 0) + first_row
         causal = own_col <= own_row
-        s0 = jnp.where(causal, scores_of(k0_ref[:own_rows, lanes]), low)
+        s0 = jnp.where(causal, scores_of(k0_ref[open_rows:own_rows, lanes]), low)
+        s_open = scores_of(k0_ref[:open_rows, lanes]) if open_rows else None
         pick = lax.broadcasted_iota(jnp.int32, (seg_rows, HD), 0) < even * seg_rows
         s2 = scores_of(jnp.where(pick, k2e_ref[:, lanes], k2o_ref[:, lanes]))
         s1 = scores_of(k1_ref[:, lanes])
@@ -64,6 +66,8 @@
             jnp.maximum(jnp.max(s2, axis=1, keepdims=True), jnp.max(s1, axis=1, keepdims=True)),
             jnp.max(s0, axis=1, keepdims=True),
         )
+        if open_rows:
+            top = jnp.maximum(top, jnp.max(s_open, axis=1, keepdims=True))
         e2 = jnp.exp(s2 - top)
         e1 = jnp.exp(s1 - top)
         if masked:
@@ -75,12 +79,19 @@
             + jnp.sum(e1, axis=1, keepdims=True)
             + jnp.sum(e0, axis=1, keepdims=True)
         )
+        if open_rows:
+            e_open = jnp.exp(s_open - top)
+            total = total + jnp.sum(e_open, axis=1, keepdims=True)
         value2 = jnp.where(pick, v2e_ref[:, lanes], v2o_ref[:, lanes])
         mixed = jnp.dot(e2.astype(jnp.bfloat16), value2, preferred_element_type=jnp.float32)
         mixed = mixed + jnp.dot(e1.astype(jnp.bfloat16), v1_ref[:, lanes], preferred_element_type=jnp.float32)
         mixed = mixed + jnp.dot(
-            e0.astype(jnp.bfloat16), v0_ref[:own_rows, lanes], preferred_element_type=jnp.float32
+            e0.astype(jnp.bfloat16), v0_ref[open_rows:own_rows, lanes], preferred_element_type=jnp.float32
         )
+        if open_rows:
+            mixed = mixed + jnp.dot(
+                e_open.astype(jnp.bfloat16), v0_ref[:open_rows, lanes], preferred_element_type=jnp.float32
+            )
         o_ref[:, lanes] = (mixed / total).astype(o_ref.dtype)
 
     def run(masked, own_rows):

time: 203 us -> 197 us (0.970)
  Pallas kernels: 51 us -> 45.6 us
    pallas_call x4, Pallas kernels: 51 us -> 45.6 us  [attend(): pl.pallas_call(attention_kernel, grid_spec=grid_spec, out_shape=jax.Shape...]
  transfers between devices with their start and end apart: 13 -> 13, of which waited for: 5 -> 5; matrix products, arithmetic and copies ran while one was open for 3% -> 3% of each run, Pallas kernels for 18% -> 17%
where the time goes in v9:
time: 197 us; the launch traced here: 196 us
  waiting for transfers between devices  98.3 us (50%)
  Pallas kernels  45.6 us (23%)
  starting transfers between devices  27.9 us (14%)
  other arithmetic  12.9 us (7%)
  matrix products  6.85 us (3%)
  local copies, waits for them, and re-layouts  4.4 us (2%)
    ppermute x2, waiting for transfers between devices, from_behind(): lax.ppermute(value, axis, [(source, source + steps) for source in range(l...  56.7 us
    pallas_call x4, Pallas kernels, attend(): pl.pallas_call(attention_kernel, grid_spec=grid_spec, out_shape=jax.Shape...  45.6 us
    ppermute x1, waiting for transfers between devices, body(): right_got = lax.ppermute(served[:, piece:], ('seg', 'fsdp'), wrap_pairs)  30.8 us
    ppermute x5, waiting for transfers between devices, swap_halves(): return lax.ppermute(value, 'fsdp', [(0, 1), (1, 0)])  10.8 us
    ppermute x2, starting transfers between devices, shifted(): even_two = lax.ppermute(own, 'seg', even_pairs)  7.65 us
    select_n x3, other arithmetic, in_order(): lead = jnp.where(first_is_mine, mine, other)  7.2 us
    ppermute x5, starting transfers between devices, swap_halves(): return lax.ppermute(value, 'fsdp', [(0, 1), (1, 0)])  6.5 us
    ppermute x2, starting transfers between devices, from_behind(): lax.ppermute(value, axis, [(source, source + steps) for source in range(l...  5.85 us
  transfers between devices with their start and end apart: 13, of which 5 were waited for; matrix products, arithmetic and copies ran while one was open for 3% of the time, Pallas kernels for 17%

profile of v9, /device:TPU:24, one launch (start us, length us, event | category | flops | bytes accessed | tf_op | source)
XLA Modules:
  0.0 196.2 jit_solution(11092677836614331152)
XLA Ops:
  0.0 3.2 %dynamic-slice_select_fusion = bf16[1024,1024]{1,0:T(8,128)(2,1)S(1)} fusion(bf16[1024,2048]{1,0:T(8,128)(2,1)} %param.7, s32[]{:T(128)S(6)} %select_n.84, bf16[1024,2048]{1,0:T(8,128)(2,1)} %param.6, pred[]{:T(512)S(6)} %eq.17), kind=kLoop, calls=%fused_computation.9 | loop fusion | flops 1048576 | bytes 6291461 | tf_op jit(solution)/shard_map/jit(_where)/select_n | solution.py:159
  3.2 0.2 slice.9
  3.4 2.8 %collective-permute-start.2 = (bf16[1024,896]{1,0:T(8,128)(2,1)S(1)}, bf16[1024,896]{1,0:T(8,128)(2,1)S(1)}, u32[]{:S(2)}, u32[]{:S(2)}) collective-permute-start(bf16[1024,896]{1,0:T(8,128)(2,1)S(1)} %slice.9), channel_id=1, source_target_pairs={{33,0},{32,1},{35,2},{34,3},{37,4},{36,5},{39,6},{38,7},{41,8},{40... | collective-permute-start | bytes 5505032 | tf_op jit(solution)/shard_map/ppermute | solution.py:166
  6.2 0.1 slice.8
  6.3 0.3 collective-permute-start.1
  6.6 1.8 collective-permute-start
  8.4 7.1 %collective-permute-done.1 = bf16[1024,128]{1,0:T(8,128)(2,1)S(1)} collective-permute-done((bf16[1024,128]{1,0:T(8,128)(2,1)S(1)}, bf16[1024,128]{1,0:T(8,128)(2,1)S(1)}, u32[]{:S(2)}, u32[]{:S(2)}) %collective-permute-start.1) | collective-permute-done | bytes 262176 | tf_op jit(solution)/shard_map/ppermute | solution.py:23
  15.5 0.1 constant_dynamic-update-slice_fusion.1
  15.6 30.8 %collective-permute-done.2 = bf16[1024,896]{1,0:T(8,128)(2,1)S(1)} collective-permute-done((bf16[1024,896]{1,0:T(8,128)(2,1)S(1)}, bf16[1024,896]{1,0:T(8,128)(2,1)S(1)}, u32[]{:S(2)}, u32[]{:S(2)}) %collective-permute-start.2) | collective-permute-done | bytes 1835040 | tf_op jit(solution)/shard_map/ppermute | solution.py:166
  46.4 0.3 constant_dynamic-update-slice_fusion
  46.7 0.1 collective-permute-start.3
  46.8 0.0 copy-start.3
  46.9 2.8 %constant_dynamic-slice_fusion = (bf16[384,1024]{1,0:T(8,128)(2,1)}, bf16[384,1024]{1,0:T(8,128)(2,1)}) fusion(bf16[384,2048]{1,0:T(8,128)(2,1)} %param.5, s32[]{:T(128)S(6)} %select_n.89, s32[]{:T(128)S(6)} %select_n.84), kind=kLoop, calls=%fused_computation.28 | loop fusion | bytes 3145736 | tf_op jit(solution)/shard_map/dynamic_slice | solution.py:154
  49.7 0.0 copy-start.2
  49.7 0.0 collective-permute-done
  49.7 2.2 %broadcast_select_fusion.7 = (bf16[384,2048]{1,0:T(8,128)(2,1)S(1)}, bf16[384,2048]{1,0:T(8,128)(2,1)S(1)}) fusion(bf16[384,2048]{1,0:T(8,128)(2,1)} %param.4, bf16[384,2048]{1,0:T(8,128)(2,1)} %collective-permute-done, pred[]{:T(512)S(6)} %eq.16), kind=kLoop, calls=%fused_computation.20 | loop fusion | flops 1572864 | bytes 6291457 | tf_op jit(solution)/shard_map/jit(_where)/select_n | solution.py:27
  51.9 0.0 collective-permute-done.3
  51.9 0.0 copy-done.3
  51.9 0.9 copy-done.2
  52.8 3.7 %broadcast_select_fusion.3 = (bf16[1024,1024]{1,0:T(8,128)(2,1)S(1)}, bf16[1024,1024]{1,0:T(8,128)(2,1)S(1)}, bf16[1024,1024]{1,0:T(8,128)(2,1)S(1)}, bf16[1024,1024]{1,0:T(8,128)(2,1)S(1)}) fusion(pred[]{:T(512)S(6)} %eq.16, bf16[1024,2048]{1,0:T(8,128)(2,1)S(1)} %copy-done.2, s32[]{:T(128)S(6)} %select_n.89, bf16[1024,1024]{1,0:T(8,128)(2,1)} %collective-permute-done.3, ...), kind=kLoop, calls=%fused_computation.13 | loop fusion | flops 6291456 | bytes 16777222 | tf_op jit(solution)/shard_map/jit(_where)/select_n | solution.py:27
  56.5 3.4 %fusion.8.v0_ref = bf16[768,1024]{1,0:T(8,128)(2,1)S(1)} fusion(bf16[1024,1024]{1,0:T(8,128)(2,1)S(1)} %get-tuple-element.18, bf16[1024,1024]{1,0:T(8,128)(2,1)S(1)} %get-tuple-element.17, bf16[384,2048]{1,0:T(8,128)(2,1)S(1)} %get-tuple-element.24, bf16[384,2048]{1,0:T(8,128)(2,1)S(1)} %get-tuple-element.23), kind=kOutput, calls=%fused_computation.16 | convolution fusion | flops 3236691968 | bytes 8912896 | tf_op jit(solution)/shard_map/dot_general | solution.py:180
  59.9 0.0 copy-start
  59.9 3.4 %fusion.11.k0_ref = bf16[768,1024]{1,0:T(8,128)(2,1)S(1)} fusion(bf16[1024,1024]{1,0:T(8,128)(2,1)S(1)} %get-tuple-element.21, bf16[1024,1024]{1,0:T(8,128)(2,1)S(1)} %get-tuple-element.22, bf16[384,2048]{1,0:T(8,128)(2,1)S(1)} %get-tuple-element.24, bf16[384,2048]{1,0:T(8,128)(2,1)S(1)} %get-tuple-element.23), kind=kOutput, calls=%fused_computation.17 | convolution fusion | flops 3236691968 | bytes 8912896 | tf_op jit(solution)/shard_map/dot_general | solution.py:179
  63.4 0.0 copy-start.1
  63.4 2.4 %collective-permute-start.9 = (bf16[768,1024]{1,0:T(8,128)(2,1)S(1)}, bf16[768,1024]{1,0:T(8,128)(2,1)}, u32[]{:S(2)}, u32[]{:S(2)}) collective-permute-start(bf16[768,1024]{1,0:T(8,128)(2,1)S(1)} %fusion.8.v0_ref), channel_id=1, source_target_pairs={{0,2},{2,4},{4,6},{6,8},{8,10},{10,12},{12,14},{14,16},{16,18},{18... | collective-permute-start | bytes 4718600 | tf_op jit(solution)/shard_map/ppermute | solution.py:19
  65.8 3.5 %collective-permute-start.6 = (bf16[768,1024]{1,0:T(8,128)(2,1)S(1)}, bf16[768,1024]{1,0:T(8,128)(2,1)}, u32[]{:S(2)}, u32[]{:S(2)}) collective-permute-start(bf16[768,1024]{1,0:T(8,128)(2,1)S(1)} %fusion.11.k0_ref), channel_id=1, source_target_pairs={{0,2},{2,4},{4,6},{6,8},{8,10},{10,12},{12,14},{14,16},{16,18},{18... | collective-permute-start | bytes 4718600 | tf_op jit(solution)/shard_map/ppermute | solution.py:19
  69.2 3.8 %collective-permute-start.5 = (bf16[768,1024]{1,0:T(8,128)(2,1)S(1)}, bf16[768,1024]{1,0:T(8,128)(2,1)}, u32[]{:S(2)}, u32[]{:S(2)}) collective-permute-start(bf16[768,1024]{1,0:T(8,128)(2,1)S(1)} %fusion.11.k0_ref), channel_id=1, source_target_pairs={{0,4},{4,8},{8,12},{12,16},{16,20},{20,24},{24,28},{28,32},{32,36}... | collective-permute-start | bytes 4718600 | tf_op jit(solution)/shard_map/ppermute | solution.py:191
  73.1 0.0 copy-done
  73.1 3.8 %collective-permute-start.8 = (bf16[768,1024]{1,0:T(8,128)(2,1)S(1)}, bf16[768,1024]{1,0:T(8,128)(2,1)}, u32[]{:S(2)}, u32[]{:S(2)}) collective-permute-start(bf16[768,1024]{1,0:T(8,128)(2,1)S(1)} %fusion.8.v0_ref), channel_id=1, source_target_pairs={{0,4},{4,8},{8,12},{12,16},{16,20},{20,24},{24,28},{28,32},{32,36}... | collective-permute-start | bytes 4718600 | tf_op jit(solution)/shard_map/ppermute | solution.py:191
  76.9 25.5 %collective-permute-done.9.v1_ref = bf16[768,1024]{1,0:T(8,128)(2,1)} collective-permute-done((bf16[768,1024]{1,0:T(8,128)(2,1)S(1)}, bf16[768,1024]{1,0:T(8,128)(2,1)}, u32[]{:S(2)}, u32[]{:S(2)}) %collective-permute-start.9) | collective-permute-done | bytes 1572896 | tf_op jit(solution)/shard_map/ppermute | solution.py:19
  102.4 2.5 %collective-permute-start.10 = (bf16[768,1024]{1,0:T(8,128)(2,1)}, bf16[768,1024]{1,0:T(8,128)(2,1)}, u32[]{:S(2)}, u32[]{:S(2)}) collective-permute-start(bf16[768,1024]{1,0:T(8,128)(2,1)} %collective-permute-done.9.v1_ref), channel_id=1, source_target_pairs={{0,2},{4,6},{8,10},{12,14},{16,18},{20,22},{24,26},{28,30},{32,34}... | collective-permute-start | bytes 4718600 | tf_op jit(solution)/shard_map/ppermute | solution.py:192
  104.9 31.2 %collective-permute-done.6.k1_ref = bf16[768,1024]{1,0:T(8,128)(2,1)} collective-permute-done((bf16[768,1024]{1,0:T(8,128)(2,1)S(1)}, bf16[768,1024]{1,0:T(8,128)(2,1)}, u32[]{:S(2)}, u32[]{:S(2)}) %collective-permute-start.6) | collective-permute-done | bytes 1572896 | tf_op jit(solution)/shard_map/ppermute | solution.py:19
  136.1 2.4 %collective-permute-start.7 = (bf16[768,1024]{1,0:T(8,128)(2,1)}, bf16[768,1024]{1,0:T(8,128)(2,1)}, u32[]{:S(2)}, u32[]{:S(2)}) collective-permute-start(bf16[768,1024]{1,0:T(8,128)(2,1)} %collective-permute-done.6.k1_ref), channel_id=1, source_target_pairs={{0,2},{4,6},{8,10},{12,14},{16,18},{20,22},{24,26},{28,30},{32,34}... | collective-permute-start | bytes 4718600 | tf_op jit(solution)/shard_map/ppermute | solution.py:192
  138.6 2.6 %collective-permute-start.4 = (bf16[384,1024]{1,0:T(8,128)(2,1)}, bf16[384,1024]{1,0:T(8,128)(2,1)}, u32[]{:S(2)}, u32[]{:S(2)}) collective-permute-start(bf16[384,1024]{1,0:T(8,128)(2,1)} %get-tuple-element.11), channel_id=1, source_target_pairs={{0,1},{1,0},{2,3},{3,2},{4,5},{5,4},{6,7},{7,6},{8,9},{9,8},{10,11... | collective-permute-start | bytes 2359304 | tf_op jit(solution)/shard_map/ppermute | solution.py:23
  141.2 0.7 add_add_fusion.seg_ref
  141.9 0.7 add_add_fusion.1.seg_ref
  142.5 0.0 collective-permute-done.5.k2e_ref
  142.5 0.0 collective-permute-done.8.v2e_ref
  142.5 0.0 collective-permute-done.10.v2o_ref
  142.6 0.0 collective-permute-done.7.k2o_ref
  142.6 0.0 copy-done.1
  142.6 15.4 %shard_map.46 = bf16[384,768]{1,0:T(8,128)(2,1)} custom-call(s32[3]{0:T(128)} %add_add_fusion.seg_ref, bf16[384,1024]{1,0:T(8,128)(2,1)} %get-tuple-element.16.q_ref, bf16[768,1024]{1,0:T(8,128)(2,1)} %collective-permute-done.5.k2e_ref, bf16[768,1024]{1,0:T(8,128)(2,1)} %collective-permute-done.7.k2o_ref, bf16[768,1024]{1,0:T(8,128)(2,1)} %collective-permute-done.6.k1_ref, ...), custom_call_target="tpu_custom_call" | custom-call | tf_op jit(solution)/shard_map/pallas_call | solution.py:131
  158.0 0.0 collective-permute-done.4.q_ref
  158.0 11.6 %shard_map.49 = bf16[384,512]{1,0:T(8,128)(2,1)} custom-call(s32[3]{0:T(128)} %add_add_fusion.1.seg_ref, bf16[384,1024]{1,0:T(8,128)(2,1)} %collective-permute-done.4.q_ref, bf16[768,1024]{1,0:T(8,128)(2,1)} %collective-permute-done.5.k2e_ref, bf16[768,1024]{1,0:T(8,128)(2,1)} %collective-permute-done.7.k2o_ref, ...), custom_call_target="tpu_custom_call" | custom-call | tf_op jit(solution)/shard_map/pallas_call | solution.py:131
  169.6 1.0 collective-permute-start.11
  170.6 11.6 %shard_map.47 = bf16[384,512]{1,0:T(8,128)(2,1)} custom-call(s32[3]{0:T(128)} %add_add_fusion.1.seg_ref, bf16[384,1024]{1,0:T(8,128)(2,1)} %collective-permute-done.4.q_ref, bf16[768,1024]{1,0:T(8,128)(2,1)} %collective-permute-done.5.k2e_ref, bf16[768,1024]{1,0:T(8,128)(2,1)} %collective-permute-done.7.k2o_ref, ...), custom_call_target="tpu_custom_call" | custom-call | tf_op jit(solution)/shard_map/pallas_call | solution.py:131
  182.2 0.0 copy-start.4
  182.2 0.8 collective-permute-start.12
  183.0 7.0 %shard_map.48 = bf16[384,256]{1,0:T(8,128)(2,1)} custom-call(s32[3]{0:T(128)} %add_add_fusion.seg_ref, bf16[384,1024]{1,0:T(8,128)(2,1)} %get-tuple-element.16.q_ref, bf16[768,1024]{1,0:T(8,128)(2,1)} %collective-permute-done.5.k2e_ref, bf16[768,1024]{1,0:T(8,128)(2,1)} %collective-permute-done.7.k2o_ref, bf16[768,1024]{1,0:T(8,128)(2,1)} %collective-permute-done.6.k1_ref, ...), custom_call_target="tpu_custom_call" | custom-call | tf_op jit(solution)/shard_map/pallas_call | solution.py:131
  190.0 0.0 collective-permute-done.11
  190.0 3.6 %collective-permute-done.12 = bf16[384,512]{1,0:T(8,128)(2,1)S(1)} collective-permute-done((bf16[384,512]{1,0:T(8,128)(2,1)}, bf16[384,512]{1,0:T(8,128)(2,1)S(1)}, u32[]{:S(2)}, u32[]{:S(2)}) %collective-permute-start.12) | collective-permute-done | bytes 393248 | tf_op jit(solution)/shard_map/ppermute | solution.py:23
  193.7 0.0 copy-done.4
  193.7 1.3 broadcast_select_fusion.9
  195.0 1.2 pad_maximum_fusion.7
  (2 shorter events, 0.1 us)
Async XLA Ops:
  3.4 43.0 %collective-permute-start.2 = (bf16[1024,896]{1,0:T(8,128)(2,1)S(1)}, bf16[1024,896]{1,0:T(8,128)(2,1)S(1)}, u32[]{:S(2)}, u32[]{:S(2)}) collective-permute-start(bf16[1024,896]{1,0:T(8,128)(2,1)S(1)} %slice.9), channel_id=1, source_target_pairs={{33,0},{32,1},{35,2},{34,3},{37,4},{36,5},{39,6},{38,7},{41,8},{40... | collective-permute-start | bytes 5505032 | tf_op jit(solution)/shard_map/ppermute | solution.py:166
  6.3 9.3 %collective-permute-start.1 = (bf16[1024,128]{1,0:T(8,128)(2,1)S(1)}, bf16[1024,128]{1,0:T(8,128)(2,1)S(1)}, u32[]{:S(2)}, u32[]{:S(2)}) collective-permute-start(bf16[1024,128]{1,0:T(8,128)(2,1)S(1)} %slice.8), channel_id=1, source_target_pairs={{0,1},{1,0},{2,3},{3,2},{4,5},{5,4},{6,7},{7,6},{8,9},{9,8},{10,11... | collective-permute-start | bytes 786440 | tf_op jit(solution)/shard_map/ppermute | solution.py:23
  6.6 43.1 %collective-permute-start = (bf16[384,2048]{1,0:T(8,128)(2,1)}, bf16[384,2048]{1,0:T(8,128)(2,1)}, u32[]{:S(2)}, u32[]{:S(2)}) collective-permute-start(bf16[384,2048]{1,0:T(8,128)(2,1)} %param.4), channel_id=1, source_target_pairs={{0,1},{1,0},{2,3},{3,2},{4,5},{5,4},{6,7},{7,6},{8,9},{9,8},{10,11... | collective-permute-start | bytes 4718600 | tf_op jit(solution)/shard_map/ppermute | solution.py:23
  46.7 5.2 %collective-permute-start.3 = (bf16[1024,1024]{1,0:T(8,128)(2,1)S(1)}, bf16[1024,1024]{1,0:T(8,128)(2,1)}, u32[]{:S(2)}, u32[]{:S(2)}) collective-permute-start(bf16[1024,1024]{1,0:T(8,128)(2,1)S(1)} %constant_dynamic-update-slice_fusion), channel_id=1, source_target_pairs={{0,2},{2,0},{4,6},{6,4},{8,10},{10,8},{12,14},{14,12},{16,18},{18,... | collective-permute-start | bytes 6291464 | tf_op jit(solution)/shard_map/ppermute | solution.py:169
  46.8 5.1 %copy-start.3 = (bf16[1024,2048]{1,0:T(8,128)(2,1)S(1)}, bf16[1024,2048]{1,0:T(8,128)(2,1)}, u32[]{:S(2)}) copy-start(bf16[1024,2048]{1,0:T(8,128)(2,1)} %param.6) | copy-start | bytes 12582916
  49.7 3.1 %copy-start.2 = (bf16[1024,2048]{1,0:T(8,128)(2,1)S(1)}, bf16[1024,2048]{1,0:T(8,128)(2,1)}, u32[]{:S(2)}) copy-start(bf16[1024,2048]{1,0:T(8,128)(2,1)} %param.7) | copy-start | bytes 12582916
  59.9 13.2 %copy-start = (bf16[768,1024]{1,0:T(8,128)(2,1)}, bf16[768,1024]{1,0:T(8,128)(2,1)S(1)}, u32[]{:S(2)}) copy-start(bf16[768,1024]{1,0:T(8,128)(2,1)S(1)} %fusion.8.v0_ref) | copy-start | bytes 4718596
  63.4 79.2 %copy-start.1 = (bf16[768,1024]{1,0:T(8,128)(2,1)}, bf16[768,1024]{1,0:T(8,128)(2,1)S(1)}, u32[]{:S(2)}) copy-start(bf16[768,1024]{1,0:T(8,128)(2,1)S(1)} %fusion.11.k0_ref) | copy-start | bytes 4718596
  63.4 39.0 %collective-permute-start.9 = (bf16[768,1024]{1,0:T(8,128)(2,1)S(1)}, bf16[768,1024]{1,0:T(8,128)(2,1)}, u32[]{:S(2)}, u32[]{:S(2)}) collective-permute-start(bf16[768,1024]{1,0:T(8,128)(2,1)S(1)} %fusion.8.v0_ref), channel_id=1, source_target_pairs={{0,2},{2,4},{4,6},{6,8},{8,10},{10,12},{12,14},{14,16},{16,18},{18... | collective-permute-start | bytes 4718600 | tf_op jit(solution)/shard_map/ppermute | solution.py:19
  65.8 70.4 %collective-permute-start.6 = (bf16[768,1024]{1,0:T(8,128)(2,1)S(1)}, bf16[768,1024]{1,0:T(8,128)(2,1)}, u32[]{:S(2)}, u32[]{:S(2)}) collective-permute-start(bf16[768,1024]{1,0:T(8,128)(2,1)S(1)} %fusion.11.k0_ref), channel_id=1, source_target_pairs={{0,2},{2,4},{4,6},{6,8},{8,10},{10,12},{12,14},{14,16},{16,18},{18... | collective-permute-start | bytes 4718600 | tf_op jit(solution)/shard_map/ppermute | solution.py:19
  69.2 73.3 %collective-permute-start.5 = (bf16[768,1024]{1,0:T(8,128)(2,1)S(1)}, bf16[768,1024]{1,0:T(8,128)(2,1)}, u32[]{:S(2)}, u32[]{:S(2)}) collective-permute-start(bf16[768,1024]{1,0:T(8,128)(2,1)S(1)} %fusion.11.k0_ref), channel_id=1, source_target_pairs={{0,4},{4,8},{8,12},{12,16},{16,20},{20,24},{24,28},{28,32},{32,36}... | collective-permute-start | bytes 4718600 | tf_op jit(solution)/shard_map/ppermute | solution.py:191
  73.1 69.5 %collective-permute-start.8 = (bf16[768,1024]{1,0:T(8,128)(2,1)S(1)}, bf16[768,1024]{1,0:T(8,128)(2,1)}, u32[]{:S(2)}, u32[]{:S(2)}) collective-permute-start(bf16[768,1024]{1,0:T(8,128)(2,1)S(1)} %fusion.8.v0_ref), channel_id=1, source_target_pairs={{0,4},{4,8},{8,12},{12,16},{16,20},{20,24},{24,28},{28,32},{32,36}... | collective-permute-start | bytes 4718600 | tf_op jit(solution)/shard_map/ppermute | solution.py:191
  102.4 40.2 %collective-permute-start.10 = (bf16[768,1024]{1,0:T(8,128)(2,1)}, bf16[768,1024]{1,0:T(8,128)(2,1)}, u32[]{:S(2)}, u32[]{:S(2)}) collective-permute-start(bf16[768,1024]{1,0:T(8,128)(2,1)} %collective-permute-done.9.v1_ref), channel_id=1, source_target_pairs={{0,2},{4,6},{8,10},{12,14},{16,18},{20,22},{24,26},{28,30},{32,34}... | collective-permute-start | bytes 4718600 | tf_op jit(solution)/shard_map/ppermute | solution.py:192
  136.1 6.4 %collective-permute-start.7 = (bf16[768,1024]{1,0:T(8,128)(2,1)}, bf16[768,1024]{1,0:T(8,128)(2,1)}, u32[]{:S(2)}, u32[]{:S(2)}) collective-permute-start(bf16[768,1024]{1,0:T(8,128)(2,1)} %collective-permute-done.6.k1_ref), channel_id=1, source_target_pairs={{0,2},{4,6},{8,10},{12,14},{16,18},{20,22},{24,26},{28,30},{32,34}... | collective-permute-start | bytes 4718600 | tf_op jit(solution)/shard_map/ppermute | solution.py:192
  138.6 19.4 %collective-permute-start.4 = (bf16[384,1024]{1,0:T(8,128)(2,1)}, bf16[384,1024]{1,0:T(8,128)(2,1)}, u32[]{:S(2)}, u32[]{:S(2)}) collective-permute-start(bf16[384,1024]{1,0:T(8,128)(2,1)} %get-tuple-element.11), channel_id=1, source_target_pairs={{0,1},{1,0},{2,3},{3,2},{4,5},{5,4},{6,7},{7,6},{8,9},{9,8},{10,11... | collective-permute-start | bytes 2359304 | tf_op jit(solution)/shard_map/ppermute | solution.py:23
  169.6 20.4 %collective-permute-start.11 = (bf16[384,512]{1,0:T(8,128)(2,1)}, bf16[384,512]{1,0:T(8,128)(2,1)S(1)}, u32[]{:S(2)}, u32[]{:S(2)}) collective-permute-start(bf16[384,512]{1,0:T(8,128)(2,1)} %shard_map.49), channel_id=1, source_target_pairs={{0,1},{1,0},{2,3},{3,2},{4,5},{5,4},{6,7},{7,6},{8,9},{9,8},{10,11... | collective-permute-start | bytes 1179656 | tf_op jit(solution)/shard_map/ppermute | solution.py:23
  182.2 11.5 %copy-start.4 = (bf16[384,768]{1,0:T(8,128)(2,1)S(1)}, bf16[384,768]{1,0:T(8,128)(2,1)}, u32[]{:S(2)}) copy-start(bf16[384,768]{1,0:T(8,128)(2,1)} %shard_map.46) | copy-start | bytes 1769476
  182.2 11.4 %collective-permute-start.12 = (bf16[384,512]{1,0:T(8,128)(2,1)}, bf16[384,512]{1,0:T(8,128)(2,1)S(1)}, u32[]{:S(2)}, u32[]{:S(2)}) collective-permute-start(bf16[384,512]{1,0:T(8,128)(2,1)} %shard_map.47), channel_id=1, source_target_pairs={{0,1},{1,0},{2,3},{3,2},{4,5},{5,4},{6,7},{7,6},{8,9},{9,8},{10,11... | collective-permute-start | bytes 1179656 | tf_op jit(solution)/shard_map/ppermute | solution.py:23

commit v10 on v9

--- a/solution.py
+++ b/solution.py
@@ -198,7 +198,7 @@
     values = (*value_two, value_one, own_value)
 
     heads = cols // HD
-    lead = heads - heads // 4
+    lead = heads - 3 * heads // 8
     mine_q = mine_of(queries)
     mine_lead = attend(seg_number, half_number * tok_rows, mine_q, keys, values, 0, lead)
     query_got, mine_lead = lax.optimization_barrier((query_got, mine_lead))
@@ -208,9 +208,9 @@
         got.append(swap_halves(their_rows))
     mine_q, their_rows = lax.optimization_barrier((mine_q, their_rows))
     mine_tail = attend(seg_number, half_number * tok_rows, mine_q, keys, values, lead, heads - lead)
-    mine_rows = jnp.concatenate([mine_lead, mine_tail], axis=1)
-    rows_got = jnp.concatenate(got, axis=1)
-    return in_order(first_is_mine, mine_rows, rows_got, 1)
+    mine_first = jnp.concatenate([mine_lead, mine_tail, *got], axis=1)
+    theirs_first = jnp.concatenate([*got, mine_lead, mine_tail], axis=1)
+    return jnp.where(first_is_mine, mine_first, theirs_first)
 
 
 def solution(mesh):

time: 197 us -> 195 us (0.990)
  waiting for transfers between devices: 98.3 us -> 96.1 us
    select_n x0 -> x1, other arithmetic: none -> 2.34 us  [body(): return jnp.where(first_is_mine, mine_first, theirs_first)]
    ppermute x5, waiting for transfers between devices: 10.8 us -> 8.65 us  [swap_halves(): return lax.ppermute(value, 'fsdp', [(0, 1), (1, 0)])]
    select_n x3 -> x2, other arithmetic: 7.2 us -> 5.91 us  [in_order(): lead = jnp.where(first_is_mine, mine, other)]
  transfers between devices with their start and end apart: 13 -> 13, of which waited for: 5 -> 6; matrix products, arithmetic and copies ran while one was open for 3% -> 3% of each run, Pallas kernels for 17% -> 18%
where the time goes in v10:
time: 195 us; the launch traced here: 194 us
  waiting for transfers between devices  96.1 us (49%)
  Pallas kernels  45.7 us (23%)
  starting transfers between devices  27.9 us (14%)
  other arithmetic  12.7 us (7%)
  matrix products  6.85 us (4%)
  local copies, waits for them, and re-layouts  4.33 us (2%)
    ppermute x2, waiting for transfers between devices, from_behind(): lax.ppermute(value, axis, [(source, source + steps) for source in range(l...  56.7 us
    pallas_call x4, Pallas kernels, attend(): pl.pallas_call(attention_kernel, grid_spec=grid_spec, out_shape=jax.Shape...  45.7 us
    ppermute x1, waiting for transfers between devices, body(): right_got = lax.ppermute(served[:, piece:], ('seg', 'fsdp'), wrap_pairs)  30.8 us
    ppermute x5, waiting for transfers between devices, swap_halves(): return lax.ppermute(value, 'fsdp', [(0, 1), (1, 0)])  8.65 us
    ppermute x2, starting transfers between devices, shifted(): even_two = lax.ppermute(own, 'seg', even_pairs)  7.65 us
    ppermute x5, starting transfers between devices, swap_halves(): return lax.ppermute(value, 'fsdp', [(0, 1), (1, 0)])  6.51 us
    select_n x2, other arithmetic, in_order(): lead = jnp.where(first_is_mine, mine, other)  5.91 us
    ppermute x2, starting transfers between devices, from_behind(): lax.ppermute(value, axis, [(source, source + steps) for source in range(l...  5.85 us
  transfers between devices with their start and end apart: 13, of which 6 were waited for; matrix products, arithmetic and copies ran while one was open for 3% of the time, Pallas kernels for 18%

profile of v10, /device:TPU:24, one launch (start us, length us, event | category | flops | bytes accessed | tf_op | source)
XLA Modules:
  0.0 193.8 jit_solution(1768008106595767638)
XLA Ops:
  0.0 3.2 %dynamic-slice_select_fusion = bf16[1024,1024]{1,0:T(8,128)(2,1)S(1)} fusion(bf16[1024,2048]{1,0:T(8,128)(2,1)} %param.7, s32[]{:T(128)S(6)} %select_n.76, bf16[1024,2048]{1,0:T(8,128)(2,1)} %param.6, pred[]{:T(512)S(6)} %eq.17), kind=kLoop, calls=%fused_computation.9 | loop fusion | flops 1048576 | bytes 6291461 | tf_op jit(solution)/shard_map/jit(_where)/select_n | solution.py:159
  3.2 0.2 slice.9
  3.4 2.8 %collective-permute-start.2 = (bf16[1024,896]{1,0:T(8,128)(2,1)S(1)}, bf16[1024,896]{1,0:T(8,128)(2,1)S(1)}, u32[]{:S(2)}, u32[]{:S(2)}) collective-permute-start(bf16[1024,896]{1,0:T(8,128)(2,1)S(1)} %slice.9), channel_id=1, source_target_pairs={{33,0},{32,1},{35,2},{34,3},{37,4},{36,5},{39,6},{38,7},{41,8},{40... | collective-permute-start | bytes 5505032 | tf_op jit(solution)/shard_map/ppermute | solution.py:166
  6.2 0.1 slice.8
  6.3 0.3 collective-permute-start.1
  6.6 1.8 collective-permute-start
  8.4 7.1 %collective-permute-done.1 = bf16[1024,128]{1,0:T(8,128)(2,1)S(1)} collective-permute-done((bf16[1024,128]{1,0:T(8,128)(2,1)S(1)}, bf16[1024,128]{1,0:T(8,128)(2,1)S(1)}, u32[]{:S(2)}, u32[]{:S(2)}) %collective-permute-start.1) | collective-permute-done | bytes 262176 | tf_op jit(solution)/shard_map/ppermute | solution.py:23
  15.5 0.1 constant_dynamic-update-slice_fusion.1
  15.6 30.8 %collective-permute-done.2 = bf16[1024,896]{1,0:T(8,128)(2,1)S(1)} collective-permute-done((bf16[1024,896]{1,0:T(8,128)(2,1)S(1)}, bf16[1024,896]{1,0:T(8,128)(2,1)S(1)}, u32[]{:S(2)}, u32[]{:S(2)}) %collective-permute-start.2) | collective-permute-done | bytes 1835040 | tf_op jit(solution)/shard_map/ppermute | solution.py:166
  46.4 0.3 constant_dynamic-update-slice_fusion
  46.7 0.1 collective-permute-start.3
  46.8 0.0 copy-start.3
  46.9 2.8 %constant_dynamic-slice_fusion = (bf16[384,1024]{1,0:T(8,128)(2,1)}, bf16[384,1024]{1,0:T(8,128)(2,1)}) fusion(bf16[384,2048]{1,0:T(8,128)(2,1)} %param.5, s32[]{:T(128)S(6)} %select_n.80, s32[]{:T(128)S(6)} %select_n.76), kind=kLoop, calls=%fused_computation.23 | loop fusion | bytes 3145736 | tf_op jit(solution)/shard_map/dynamic_slice | solution.py:154
  49.7 0.0 copy-start.2
  49.7 0.0 collective-permute-done
  49.7 2.2 %broadcast_select_fusion.7 = (bf16[384,2048]{1,0:T(8,128)(2,1)S(1)}, bf16[384,2048]{1,0:T(8,128)(2,1)S(1)}) fusion(bf16[384,2048]{1,0:T(8,128)(2,1)} %param.4, bf16[384,2048]{1,0:T(8,128)(2,1)} %collective-permute-done, pred[]{:T(512)S(6)} %eq.16), kind=kLoop, calls=%fused_computation.20 | loop fusion | flops 1572864 | bytes 6291457 | tf_op jit(solution)/shard_map/jit(_where)/select_n | solution.py:27
  51.9 0.0 collective-permute-done.3
  51.9 0.0 copy-done.3
  52.0 0.9 copy-done.2
  52.8 3.7 %broadcast_select_fusion.3 = (bf16[1024,1024]{1,0:T(8,128)(2,1)S(1)}, bf16[1024,1024]{1,0:T(8,128)(2,1)S(1)}, bf16[1024,1024]{1,0:T(8,128)(2,1)S(1)}, bf16[1024,1024]{1,0:T(8,128)(2,1)S(1)}) fusion(pred[]{:T(512)S(6)} %eq.16, bf16[1024,2048]{1,0:T(8,128)(2,1)S(1)} %copy-done.2, s32[]{:T(128)S(6)} %select_n.80, bf16[1024,1024]{1,0:T(8,128)(2,1)} %collective-permute-done.3, ...), kind=kLoop, calls=%fused_computation.13 | loop fusion | flops 6291456 | bytes 16777222 | tf_op jit(solution)/shard_map/jit(_where)/select_n | solution.py:27
  56.5 3.4 %fusion.8.v0_ref = bf16[768,1024]{1,0:T(8,128)(2,1)S(1)} fusion(bf16[1024,1024]{1,0:T(8,128)(2,1)S(1)} %get-tuple-element.18, bf16[1024,1024]{1,0:T(8,128)(2,1)S(1)} %get-tuple-element.17, bf16[384,2048]{1,0:T(8,128)(2,1)S(1)} %get-tuple-element.24, bf16[384,2048]{1,0:T(8,128)(2,1)S(1)} %get-tuple-element.23), kind=kOutput, calls=%fused_computation.16 | convolution fusion | flops 3236691968 | bytes 8912896 | tf_op jit(solution)/shard_map/dot_general | solution.py:180
  59.9 0.0 copy-start
  59.9 3.4 %fusion.11.k0_ref = bf16[768,1024]{1,0:T(8,128)(2,1)S(1)} fusion(bf16[1024,1024]{1,0:T(8,128)(2,1)S(1)} %get-tuple-element.21, bf16[1024,1024]{1,0:T(8,128)(2,1)S(1)} %get-tuple-element.22, bf16[384,2048]{1,0:T(8,128)(2,1)S(1)} %get-tuple-element.24, bf16[384,2048]{1,0:T(8,128)(2,1)S(1)} %get-tuple-element.23), kind=kOutput, calls=%fused_computation.17 | convolution fusion | flops 3236691968 | bytes 8912896 | tf_op jit(solution)/shard_map/dot_general | solution.py:179
  63.4 0.0 copy-start.1
  63.4 2.4 %collective-permute-start.9 = (bf16[768,1024]{1,0:T(8,128)(2,1)S(1)}, bf16[768,1024]{1,0:T(8,128)(2,1)}, u32[]{:S(2)}, u32[]{:S(2)}) collective-permute-start(bf16[768,1024]{1,0:T(8,128)(2,1)S(1)} %fusion.8.v0_ref), channel_id=1, source_target_pairs={{0,2},{2,4},{4,6},{6,8},{8,10},{10,12},{12,14},{14,16},{16,18},{18... | collective-permute-start | bytes 4718600 | tf_op jit(solution)/shard_map/ppermute | solution.py:19
  65.8 3.5 %collective-permute-start.6 = (bf16[768,1024]{1,0:T(8,128)(2,1)S(1)}, bf16[768,1024]{1,0:T(8,128)(2,1)}, u32[]{:S(2)}, u32[]{:S(2)}) collective-permute-start(bf16[768,1024]{1,0:T(8,128)(2,1)S(1)} %fusion.11.k0_ref), channel_id=1, source_target_pairs={{0,2},{2,4},{4,6},{6,8},{8,10},{10,12},{12,14},{14,16},{16,18},{18... | collective-permute-start | bytes 4718600 | tf_op jit(solution)/shard_map/ppermute | solution.py:19
  69.3 3.8 %collective-permute-start.5 = (bf16[768,1024]{1,0:T(8,128)(2,1)S(1)}, bf16[768,1024]{1,0:T(8,128)(2,1)}, u32[]{:S(2)}, u32[]{:S(2)}) collective-permute-start(bf16[768,1024]{1,0:T(8,128)(2,1)S(1)} %fusion.11.k0_ref), channel_id=1, source_target_pairs={{0,4},{4,8},{8,12},{12,16},{16,20},{20,24},{24,28},{28,32},{32,36}... | collective-permute-start | bytes 4718600 | tf_op jit(solution)/shard_map/ppermute | solution.py:191
  73.1 0.0 copy-done
  73.1 3.8 %collective-permute-start.8 = (bf16[768,1024]{1,0:T(8,128)(2,1)S(1)}, bf16[768,1024]{1,0:T(8,128)(2,1)}, u32[]{:S(2)}, u32[]{:S(2)}) collective-permute-start(bf16[768,1024]{1,0:T(8,128)(2,1)S(1)} %fusion.8.v0_ref), channel_id=1, source_target_pairs={{0,4},{4,8},{8,12},{12,16},{16,20},{20,24},{24,28},{28,32},{32,36}... | collective-permute-start | bytes 4718600 | tf_op jit(solution)/shard_map/ppermute | solution.py:191
  76.9 25.5 %collective-permute-done.9.v1_ref = bf16[768,1024]{1,0:T(8,128)(2,1)} collective-permute-done((bf16[768,1024]{1,0:T(8,128)(2,1)S(1)}, bf16[768,1024]{1,0:T(8,128)(2,1)}, u32[]{:S(2)}, u32[]{:S(2)}) %collective-permute-start.9) | collective-permute-done | bytes 1572896 | tf_op jit(solution)/shard_map/ppermute | solution.py:19
  102.4 2.5 %collective-permute-start.10 = (bf16[768,1024]{1,0:T(8,128)(2,1)}, bf16[768,1024]{1,0:T(8,128)(2,1)}, u32[]{:S(2)}, u32[]{:S(2)}) collective-permute-start(bf16[768,1024]{1,0:T(8,128)(2,1)} %collective-permute-done.9.v1_ref), channel_id=1, source_target_pairs={{0,2},{4,6},{8,10},{12,14},{16,18},{20,22},{24,26},{28,30},{32,34}... | collective-permute-start | bytes 4718600 | tf_op jit(solution)/shard_map/ppermute | solution.py:192
  104.9 31.2 %collective-permute-done.6.k1_ref = bf16[768,1024]{1,0:T(8,128)(2,1)} collective-permute-done((bf16[768,1024]{1,0:T(8,128)(2,1)S(1)}, bf16[768,1024]{1,0:T(8,128)(2,1)}, u32[]{:S(2)}, u32[]{:S(2)}) %collective-permute-start.6) | collective-permute-done | bytes 1572896 | tf_op jit(solution)/shard_map/ppermute | solution.py:19
  136.1 2.4 %collective-permute-start.7 = (bf16[768,1024]{1,0:T(8,128)(2,1)}, bf16[768,1024]{1,0:T(8,128)(2,1)}, u32[]{:S(2)}, u32[]{:S(2)}) collective-permute-start(bf16[768,1024]{1,0:T(8,128)(2,1)} %collective-permute-done.6.k1_ref), channel_id=1, source_target_pairs={{0,2},{4,6},{8,10},{12,14},{16,18},{20,22},{24,26},{28,30},{32,34}... | collective-permute-start | bytes 4718600 | tf_op jit(solution)/shard_map/ppermute | solution.py:192
  138.6 2.6 %collective-permute-start.4 = (bf16[384,1024]{1,0:T(8,128)(2,1)}, bf16[384,1024]{1,0:T(8,128)(2,1)}, u32[]{:S(2)}, u32[]{:S(2)}) collective-permute-start(bf16[384,1024]{1,0:T(8,128)(2,1)} %get-tuple-element.11), channel_id=1, source_target_pairs={{0,1},{1,0},{2,3},{3,2},{4,5},{5,4},{6,7},{7,6},{8,9},{9,8},{10,11... | collective-permute-start | bytes 2359304 | tf_op jit(solution)/shard_map/ppermute | solution.py:23
  141.2 0.6 add_add_fusion.seg_ref
  141.9 0.6 add_add_fusion.1.seg_ref
  142.5 0.0 collective-permute-done.5.k2e_ref
  142.5 0.0 collective-permute-done.8.v2e_ref
  142.5 0.0 collective-permute-done.10.v2o_ref
  142.5 0.0 collective-permute-done.7.k2o_ref
  142.5 0.0 copy-done.1
  142.5 13.4 %shard_map.46 = bf16[384,640]{1,0:T(8,128)(2,1)} custom-call(s32[3]{0:T(128)} %add_add_fusion.seg_ref, bf16[384,1024]{1,0:T(8,128)(2,1)} %get-tuple-element.16.q_ref, bf16[768,1024]{1,0:T(8,128)(2,1)} %collective-permute-done.5.k2e_ref, bf16[768,1024]{1,0:T(8,128)(2,1)} %collective-permute-done.7.k2o_ref, bf16[768,1024]{1,0:T(8,128)(2,1)} %collective-permute-done.6.k1_ref, ...), custom_call_target="tpu_custom_call" | custom-call | tf_op jit(solution)/shard_map/pallas_call | solution.py:131
  155.9 0.7 collective-permute-done.4.q_ref
  156.6 11.6 %shard_map.49 = bf16[384,512]{1,0:T(8,128)(2,1)} custom-call(s32[3]{0:T(128)} %add_add_fusion.1.seg_ref, bf16[384,1024]{1,0:T(8,128)(2,1)} %collective-permute-done.4.q_ref, bf16[768,1024]{1,0:T(8,128)(2,1)} %collective-permute-done.5.k2e_ref, bf16[768,1024]{1,0:T(8,128)(2,1)} %collective-permute-done.7.k2o_ref, ...), custom_call_target="tpu_custom_call" | custom-call | tf_op jit(solution)/shard_map/pallas_call | solution.py:131
  168.1 1.4 collective-permute-start.11
  169.5 11.6 %shard_map.47 = bf16[384,512]{1,0:T(8,128)(2,1)} custom-call(s32[3]{0:T(128)} %add_add_fusion.1.seg_ref, bf16[384,1024]{1,0:T(8,128)(2,1)} %collective-permute-done.4.q_ref, bf16[768,1024]{1,0:T(8,128)(2,1)} %collective-permute-done.5.k2e_ref, bf16[768,1024]{1,0:T(8,128)(2,1)} %collective-permute-done.7.k2o_ref, ...), custom_call_target="tpu_custom_call" | custom-call | tf_op jit(solution)/shard_map/pallas_call | solution.py:131
  181.1 0.0 copy-start.4
  181.1 0.4 collective-permute-start.12
  181.5 9.2 %shard_map.48 = bf16[384,384]{1,0:T(8,128)(2,1)} custom-call(s32[3]{0:T(128)} %add_add_fusion.seg_ref, bf16[384,1024]{1,0:T(8,128)(2,1)} %get-tuple-element.16.q_ref, bf16[768,1024]{1,0:T(8,128)(2,1)} %collective-permute-done.5.k2e_ref, bf16[768,1024]{1,0:T(8,128)(2,1)} %collective-permute-done.7.k2o_ref, bf16[768,1024]{1,0:T(8,128)(2,1)} %collective-permute-done.6.k1_ref, ...), custom_call_target="tpu_custom_call" | custom-call | tf_op jit(solution)/shard_map/pallas_call | solution.py:131
  190.6 0.0 collective-permute-done.11
  190.6 0.8 collective-permute-done.12
  191.4 0.0 copy-done.4
  191.4 2.3 %maximum_select_fusion = bf16[384,2048]{1,0:T(8,128)(2,1)} fusion(bf16[384,512]{1,0:T(8,128)(2,1)S(1)} %collective-permute-done.12, bf16[384,512]{1,0:T(8,128)(2,1)S(1)} %collective-permute-done.11, bf16[384,384]{1,0:T(8,128)(2,1)} %shard_map.48, bf16[384,640]{1,0:T(8,128)(2,1)S(1)} %copy-done.4, pred[]{:T(512)S(6)} %eq.16), kind=kLoop, calls=%fused_computation.18 | loop fusion | flops 13369344 | bytes 3145729 | tf_op jit(solution)/shard_map/jit(_where)/select_n | solution.py:213
Async XLA Ops:
  3.4 43.0 %collective-permute-start.2 = (bf16[1024,896]{1,0:T(8,128)(2,1)S(1)}, bf16[1024,896]{1,0:T(8,128)(2,1)S(1)}, u32[]{:S(2)}, u32[]{:S(2)}) collective-permute-start(bf16[1024,896]{1,0:T(8,128)(2,1)S(1)} %slice.9), channel_id=1, source_target_pairs={{33,0},{32,1},{35,2},{34,3},{37,4},{36,5},{39,6},{38,7},{41,8},{40... | collective-permute-start | bytes 5505032 | tf_op jit(solution)/shard_map/ppermute | solution.py:166
  6.3 9.3 %collective-permute-start.1 = (bf16[1024,128]{1,0:T(8,128)(2,1)S(1)}, bf16[1024,128]{1,0:T(8,128)(2,1)S(1)}, u32[]{:S(2)}, u32[]{:S(2)}) collective-permute-start(bf16[1024,128]{1,0:T(8,128)(2,1)S(1)} %slice.8), channel_id=1, source_target_pairs={{0,1},{1,0},{2,3},{3,2},{4,5},{5,4},{6,7},{7,6},{8,9},{9,8},{10,11... | collective-permute-start | bytes 786440 | tf_op jit(solution)/shard_map/ppermute | solution.py:23
  6.6 43.1 %collective-permute-start = (bf16[384,2048]{1,0:T(8,128)(2,1)}, bf16[384,2048]{1,0:T(8,128)(2,1)}, u32[]{:S(2)}, u32[]{:S(2)}) collective-permute-start(bf16[384,2048]{1,0:T(8,128)(2,1)} %param.4), channel_id=1, source_target_pairs={{0,1},{1,0},{2,3},{3,2},{4,5},{5,4},{6,7},{7,6},{8,9},{9,8},{10,11... | collective-permute-start | bytes 4718600 | tf_op jit(solution)/shard_map/ppermute | solution.py:23
  46.7 5.2 %collective-permute-start.3 = (bf16[1024,1024]{1,0:T(8,128)(2,1)S(1)}, bf16[1024,1024]{1,0:T(8,128)(2,1)}, u32[]{:S(2)}, u32[]{:S(2)}) collective-permute-start(bf16[1024,1024]{1,0:T(8,128)(2,1)S(1)} %constant_dynamic-update-slice_fusion), channel_id=1, source_target_pairs={{0,2},{2,0},{4,6},{6,4},{8,10},{10,8},{12,14},{14,12},{16,18},{18,... | collective-permute-start | bytes 6291464 | tf_op jit(solution)/shard_map/ppermute | solution.py:169
  46.8 5.1 %copy-start.3 = (bf16[1024,2048]{1,0:T(8,128)(2,1)S(1)}, bf16[1024,2048]{1,0:T(8,128)(2,1)}, u32[]{:S(2)}) copy-start(bf16[1024,2048]{1,0:T(8,128)(2,1)} %param.6) | copy-start | bytes 12582916
  49.7 3.1 %copy-start.2 = (bf16[1024,2048]{1,0:T(8,128)(2,1)S(1)}, bf16[1024,2048]{1,0:T(8,128)(2,1)}, u32[]{:S(2)}) copy-start(bf16[1024,2048]{1,0:T(8,128)(2,1)} %param.7) | copy-start | bytes 12582916
  59.9 13.2 %copy-start = (bf16[768,1024]{1,0:T(8,128)(2,1)}, bf16[768,1024]{1,0:T(8,128)(2,1)S(1)}, u32[]{:S(2)}) copy-start(bf16[768,1024]{1,0:T(8,128)(2,1)S(1)} %fusion.8.v0_ref) | copy-start | bytes 4718596
  63.4 79.1 %copy-start.1 = (bf16[768,1024]{1,0:T(8,128)(2,1)}, bf16[768,1024]{1,0:T(8,128)(2,1)S(1)}, u32[]{:S(2)}) copy-start(bf16[768,1024]{1,0:T(8,128)(2,1)S(1)} %fusion.11.k0_ref) | copy-start | bytes 4718596
  63.4 39.0 %collective-permute-start.9 = (bf16[768,1024]{1,0:T(8,128)(2,1)S(1)}, bf16[768,1024]{1,0:T(8,128)(2,1)}, u32[]{:S(2)}, u32[]{:S(2)}) collective-permute-start(bf16[768,1024]{1,0:T(8,128)(2,1)S(1)} %fusion.8.v0_ref), channel_id=1, source_target_pairs={{0,2},{2,4},{4,6},{6,8},{8,10},{10,12},{12,14},{14,16},{16,18},{18... | collective-permute-start | bytes 4718600 | tf_op jit(solution)/shard_map/ppermute | solution.py:19
  65.8 70.4 %collective-permute-start.6 = (bf16[768,1024]{1,0:T(8,128)(2,1)S(1)}, bf16[768,1024]{1,0:T(8,128)(2,1)}, u32[]{:S(2)}, u32[]{:S(2)}) collective-permute-start(bf16[768,1024]{1,0:T(8,128)(2,1)S(1)} %fusion.11.k0_ref), channel_id=1, source_target_pairs={{0,2},{2,4},{4,6},{6,8},{8,10},{10,12},{12,14},{14,16},{16,18},{18... | collective-permute-start | bytes 4718600 | tf_op jit(solution)/shard_map/ppermute | solution.py:19
  69.3 73.2 %collective-permute-start.5 = (bf16[768,1024]{1,0:T(8,128)(2,1)S(1)}, bf16[768,1024]{1,0:T(8,128)(2,1)}, u32[]{:S(2)}, u32[]{:S(2)}) collective-permute-start(bf16[768,1024]{1,0:T(8,128)(2,1)S(1)} %fusion.11.k0_ref), channel_id=1, source_target_pairs={{0,4},{4,8},{8,12},{12,16},{16,20},{20,24},{24,28},{28,32},{32,36}... | collective-permute-start | bytes 4718600 | tf_op jit(solution)/shard_map/ppermute | solution.py:191
  73.1 69.4 %collective-permute-start.8 = (bf16[768,1024]{1,0:T(8,128)(2,1)S(1)}, bf16[768,1024]{1,0:T(8,128)(2,1)}, u32[]{:S(2)}, u32[]{:S(2)}) collective-permute-start(bf16[768,1024]{1,0:T(8,128)(2,1)S(1)} %fusion.8.v0_ref), channel_id=1, source_target_pairs={{0,4},{4,8},{8,12},{12,16},{16,20},{20,24},{24,28},{28,32},{32,36}... | collective-permute-start | bytes 4718600 | tf_op jit(solution)/shard_map/ppermute | solution.py:191
  102.4 40.1 %collective-permute-start.10 = (bf16[768,1024]{1,0:T(8,128)(2,1)}, bf16[768,1024]{1,0:T(8,128)(2,1)}, u32[]{:S(2)}, u32[]{:S(2)}) collective-permute-start(bf16[768,1024]{1,0:T(8,128)(2,1)} %collective-permute-done.9.v1_ref), channel_id=1, source_target_pairs={{0,2},{4,6},{8,10},{12,14},{16,18},{20,22},{24,26},{28,30},{32,34}... | collective-permute-start | bytes 4718600 | tf_op jit(solution)/shard_map/ppermute | solution.py:192
  136.1 6.3 %collective-permute-start.7 = (bf16[768,1024]{1,0:T(8,128)(2,1)}, bf16[768,1024]{1,0:T(8,128)(2,1)}, u32[]{:S(2)}, u32[]{:S(2)}) collective-permute-start(bf16[768,1024]{1,0:T(8,128)(2,1)} %collective-permute-done.6.k1_ref), channel_id=1, source_target_pairs={{0,2},{4,6},{8,10},{12,14},{16,18},{20,22},{24,26},{28,30},{32,34}... | collective-permute-start | bytes 4718600 | tf_op jit(solution)/shard_map/ppermute | solution.py:192
  138.6 18.0 %collective-permute-start.4 = (bf16[384,1024]{1,0:T(8,128)(2,1)}, bf16[384,1024]{1,0:T(8,128)(2,1)}, u32[]{:S(2)}, u32[]{:S(2)}) collective-permute-start(bf16[384,1024]{1,0:T(8,128)(2,1)} %get-tuple-element.11), channel_id=1, source_target_pairs={{0,1},{1,0},{2,3},{3,2},{4,5},{5,4},{6,7},{7,6},{8,9},{9,8},{10,11... | collective-permute-start | bytes 2359304 | tf_op jit(solution)/shard_map/ppermute | solution.py:23
  168.1 22.5 %collective-permute-start.11 = (bf16[384,512]{1,0:T(8,128)(2,1)}, bf16[384,512]{1,0:T(8,128)(2,1)S(1)}, u32[]{:S(2)}, u32[]{:S(2)}) collective-permute-start(bf16[384,512]{1,0:T(8,128)(2,1)} %shard_map.49), channel_id=1, source_target_pairs={{0,1},{1,0},{2,3},{3,2},{4,5},{5,4},{6,7},{7,6},{8,9},{9,8},{10,11... | collective-permute-start | bytes 1179656 | tf_op jit(solution)/shard_map/ppermute | solution.py:23
  181.1 10.3 %copy-start.4 = (bf16[384,640]{1,0:T(8,128)(2,1)S(1)}, bf16[384,640]{1,0:T(8,128)(2,1)}, u32[]{:S(2)}) copy-start(bf16[384,640]{1,0:T(8,128)(2,1)} %shard_map.46) | copy-start | bytes 1474564
  181.1 10.3 %collective-permute-start.12 = (bf16[384,512]{1,0:T(8,128)(2,1)}, bf16[384,512]{1,0:T(8,128)(2,1)S(1)}, u32[]{:S(2)}, u32[]{:S(2)}) collective-permute-start(bf16[384,512]{1,0:T(8,128)(2,1)} %shard_map.47), channel_id=1, source_target_pairs={{0,1},{1,0},{2,3},{3,2},{4,5},{5,4},{6,7},{7,6},{8,9},{9,8},{10,11... | collective-permute-start | bytes 1179656 | tf_op jit(solution)/shard_map/ppermute | solution.py:23

commit v11 on v10

--- a/solution.py
+++ b/solution.py
@@ -198,13 +198,14 @@
     values = (*value_two, value_one, own_value)
 
     heads = cols // HD
-    lead = heads - 3 * heads // 8
+    lead = heads - heads // 4
     mine_q = mine_of(queries)
     mine_lead = attend(seg_number, half_number * tok_rows, mine_q, keys, values, 0, lead)
     query_got, mine_lead = lax.optimization_barrier((query_got, mine_lead))
     got = []
-    for head_lo in range(0, heads, heads // 2):
-        their_rows = attend(seg_number, other_half * tok_rows, query_got, keys, values, head_lo, heads // 2)
+    split = heads - 3 * heads // 8
+    for head_lo, head_count in ((0, split), (split, heads - split)):
+        their_rows = attend(seg_number, other_half * tok_rows, query_got, keys, values, head_lo, head_count)
         got.append(swap_halves(their_rows))
     mine_q, their_rows = lax.optimization_barrier((mine_q, their_rows))
     mine_tail = attend(seg_number, half_number * tok_rows, mine_q, keys, values, lead, heads - lead)

time: 195 us -> 194 us (level)
  transfers between devices with their start and end apart: 13 -> 13, of which waited for: 6 -> 5; matrix products, arithmetic and copies ran while one was open for 3% -> 4% of each run, Pallas kernels for 18% -> 16%
where the time goes in v11:
time: 194 us
  waiting for transfers between devices  96 us (49%)
  Pallas kernels  45.6 us (24%)
  starting transfers between devices  28 us (14%)
  other arithmetic  12.7 us (7%)
  matrix products  6.85 us (4%)
  local copies, waits for them, and re-layouts  4.33 us (2%)
    ppermute x2, waiting for transfers between devices, from_behind(): lax.ppermute(value, axis, [(source, source + steps) for source in range(l...  56.7 us
    pallas_call x4, Pallas kernels, attend(): pl.pallas_call(attention_kernel, grid_spec=grid_spec, out_shape=jax.Shape...  45.6 us
    ppermute x1, waiting for transfers between devices, body(): right_got = lax.ppermute(served[:, piece:], ('seg', 'fsdp'), wrap_pairs)  30.8 us
    ppermute x5, waiting for transfers between devices, swap_halves(): return lax.ppermute(value, 'fsdp', [(0, 1), (1, 0)])  8.54 us
    ppermute x2, starting transfers between devices, shifted(): even_two = lax.ppermute(own, 'seg', even_pairs)  7.65 us
    ppermute x5, starting transfers between devices, swap_halves(): return lax.ppermute(value, 'fsdp', [(0, 1), (1, 0)])  6.59 us
    select_n x2, other arithmetic, in_order(): lead = jnp.where(first_is_mine, mine, other)  5.91 us
    ppermute x2, starting transfers between devices, from_behind(): lax.ppermute(value, axis, [(source, source + steps) for source in range(l...  5.85 us
  transfers between devices with their start and end apart: 13, of which 5 were waited for; matrix products, arithmetic and copies ran while one was open for 4% of the time, Pallas kernels for 16%

profile of v11, /device:TPU:24, one launch (start us, length us, event | category | flops | bytes accessed | tf_op | source)
XLA Modules:
  0.0 193.8 jit_solution(13382843107937399205)
XLA Ops:
  0.0 3.2 %dynamic-slice_select_fusion = bf16[1024,1024]{1,0:T(8,128)(2,1)S(1)} fusion(bf16[1024,2048]{1,0:T(8,128)(2,1)} %param.7, s32[]{:T(128)S(6)} %select_n.76, bf16[1024,2048]{1,0:T(8,128)(2,1)} %param.6, pred[]{:T(512)S(6)} %eq.17), kind=kLoop, calls=%fused_computation.9 | loop fusion | flops 1048576 | bytes 6291461 | tf_op jit(solution)/shard_map/jit(_where)/select_n | solution.py:159
  3.2 0.2 slice.9
  3.4 2.8 %collective-permute-start.2 = (bf16[1024,896]{1,0:T(8,128)(2,1)S(1)}, bf16[1024,896]{1,0:T(8,128)(2,1)S(1)}, u32[]{:S(2)}, u32[]{:S(2)}) collective-permute-start(bf16[1024,896]{1,0:T(8,128)(2,1)S(1)} %slice.9), channel_id=1, source_target_pairs={{33,0},{32,1},{35,2},{34,3},{37,4},{36,5},{39,6},{38,7},{41,8},{40... | collective-permute-start | bytes 5505032 | tf_op jit(solution)/shard_map/ppermute | solution.py:166
  6.2 0.1 slice.8
  6.3 0.3 collective-permute-start.1
  6.6 1.8 collective-permute-start
  8.4 7.1 %collective-permute-done.1 = bf16[1024,128]{1,0:T(8,128)(2,1)S(1)} collective-permute-done((bf16[1024,128]{1,0:T(8,128)(2,1)S(1)}, bf16[1024,128]{1,0:T(8,128)(2,1)S(1)}, u32[]{:S(2)}, u32[]{:S(2)}) %collective-permute-start.1) | collective-permute-done | bytes 262176 | tf_op jit(solution)/shard_map/ppermute | solution.py:23
  15.5 0.1 constant_dynamic-update-slice_fusion.1
  15.6 30.8 %collective-permute-done.2 = bf16[1024,896]{1,0:T(8,128)(2,1)S(1)} collective-permute-done((bf16[1024,896]{1,0:T(8,128)(2,1)S(1)}, bf16[1024,896]{1,0:T(8,128)(2,1)S(1)}, u32[]{:S(2)}, u32[]{:S(2)}) %collective-permute-start.2) | collective-permute-done | bytes 1835040 | tf_op jit(solution)/shard_map/ppermute | solution.py:166
  46.4 0.3 constant_dynamic-update-slice_fusion
  46.7 0.1 collective-permute-start.3
  46.8 0.0 copy-start.3
  46.9 2.8 %constant_dynamic-slice_fusion = (bf16[384,1024]{1,0:T(8,128)(2,1)}, bf16[384,1024]{1,0:T(8,128)(2,1)}) fusion(bf16[384,2048]{1,0:T(8,128)(2,1)} %param.5, s32[]{:T(128)S(6)} %select_n.80, s32[]{:T(128)S(6)} %select_n.76), kind=kLoop, calls=%fused_computation.23 | loop fusion | bytes 3145736 | tf_op jit(solution)/shard_map/dynamic_slice | solution.py:154
  49.7 0.0 copy-start.2
  49.7 0.0 collective-permute-done
  49.7 2.2 %broadcast_select_fusion.7 = (bf16[384,2048]{1,0:T(8,128)(2,1)S(1)}, bf16[384,2048]{1,0:T(8,128)(2,1)S(1)}) fusion(bf16[384,2048]{1,0:T(8,128)(2,1)} %param.4, bf16[384,2048]{1,0:T(8,128)(2,1)} %collective-permute-done, pred[]{:T(512)S(6)} %eq.16), kind=kLoop, calls=%fused_computation.20 | loop fusion | flops 1572864 | bytes 6291457 | tf_op jit(solution)/shard_map/jit(_where)/select_n | solution.py:27
  51.9 0.0 collective-permute-done.3
  51.9 0.0 copy-done.3
  52.0 0.9 copy-done.2
  52.8 3.7 %broadcast_select_fusion.3 = (bf16[1024,1024]{1,0:T(8,128)(2,1)S(1)}, bf16[1024,1024]{1,0:T(8,128)(2,1)S(1)}, bf16[1024,1024]{1,0:T(8,128)(2,1)S(1)}, bf16[1024,1024]{1,0:T(8,128)(2,1)S(1)}) fusion(pred[]{:T(512)S(6)} %eq.16, bf16[1024,2048]{1,0:T(8,128)(2,1)S(1)} %copy-done.2, s32[]{:T(128)S(6)} %select_n.80, bf16[1024,1024]{1,0:T(8,128)(2,1)} %collective-permute-done.3, ...), kind=kLoop, calls=%fused_computation.13 | loop fusion | flops 6291456 | bytes 16777222 | tf_op jit(solution)/shard_map/jit(_where)/select_n | solution.py:27
  56.5 3.4 %fusion.8.v0_ref = bf16[768,1024]{1,0:T(8,128)(2,1)S(1)} fusion(bf16[1024,1024]{1,0:T(8,128)(2,1)S(1)} %get-tuple-element.18, bf16[1024,1024]{1,0:T(8,128)(2,1)S(1)} %get-tuple-element.17, bf16[384,2048]{1,0:T(8,128)(2,1)S(1)} %get-tuple-element.24, bf16[384,2048]{1,0:T(8,128)(2,1)S(1)} %get-tuple-element.23), kind=kOutput, calls=%fused_computation.16 | convolution fusion | flops 3236691968 | bytes 8912896 | tf_op jit(solution)/shard_map/dot_general | solution.py:180
  59.9 0.0 copy-start
  59.9 3.4 %fusion.11.k0_ref = bf16[768,1024]{1,0:T(8,128)(2,1)S(1)} fusion(bf16[1024,1024]{1,0:T(8,128)(2,1)S(1)} %get-tuple-element.21, bf16[1024,1024]{1,0:T(8,128)(2,1)S(1)} %get-tuple-element.22, bf16[384,2048]{1,0:T(8,128)(2,1)S(1)} %get-tuple-element.24, bf16[384,2048]{1,0:T(8,128)(2,1)S(1)} %get-tuple-element.23), kind=kOutput, calls=%fused_computation.17 | convolution fusion | flops 3236691968 | bytes 8912896 | tf_op jit(solution)/shard_map/dot_general | solution.py:179
  63.4 0.0 copy-start.1
  63.4 2.4 %collective-permute-start.9 = (bf16[768,1024]{1,0:T(8,128)(2,1)S(1)}, bf16[768,1024]{1,0:T(8,128)(2,1)}, u32[]{:S(2)}, u32[]{:S(2)}) collective-permute-start(bf16[768,1024]{1,0:T(8,128)(2,1)S(1)} %fusion.8.v0_ref), channel_id=1, source_target_pairs={{0,2},{2,4},{4,6},{6,8},{8,10},{10,12},{12,14},{14,16},{16,18},{18... | collective-permute-start | bytes 4718600 | tf_op jit(solution)/shard_map/ppermute | solution.py:19
  65.8 3.5 %collective-permute-start.6 = (bf16[768,1024]{1,0:T(8,128)(2,1)S(1)}, bf16[768,1024]{1,0:T(8,128)(2,1)}, u32[]{:S(2)}, u32[]{:S(2)}) collective-permute-start(bf16[768,1024]{1,0:T(8,128)(2,1)S(1)} %fusion.11.k0_ref), channel_id=1, source_target_pairs={{0,2},{2,4},{4,6},{6,8},{8,10},{10,12},{12,14},{14,16},{16,18},{18... | collective-permute-start | bytes 4718600 | tf_op jit(solution)/shard_map/ppermute | solution.py:19
  69.3 3.8 %collective-permute-start.5 = (bf16[768,1024]{1,0:T(8,128)(2,1)S(1)}, bf16[768,1024]{1,0:T(8,128)(2,1)}, u32[]{:S(2)}, u32[]{:S(2)}) collective-permute-start(bf16[768,1024]{1,0:T(8,128)(2,1)S(1)} %fusion.11.k0_ref), channel_id=1, source_target_pairs={{0,4},{4,8},{8,12},{12,16},{16,20},{20,24},{24,28},{28,32},{32,36}... | collective-permute-start | bytes 4718600 | tf_op jit(solution)/shard_map/ppermute | solution.py:191
  73.1 0.0 copy-done
  73.1 3.8 %collective-permute-start.8 = (bf16[768,1024]{1,0:T(8,128)(2,1)S(1)}, bf16[768,1024]{1,0:T(8,128)(2,1)}, u32[]{:S(2)}, u32[]{:S(2)}) collective-permute-start(bf16[768,1024]{1,0:T(8,128)(2,1)S(1)} %fusion.8.v0_ref), channel_id=1, source_target_pairs={{0,4},{4,8},{8,12},{12,16},{16,20},{20,24},{24,28},{28,32},{32,36}... | collective-permute-start | bytes 4718600 | tf_op jit(solution)/shard_map/ppermute | solution.py:191
  76.9 25.5 %collective-permute-done.9.v1_ref = bf16[768,1024]{1,0:T(8,128)(2,1)} collective-permute-done((bf16[768,1024]{1,0:T(8,128)(2,1)S(1)}, bf16[768,1024]{1,0:T(8,128)(2,1)}, u32[]{:S(2)}, u32[]{:S(2)}) %collective-permute-start.9) | collective-permute-done | bytes 1572896 | tf_op jit(solution)/shard_map/ppermute | solution.py:19
  102.4 2.5 %collective-permute-start.10 = (bf16[768,1024]{1,0:T(8,128)(2,1)}, bf16[768,1024]{1,0:T(8,128)(2,1)}, u32[]{:S(2)}, u32[]{:S(2)}) collective-permute-start(bf16[768,1024]{1,0:T(8,128)(2,1)} %collective-permute-done.9.v1_ref), channel_id=1, source_target_pairs={{0,2},{4,6},{8,10},{12,14},{16,18},{20,22},{24,26},{28,30},{32,34}... | collective-permute-start | bytes 4718600 | tf_op jit(solution)/shard_map/ppermute | solution.py:192
  104.9 31.2 %collective-permute-done.6.k1_ref = bf16[768,1024]{1,0:T(8,128)(2,1)} collective-permute-done((bf16[768,1024]{1,0:T(8,128)(2,1)S(1)}, bf16[768,1024]{1,0:T(8,128)(2,1)}, u32[]{:S(2)}, u32[]{:S(2)}) %collective-permute-start.6) | collective-permute-done | bytes 1572896 | tf_op jit(solution)/shard_map/ppermute | solution.py:19
  136.1 2.4 %collective-permute-start.7 = (bf16[768,1024]{1,0:T(8,128)(2,1)}, bf16[768,1024]{1,0:T(8,128)(2,1)}, u32[]{:S(2)}, u32[]{:S(2)}) collective-permute-start(bf16[768,1024]{1,0:T(8,128)(2,1)} %collective-permute-done.6.k1_ref), channel_id=1, source_target_pairs={{0,2},{4,6},{8,10},{12,14},{16,18},{20,22},{24,26},{28,30},{32,34}... | collective-permute-start | bytes 4718600 | tf_op jit(solution)/shard_map/ppermute | solution.py:192
  138.6 2.6 %collective-permute-start.4 = (bf16[384,1024]{1,0:T(8,128)(2,1)}, bf16[384,1024]{1,0:T(8,128)(2,1)}, u32[]{:S(2)}, u32[]{:S(2)}) collective-permute-start(bf16[384,1024]{1,0:T(8,128)(2,1)} %get-tuple-element.11), channel_id=1, source_target_pairs={{0,1},{1,0},{2,3},{3,2},{4,5},{5,4},{6,7},{7,6},{8,9},{9,8},{10,11... | collective-permute-start | bytes 2359304 | tf_op jit(solution)/shard_map/ppermute | solution.py:23
  141.2 0.7 add_add_fusion.seg_ref
  141.9 0.7 add_add_fusion.1.seg_ref
  142.5 0.0 collective-permute-done.5.k2e_ref
  142.5 0.0 collective-permute-done.8.v2e_ref
  142.5 0.0 collective-permute-done.10.v2o_ref
  142.5 0.0 collective-permute-done.7.k2o_ref
  142.5 0.0 copy-done.1
  142.6 15.5 %shard_map.46 = bf16[384,768]{1,0:T(8,128)(2,1)} custom-call(s32[3]{0:T(128)} %add_add_fusion.seg_ref, bf16[384,1024]{1,0:T(8,128)(2,1)} %get-tuple-element.16.q_ref, bf16[768,1024]{1,0:T(8,128)(2,1)} %collective-permute-done.5.k2e_ref, bf16[768,1024]{1,0:T(8,128)(2,1)} %collective-permute-done.7.k2o_ref, bf16[768,1024]{1,0:T(8,128)(2,1)} %collective-permute-done.6.k1_ref, ...), custom_call_target="tpu_custom_call" | custom-call | tf_op jit(solution)/shard_map/pallas_call | solution.py:131
  158.0 0.0 collective-permute-done.4.q_ref
  158.0 13.8 %shard_map.49 = bf16[384,640]{1,0:T(8,128)(2,1)} custom-call(s32[3]{0:T(128)} %add_add_fusion.1.seg_ref, bf16[384,1024]{1,0:T(8,128)(2,1)} %collective-permute-done.4.q_ref, bf16[768,1024]{1,0:T(8,128)(2,1)} %collective-permute-done.5.k2e_ref, bf16[768,1024]{1,0:T(8,128)(2,1)} %collective-permute-done.7.k2o_ref, ...), custom_call_target="tpu_custom_call" | custom-call | tf_op jit(solution)/shard_map/pallas_call | solution.py:131
  171.8 0.9 collective-permute-start.11
  172.7 9.4 %shard_map.47 = bf16[384,384]{1,0:T(8,128)(2,1)} custom-call(s32[3]{0:T(128)} %add_add_fusion.1.seg_ref, bf16[384,1024]{1,0:T(8,128)(2,1)} %collective-permute-done.4.q_ref, bf16[768,1024]{1,0:T(8,128)(2,1)} %collective-permute-done.5.k2e_ref, bf16[768,1024]{1,0:T(8,128)(2,1)} %collective-permute-done.7.k2o_ref, ...), custom_call_target="tpu_custom_call" | custom-call | tf_op jit(solution)/shard_map/pallas_call | solution.py:131
  182.1 0.0 copy-start.4
  182.1 0.9 collective-permute-start.12
  183.0 7.0 %shard_map.48 = bf16[384,256]{1,0:T(8,128)(2,1)} custom-call(s32[3]{0:T(128)} %add_add_fusion.seg_ref, bf16[384,1024]{1,0:T(8,128)(2,1)} %get-tuple-element.16.q_ref, bf16[768,1024]{1,0:T(8,128)(2,1)} %collective-permute-done.5.k2e_ref, bf16[768,1024]{1,0:T(8,128)(2,1)} %collective-permute-done.7.k2o_ref, bf16[768,1024]{1,0:T(8,128)(2,1)} %collective-permute-done.6.k1_ref, ...), custom_call_target="tpu_custom_call" | custom-call | tf_op jit(solution)/shard_map/pallas_call | solution.py:131
  190.1 1.4 collective-permute-done.12
  191.4 0.0 collective-permute-done.11
  191.4 0.0 copy-done.4
  191.4 2.3 %maximum_select_fusion = bf16[384,2048]{1,0:T(8,128)(2,1)} fusion(bf16[384,384]{1,0:T(8,128)(2,1)S(1)} %collective-permute-done.12, bf16[384,640]{1,0:T(8,128)(2,1)S(1)} %collective-permute-done.11, bf16[384,256]{1,0:T(8,128)(2,1)} %shard_map.48, bf16[384,768]{1,0:T(8,128)(2,1)S(1)} %copy-done.4, pred[]{:T(512)S(6)} %eq.16), kind=kLoop, calls=%fused_computation.18 | loop fusion | flops 13369344 | bytes 3145729 | tf_op jit(solution)/shard_map/jit(_where)/select_n | solution.py:214
Async XLA Ops:
  3.4 43.0 %collective-permute-start.2 = (bf16[1024,896]{1,0:T(8,128)(2,1)S(1)}, bf16[1024,896]{1,0:T(8,128)(2,1)S(1)}, u32[]{:S(2)}, u32[]{:S(2)}) collective-permute-start(bf16[1024,896]{1,0:T(8,128)(2,1)S(1)} %slice.9), channel_id=1, source_target_pairs={{33,0},{32,1},{35,2},{34,3},{37,4},{36,5},{39,6},{38,7},{41,8},{40... | collective-permute-start | bytes 5505032 | tf_op jit(solution)/shard_map/ppermute | solution.py:166
  6.3 9.3 %collective-permute-start.1 = (bf16[1024,128]{1,0:T(8,128)(2,1)S(1)}, bf16[1024,128]{1,0:T(8,128)(2,1)S(1)}, u32[]{:S(2)}, u32[]{:S(2)}) collective-permute-start(bf16[1024,128]{1,0:T(8,128)(2,1)S(1)} %slice.8), channel_id=1, source_target_pairs={{0,1},{1,0},{2,3},{3,2},{4,5},{5,4},{6,7},{7,6},{8,9},{9,8},{10,11... | collective-permute-start | bytes 786440 | tf_op jit(solution)/shard_map/ppermute | solution.py:23
  6.6 43.1 %collective-permute-start = (bf16[384,2048]{1,0:T(8,128)(2,1)}, bf16[384,2048]{1,0:T(8,128)(2,1)}, u32[]{:S(2)}, u32[]{:S(2)}) collective-permute-start(bf16[384,2048]{1,0:T(8,128)(2,1)} %param.4), channel_id=1, source_target_pairs={{0,1},{1,0},{2,3},{3,2},{4,5},{5,4},{6,7},{7,6},{8,9},{9,8},{10,11... | collective-permute-start | bytes 4718600 | tf_op jit(solution)/shard_map/ppermute | solution.py:23
  46.7 5.2 %collective-permute-start.3 = (bf16[1024,1024]{1,0:T(8,128)(2,1)S(1)}, bf16[1024,1024]{1,0:T(8,128)(2,1)}, u32[]{:S(2)}, u32[]{:S(2)}) collective-permute-start(bf16[1024,1024]{1,0:T(8,128)(2,1)S(1)} %constant_dynamic-update-slice_fusion), channel_id=1, source_target_pairs={{0,2},{2,0},{4,6},{6,4},{8,10},{10,8},{12,14},{14,12},{16,18},{18,... | collective-permute-start | bytes 6291464 | tf_op jit(solution)/shard_map/ppermute | solution.py:169
  46.8 5.1 %copy-start.3 = (bf16[1024,2048]{1,0:T(8,128)(2,1)S(1)}, bf16[1024,2048]{1,0:T(8,128)(2,1)}, u32[]{:S(2)}) copy-start(bf16[1024,2048]{1,0:T(8,128)(2,1)} %param.6) | copy-start | bytes 12582916
  49.7 3.1 %copy-start.2 = (bf16[1024,2048]{1,0:T(8,128)(2,1)S(1)}, bf16[1024,2048]{1,0:T(8,128)(2,1)}, u32[]{:S(2)}) copy-start(bf16[1024,2048]{1,0:T(8,128)(2,1)} %param.7) | copy-start | bytes 12582916
  59.9 13.2 %copy-start = (bf16[768,1024]{1,0:T(8,128)(2,1)}, bf16[768,1024]{1,0:T(8,128)(2,1)S(1)}, u32[]{:S(2)}) copy-start(bf16[768,1024]{1,0:T(8,128)(2,1)S(1)} %fusion.8.v0_ref) | copy-start | bytes 4718596
  63.4 79.2 %copy-start.1 = (bf16[768,1024]{1,0:T(8,128)(2,1)}, bf16[768,1024]{1,0:T(8,128)(2,1)S(1)}, u32[]{:S(2)}) copy-start(bf16[768,1024]{1,0:T(8,128)(2,1)S(1)} %fusion.11.k0_ref) | copy-start | bytes 4718596
  63.4 39.0 %collective-permute-start.9 = (bf16[768,1024]{1,0:T(8,128)(2,1)S(1)}, bf16[768,1024]{1,0:T(8,128)(2,1)}, u32[]{:S(2)}, u32[]{:S(2)}) collective-permute-start(bf16[768,1024]{1,0:T(8,128)(2,1)S(1)} %fusion.8.v0_ref), channel_id=1, source_target_pairs={{0,2},{2,4},{4,6},{6,8},{8,10},{10,12},{12,14},{14,16},{16,18},{18... | collective-permute-start | bytes 4718600 | tf_op jit(solution)/shard_map/ppermute | solution.py:19
  65.8 70.4 %collective-permute-start.6 = (bf16[768,1024]{1,0:T(8,128)(2,1)S(1)}, bf16[768,1024]{1,0:T(8,128)(2,1)}, u32[]{:S(2)}, u32[]{:S(2)}) collective-permute-start(bf16[768,1024]{1,0:T(8,128)(2,1)S(1)} %fusion.11.k0_ref), channel_id=1, source_target_pairs={{0,2},{2,4},{4,6},{6,8},{8,10},{10,12},{12,14},{14,16},{16,18},{18... | collective-permute-start | bytes 4718600 | tf_op jit(solution)/shard_map/ppermute | solution.py:19
  69.3 73.3 %collective-permute-start.5 = (bf16[768,1024]{1,0:T(8,128)(2,1)S(1)}, bf16[768,1024]{1,0:T(8,128)(2,1)}, u32[]{:S(2)}, u32[]{:S(2)}) collective-permute-start(bf16[768,1024]{1,0:T(8,128)(2,1)S(1)} %fusion.11.k0_ref), channel_id=1, source_target_pairs={{0,4},{4,8},{8,12},{12,16},{16,20},{20,24},{24,28},{28,32},{32,36}... | collective-permute-start | bytes 4718600 | tf_op jit(solution)/shard_map/ppermute | solution.py:191
  73.1 69.4 %collective-permute-start.8 = (bf16[768,1024]{1,0:T(8,128)(2,1)S(1)}, bf16[768,1024]{1,0:T(8,128)(2,1)}, u32[]{:S(2)}, u32[]{:S(2)}) collective-permute-start(bf16[768,1024]{1,0:T(8,128)(2,1)S(1)} %fusion.8.v0_ref), channel_id=1, source_target_pairs={{0,4},{4,8},{8,12},{12,16},{16,20},{20,24},{24,28},{28,32},{32,36}... | collective-permute-start | bytes 4718600 | tf_op jit(solution)/shard_map/ppermute | solution.py:191
  102.4 40.1 %collective-permute-start.10 = (bf16[768,1024]{1,0:T(8,128)(2,1)}, bf16[768,1024]{1,0:T(8,128)(2,1)}, u32[]{:S(2)}, u32[]{:S(2)}) collective-permute-start(bf16[768,1024]{1,0:T(8,128)(2,1)} %collective-permute-done.9.v1_ref), channel_id=1, source_target_pairs={{0,2},{4,6},{8,10},{12,14},{16,18},{20,22},{24,26},{28,30},{32,34}... | collective-permute-start | bytes 4718600 | tf_op jit(solution)/shard_map/ppermute | solution.py:192
  136.1 6.4 %collective-permute-start.7 = (bf16[768,1024]{1,0:T(8,128)(2,1)}, bf16[768,1024]{1,0:T(8,128)(2,1)}, u32[]{:S(2)}, u32[]{:S(2)}) collective-permute-start(bf16[768,1024]{1,0:T(8,128)(2,1)} %collective-permute-done.6.k1_ref), channel_id=1, source_target_pairs={{0,2},{4,6},{8,10},{12,14},{16,18},{20,22},{24,26},{28,30},{32,34}... | collective-permute-start | bytes 4718600 | tf_op jit(solution)/shard_map/ppermute | solution.py:192
  138.6 19.4 %collective-permute-start.4 = (bf16[384,1024]{1,0:T(8,128)(2,1)}, bf16[384,1024]{1,0:T(8,128)(2,1)}, u32[]{:S(2)}, u32[]{:S(2)}) collective-permute-start(bf16[384,1024]{1,0:T(8,128)(2,1)} %get-tuple-element.11), channel_id=1, source_target_pairs={{0,1},{1,0},{2,3},{3,2},{4,5},{5,4},{6,7},{7,6},{8,9},{9,8},{10,11... | collective-permute-start | bytes 2359304 | tf_op jit(solution)/shard_map/ppermute | solution.py:23
  171.8 19.6 %collective-permute-start.11 = (bf16[384,640]{1,0:T(8,128)(2,1)}, bf16[384,640]{1,0:T(8,128)(2,1)S(1)}, u32[]{:S(2)}, u32[]{:S(2)}) collective-permute-start(bf16[384,640]{1,0:T(8,128)(2,1)} %shard_map.49), channel_id=1, source_target_pairs={{0,1},{1,0},{2,3},{3,2},{4,5},{5,4},{6,7},{7,6},{8,9},{9,8},{10,11... | collective-permute-start | bytes 1474568 | tf_op jit(solution)/shard_map/ppermute | solution.py:23
  182.1 9.3 %copy-start.4 = (bf16[384,768]{1,0:T(8,128)(2,1)S(1)}, bf16[384,768]{1,0:T(8,128)(2,1)}, u32[]{:S(2)}) copy-start(bf16[384,768]{1,0:T(8,128)(2,1)} %shard_map.46) | copy-start | bytes 1769476
  182.1 9.3 %collective-permute-start.12 = (bf16[384,384]{1,0:T(8,128)(2,1)}, bf16[384,384]{1,0:T(8,128)(2,1)S(1)}, u32[]{:S(2)}, u32[]{:S(2)}) collective-permute-start(bf16[384,384]{1,0:T(8,128)(2,1)} %shard_map.47), channel_id=1, source_target_pairs={{0,1},{1,0},{2,3},{3,2},{4,5},{5,4},{6,7},{7,6},{8,9},{9,8},{10,11... | collective-permute-start | bytes 884744 | tf_op jit(solution)/shard_map/ppermute | solution.py:23

commit v12 on v11

--- a/solution.py
+++ b/solution.py
@@ -172,14 +172,17 @@
 
     hidden_got = swap_halves(hidden_states)
 
-    key_weights = in_order(first_is_mine, mine_of(w_key), key_got, 0)
-    value_weights = in_order(first_is_mine, mine_of(w_value), value_got, 0)
     hidden_rows = in_order(first_is_mine, hidden_states, hidden_got, 0)
-
-    own_key = jnp.dot(hidden_rows, key_weights, preferred_element_type=jnp.float32).astype(jnp.bfloat16)
-    own_value = jnp.dot(hidden_rows, value_weights, preferred_element_type=jnp.float32).astype(
-        jnp.bfloat16
-    )
+    channels = w_key.shape[0]
+    hidden_rows = jnp.where(first_is_mine, hidden_rows, jnp.roll(hidden_rows, -channels, axis=1))
+
+    def project(local, got):
+        own = jnp.dot(hidden_rows[:, :channels], mine_of(local), preferred_element_type=jnp.float32)
+        own = own + jnp.dot(hidden_rows[:, channels:], got, preferred_element_type=jnp.float32)
+        return own.astype(jnp.bfloat16)
+
+    own_key = project(w_key, key_got)
+    own_value = project(w_value, value_got)
     query_sent, own_key, own_value = lax.optimization_barrier((theirs_of(queries), own_key, own_value))
     query_got = swap_halves(query_sent)
 

time: 194 us -> 198 us (1.021)
  matrix products: 6.85 us -> 11.1 us
    ppermute x5, waiting for transfers between devices: 8.54 us -> 40.1 us  [swap_halves(): return lax.ppermute(value, 'fsdp', [(0, 1), (1, 0)])]
    ppermute x1, waiting for transfers between devices: 30.8 us -> 0.01 us  [body(): right_got = lax.ppermute(served[:, piece:], ('seg', 'fsdp'), wrap_pairs)]
    dot_general x2 -> x4, matrix products: 6.85 us -> 11.1 us  [the longest x2 7.55 us: project(): jnp.dot(hidden_rows[:, channels:], got, preferred_element_type=jnp.float32)]
    select_n x2 -> x1, other arithmetic: 5.91 us -> 1.61 us  [in_order(): lead = jnp.where(first_is_mine, mine, other)]
    select_n x0 -> x1, other arithmetic: none -> 3.79 us  [body(): jnp.where(first_is_mine, hidden_rows, jnp.roll(hidden_rows, -channels, ax...]
  transfers between devices with their start and end apart: 13 -> 13, of which waited for: 5 -> 5; matrix products, arithmetic and copies ran while one was open for 4% -> 5% of each run, Pallas kernels for 16% -> 16%
where the time goes in v12:
time: 198 us; the launch traced here: 197 us
  waiting for transfers between devices  97.4 us (49%)
  Pallas kernels  45.6 us (23%)
  starting transfers between devices  26.3 us (13%)
  other arithmetic  12.6 us (6%)
  matrix products  11.1 us (6%)
  local copies, waits for them, and re-layouts  3.77 us (2%)
    ppermute x2, waiting for transfers between devices, from_behind(): lax.ppermute(value, axis, [(source, source + steps) for source in range(l...  56.2 us
    pallas_call x4, Pallas kernels, attend(): pl.pallas_call(attention_kernel, grid_spec=grid_spec, out_shape=jax.Shape...  45.6 us
    ppermute x5, waiting for transfers between devices, swap_halves(): return lax.ppermute(value, 'fsdp', [(0, 1), (1, 0)])  40.1 us
    ppermute x2, starting transfers between devices, shifted(): even_two = lax.ppermute(own, 'seg', even_pairs)  7.66 us
    dot_general x2, matrix products, project(): jnp.dot(hidden_rows[:, channels:], got, preferred_element_type=jnp.float32)  7.55 us
    ppermute x2, starting transfers between devices, from_behind(): lax.ppermute(value, axis, [(source, source + steps) for source in range(l...  6.03 us
    ppermute x2, starting transfers between devices, shifted(): odd_two = lax.ppermute(one, 'seg', forward_pairs)  4.89 us
    ppermute x5, starting transfers between devices, swap_halves(): return lax.ppermute(value, 'fsdp', [(0, 1), (1, 0)])  4.85 us
  transfers between devices with their start and end apart: 13, of which 5 were waited for; matrix products, arithmetic and copies ran while one was open for 5% of the time, Pallas kernels for 16%

profile of v12, /device:TPU:24, one launch (start us, length us, event | category | flops | bytes accessed | tf_op | source)
XLA Modules:
  0.0 197.0 jit_solution(10070798824113358485)
XLA Ops:
  0.0 3.2 %dynamic-slice_select_fusion = bf16[1024,1024]{1,0:T(8,128)(2,1)S(1)} fusion(bf16[1024,2048]{1,0:T(8,128)(2,1)} %param.7, s32[]{:T(128)S(6)} %select_n.66, bf16[1024,2048]{1,0:T(8,128)(2,1)} %param.6, pred[]{:T(512)S(6)} %eq.17), kind=kLoop, calls=%fused_computation.14 | loop fusion | flops 1048576 | bytes 6291461 | tf_op jit(solution)/shard_map/jit(_where)/select_n | solution.py:159
  3.2 0.0 copy-start.4
  3.2 0.2 slice.35
  3.4 2.8 %collective-permute-start.2 = (bf16[1024,896]{1,0:T(8,128)(2,1)S(1)}, bf16[1024,896]{1,0:T(8,128)(2,1)S(1)}, u32[]{:S(2)}, u32[]{:S(2)}) collective-permute-start(bf16[1024,896]{1,0:T(8,128)(2,1)S(1)} %slice.35), channel_id=1, source_target_pairs={{33,0},{32,1},{35,2},{34,3},{37,4},{36,5},{39,6},{38,7},{41,8},{40... | collective-permute-start | bytes 5505032 | tf_op jit(solution)/shard_map/ppermute | solution.py:166
  6.2 0.0 copy-done.4
  6.2 0.2 collective-permute-start
  6.5 0.1 slice.34
  6.5 0.0 copy-start.3
  6.5 1.9 collective-permute-start.1
  8.4 39.3 %collective-permute-done.1 = bf16[1024,128]{1,0:T(8,128)(2,1)S(1)} collective-permute-done((bf16[1024,128]{1,0:T(8,128)(2,1)S(1)}, bf16[1024,128]{1,0:T(8,128)(2,1)S(1)}, u32[]{:S(2)}, u32[]{:S(2)}) %collective-permute-start.1) | collective-permute-done | bytes 262176 | tf_op jit(solution)/shard_map/ppermute | solution.py:23
  47.7 0.7 constant_dynamic-update-slice_fusion.1
  48.4 0.0 collective-permute-done.2
  48.4 1.4 constant_dynamic-update-slice_fusion
  49.8 0.0 collective-permute-start.3
  49.8 0.0 copy-done.3
  49.8 1.3 constant_dynamic-slice_fusion
  51.2 0.0 collective-permute-done
  51.2 1.6 broadcast_select_fusion.1
  52.8 0.5 fusion.11
  53.3 3.8 %fusion = bf16[768,2048]{1,0:T(8,128)(2,1)S(1)} fusion(bf16[384,2048]{1,0:T(8,128)(2,1)S(1)} %get-tuple-element.20, bf16[384,2048]{1,0:T(8,128)(2,1)S(1)} %get-tuple-element.19, bf16[768,1024]{1,0:T(8,128)(2,1)S(1)} %get-tuple-element.18, bf16[768,1024]{1,0:T(8,128)(2,1)S(1)} %get-tuple-element.17, pred[]{:T(512)S(6)} %eq.16), kind=kLoop, calls=%fused_computation.5 | loop fusion | flops 14155776 | bytes 9437185 | tf_op jit(solution)/shard_map/jit(_where)/select_n | solution.py:177
  57.1 0.0 copy-start.5
  57.1 0.0 collective-permute-done.3
  57.1 3.6 %fusion.1 = f32[768,1024]{1,0:T(8,128)S(1)} fusion(bf16[1024,1024]{1,0:T(8,128)(2,1)} %collective-permute-done.3, bf16[1024,1024]{1,0:T(8,128)(2,1)} %constant_dynamic-update-slice_fusion, pred[]{:T(512)S(6)} %eq.17, bf16[768,2048]{1,0:T(8,128)(2,1)S(1)} %fusion), kind=kOutput, calls=%fused_computation.8 | convolution fusion | flops 1611661312 | bytes 8912897 | tf_op jit(solution)/shard_map/dot_general | solution.py:181
  60.7 0.0 copy-done.5
  60.7 1.8 add_convert_fusion.v0_ref
  62.5 0.0 copy-start
  62.5 0.0 copy-start.6
  62.5 4.0 %fusion.5 = f32[768,1024]{1,0:T(8,128)S(1)} fusion(bf16[1024,1024]{1,0:T(8,128)(2,1)} %constant_dynamic-update-slice_fusion, bf16[1024,1024]{1,0:T(8,128)(2,1)} %collective-permute-done.3, pred[]{:T(512)S(6)} %eq.17, bf16[768,2048]{1,0:T(8,128)(2,1)S(1)} %fusion), kind=kOutput, calls=%fused_computation.12 | convolution fusion | flops 1611661312 | bytes 8912897 | tf_op jit(solution)/shard_map/dot_general | solution.py:181
  66.5 0.0 copy-done.6
  66.5 1.8 add_convert_fusion.1.k0_ref
  68.3 0.0 copy-start.1
  68.3 2.6 %collective-permute-start.6 = (bf16[768,1024]{1,0:T(8,128)(2,1)S(1)}, bf16[768,1024]{1,0:T(8,128)(2,1)}, u32[]{:S(2)}, u32[]{:S(2)}) collective-permute-start(bf16[768,1024]{1,0:T(8,128)(2,1)S(1)} %add_convert_fusion.1.k0_ref), channel_id=1, source_target_pairs={{0,2},{2,4},{4,6},{6,8},{8,10},{10,12},{12,14},{14,16},{16,18},{18... | collective-permute-start | bytes 4718600 | tf_op jit(solution)/shard_map/ppermute | solution.py:19
  70.9 3.4 %collective-permute-start.9 = (bf16[768,1024]{1,0:T(8,128)(2,1)S(1)}, bf16[768,1024]{1,0:T(8,128)(2,1)}, u32[]{:S(2)}, u32[]{:S(2)}) collective-permute-start(bf16[768,1024]{1,0:T(8,128)(2,1)S(1)} %add_convert_fusion.v0_ref), channel_id=1, source_target_pairs={{0,2},{2,4},{4,6},{6,8},{8,10},{10,12},{12,14},{14,16},{16,18},{18... | collective-permute-start | bytes 4718600 | tf_op jit(solution)/shard_map/ppermute | solution.py:19
  74.4 3.8 %collective-permute-start.5 = (bf16[768,1024]{1,0:T(8,128)(2,1)S(1)}, bf16[768,1024]{1,0:T(8,128)(2,1)}, u32[]{:S(2)}, u32[]{:S(2)}) collective-permute-start(bf16[768,1024]{1,0:T(8,128)(2,1)S(1)} %add_convert_fusion.1.k0_ref), channel_id=1, source_target_pairs={{0,4},{4,8},{8,12},{12,16},{16,20},{20,24},{24,28},{28,32},{32,36}... | collective-permute-start | bytes 4718600 | tf_op jit(solution)/shard_map/ppermute | solution.py:194
  78.2 0.0 copy-done
  78.2 3.8 %collective-permute-start.8 = (bf16[768,1024]{1,0:T(8,128)(2,1)S(1)}, bf16[768,1024]{1,0:T(8,128)(2,1)}, u32[]{:S(2)}, u32[]{:S(2)}) collective-permute-start(bf16[768,1024]{1,0:T(8,128)(2,1)S(1)} %add_convert_fusion.v0_ref), channel_id=1, source_target_pairs={{0,4},{4,8},{8,12},{12,16},{16,20},{20,24},{24,28},{28,32},{32,36}... | collective-permute-start | bytes 4718600 | tf_op jit(solution)/shard_map/ppermute | solution.py:194
  82.1 24.9 %collective-permute-done.6.k1_ref = bf16[768,1024]{1,0:T(8,128)(2,1)} collective-permute-done((bf16[768,1024]{1,0:T(8,128)(2,1)S(1)}, bf16[768,1024]{1,0:T(8,128)(2,1)}, u32[]{:S(2)}, u32[]{:S(2)}) %collective-permute-start.6) | collective-permute-done | bytes 1572896 | tf_op jit(solution)/shard_map/ppermute | solution.py:19
  107.0 2.5 %collective-permute-start.7 = (bf16[768,1024]{1,0:T(8,128)(2,1)}, bf16[768,1024]{1,0:T(8,128)(2,1)}, u32[]{:S(2)}, u32[]{:S(2)}) collective-permute-start(bf16[768,1024]{1,0:T(8,128)(2,1)} %collective-permute-done.6.k1_ref), channel_id=1, source_target_pairs={{0,2},{4,6},{8,10},{12,14},{16,18},{20,22},{24,26},{28,30},{32,34}... | collective-permute-start | bytes 4718600 | tf_op jit(solution)/shard_map/ppermute | solution.py:195
  109.4 31.3 %collective-permute-done.9.v1_ref = bf16[768,1024]{1,0:T(8,128)(2,1)} collective-permute-done((bf16[768,1024]{1,0:T(8,128)(2,1)S(1)}, bf16[768,1024]{1,0:T(8,128)(2,1)}, u32[]{:S(2)}, u32[]{:S(2)}) %collective-permute-start.9) | collective-permute-done | bytes 1572896 | tf_op jit(solution)/shard_map/ppermute | solution.py:19
  140.8 2.4 %collective-permute-start.10 = (bf16[768,1024]{1,0:T(8,128)(2,1)}, bf16[768,1024]{1,0:T(8,128)(2,1)}, u32[]{:S(2)}, u32[]{:S(2)}) collective-permute-start(bf16[768,1024]{1,0:T(8,128)(2,1)} %collective-permute-done.9.v1_ref), channel_id=1, source_target_pairs={{0,2},{4,6},{8,10},{12,14},{16,18},{20,22},{24,26},{28,30},{32,34}... | collective-permute-start | bytes 4718600 | tf_op jit(solution)/shard_map/ppermute | solution.py:195
  143.2 0.9 collective-permute-start.4
  144.1 0.6 add_add_fusion.1.seg_ref
  144.7 0.6 add_add_fusion.seg_ref
  145.3 0.0 collective-permute-done.5.k2e_ref
  145.3 1.0 collective-permute-done.8.v2e_ref
  146.4 0.0 collective-permute-done.7.k2o_ref
  146.4 0.0 collective-permute-done.10.v2o_ref
  146.4 0.0 copy-done.1
  146.4 15.5 %shard_map.46 = bf16[384,768]{1,0:T(8,128)(2,1)} custom-call(s32[3]{0:T(128)} %add_add_fusion.seg_ref, bf16[384,1024]{1,0:T(8,128)(2,1)} %get-tuple-element.16.q_ref, bf16[768,1024]{1,0:T(8,128)(2,1)} %collective-permute-done.5.k2e_ref, bf16[768,1024]{1,0:T(8,128)(2,1)} %collective-permute-done.7.k2o_ref, bf16[768,1024]{1,0:T(8,128)(2,1)} %collective-permute-done.6.k1_ref, ...), custom_call_target="tpu_custom_call" | custom-call | tf_op jit(solution)/shard_map/pallas_call | solution.py:131
  161.8 0.0 collective-permute-done.4.q_ref
  161.8 13.8 %shard_map.49 = bf16[384,640]{1,0:T(8,128)(2,1)} custom-call(s32[3]{0:T(128)} %add_add_fusion.1.seg_ref, bf16[384,1024]{1,0:T(8,128)(2,1)} %collective-permute-done.4.q_ref, bf16[768,1024]{1,0:T(8,128)(2,1)} %collective-permute-done.5.k2e_ref, bf16[768,1024]{1,0:T(8,128)(2,1)} %collective-permute-done.7.k2o_ref, ...), custom_call_target="tpu_custom_call" | custom-call | tf_op jit(solution)/shard_map/pallas_call | solution.py:131
  175.6 1.0 collective-permute-start.11
  176.6 9.4 %shard_map.47 = bf16[384,384]{1,0:T(8,128)(2,1)} custom-call(s32[3]{0:T(128)} %add_add_fusion.1.seg_ref, bf16[384,1024]{1,0:T(8,128)(2,1)} %collective-permute-done.4.q_ref, bf16[768,1024]{1,0:T(8,128)(2,1)} %collective-permute-done.5.k2e_ref, bf16[768,1024]{1,0:T(8,128)(2,1)} %collective-permute-done.7.k2o_ref, ...), custom_call_target="tpu_custom_call" | custom-call | tf_op jit(solution)/shard_map/pallas_call | solution.py:131
  186.0 0.0 copy-start.2
  186.0 0.9 collective-permute-start.12
  186.9 7.0 %shard_map.48 = bf16[384,256]{1,0:T(8,128)(2,1)} custom-call(s32[3]{0:T(128)} %add_add_fusion.seg_ref, bf16[384,1024]{1,0:T(8,128)(2,1)} %get-tuple-element.16.q_ref, bf16[768,1024]{1,0:T(8,128)(2,1)} %collective-permute-done.5.k2e_ref, bf16[768,1024]{1,0:T(8,128)(2,1)} %collective-permute-done.7.k2o_ref, bf16[768,1024]{1,0:T(8,128)(2,1)} %collective-permute-done.6.k1_ref, ...), custom_call_target="tpu_custom_call" | custom-call | tf_op jit(solution)/shard_map/pallas_call | solution.py:131
  193.9 0.8 collective-permute-done.12
  194.7 0.0 collective-permute-done.11
  194.7 0.0 copy-done.2
  194.7 2.3 %maximum_select_fusion = bf16[384,2048]{1,0:T(8,128)(2,1)} fusion(bf16[384,384]{1,0:T(8,128)(2,1)S(1)} %collective-permute-done.12, bf16[384,640]{1,0:T(8,128)(2,1)S(1)} %collective-permute-done.11, bf16[384,256]{1,0:T(8,128)(2,1)} %shard_map.48, bf16[384,768]{1,0:T(8,128)(2,1)S(1)} %copy-done.2, pred[]{:T(512)S(6)} %eq.16), kind=kLoop, calls=%fused_computation.21 | loop fusion | flops 13369344 | bytes 3145729 | tf_op jit(solution)/shard_map/jit(_where)/select_n | solution.py:217
Async XLA Ops:
  3.2 3.0 %copy-start.4 = (bf16[384,2048]{1,0:T(8,128)(2,1)S(1)}, bf16[384,2048]{1,0:T(8,128)(2,1)}, u32[]{:S(2)}) copy-start(bf16[384,2048]{1,0:T(8,128)(2,1)} %param.4) | copy-start | bytes 4718596
  3.4 45.0 %collective-permute-start.2 = (bf16[1024,896]{1,0:T(8,128)(2,1)S(1)}, bf16[1024,896]{1,0:T(8,128)(2,1)S(1)}, u32[]{:S(2)}, u32[]{:S(2)}) collective-permute-start(bf16[1024,896]{1,0:T(8,128)(2,1)S(1)} %slice.35), channel_id=1, source_target_pairs={{33,0},{32,1},{35,2},{34,3},{37,4},{36,5},{39,6},{38,7},{41,8},{40... | collective-permute-start | bytes 5505032 | tf_op jit(solution)/shard_map/ppermute | solution.py:166
  6.2 45.0 %collective-permute-start = (bf16[384,2048]{1,0:T(8,128)(2,1)S(1)}, bf16[384,2048]{1,0:T(8,128)(2,1)}, u32[]{:S(2)}, u32[]{:S(2)}) collective-permute-start(bf16[384,2048]{1,0:T(8,128)(2,1)S(1)} %copy-done.4), channel_id=1, source_target_pairs={{0,1},{1,0},{2,3},{3,2},{4,5},{5,4},{6,7},{7,6},{8,9},{9,8},{10,11... | collective-permute-start | bytes 4718600 | tf_op jit(solution)/shard_map/ppermute | solution.py:23
  6.5 43.3 %copy-start.3 = (bf16[384,2048]{1,0:T(8,128)(2,1)S(1)}, bf16[384,2048]{1,0:T(8,128)(2,1)}, u32[]{:S(2)}) copy-start(bf16[384,2048]{1,0:T(8,128)(2,1)} %param.5) | copy-start | bytes 4718596
  6.5 41.2 %collective-permute-start.1 = (bf16[1024,128]{1,0:T(8,128)(2,1)S(1)}, bf16[1024,128]{1,0:T(8,128)(2,1)S(1)}, u32[]{:S(2)}, u32[]{:S(2)}) collective-permute-start(bf16[1024,128]{1,0:T(8,128)(2,1)S(1)} %slice.34), channel_id=1, source_target_pairs={{0,1},{1,0},{2,3},{3,2},{4,5},{5,4},{6,7},{7,6},{8,9},{9,8},{10,11... | collective-permute-start | bytes 786440 | tf_op jit(solution)/shard_map/ppermute | solution.py:23
  49.8 7.2 %collective-permute-start.3 = (bf16[1024,1024]{1,0:T(8,128)(2,1)}, bf16[1024,1024]{1,0:T(8,128)(2,1)}, u32[]{:S(2)}, u32[]{:S(2)}) collective-permute-start(bf16[1024,1024]{1,0:T(8,128)(2,1)} %constant_dynamic-update-slice_fusion), channel_id=1, source_target_pairs={{0,2},{2,0},{4,6},{6,4},{8,10},{10,8},{12,14},{14,12},{16,18},{18,... | collective-permute-start | bytes 6291464 | tf_op jit(solution)/shard_map/ppermute | solution.py:169
  57.1 3.6 %copy-start.5 = (bf16[1024,2048]{1,0:T(8,128)(2,1)S(1)}, bf16[1024,2048]{1,0:T(8,128)(2,1)}, u32[]{:S(2)}) copy-start(bf16[1024,2048]{1,0:T(8,128)(2,1)} %param.7) | copy-start | bytes 12582916
  62.5 15.7 %copy-start = (bf16[768,1024]{1,0:T(8,128)(2,1)}, bf16[768,1024]{1,0:T(8,128)(2,1)S(1)}, u32[]{:S(2)}) copy-start(bf16[768,1024]{1,0:T(8,128)(2,1)S(1)} %add_convert_fusion.v0_ref) | copy-start | bytes 4718596
  62.5 4.0 %copy-start.6 = (bf16[1024,2048]{1,0:T(8,128)(2,1)S(1)}, bf16[1024,2048]{1,0:T(8,128)(2,1)}, u32[]{:S(2)}) copy-start(bf16[1024,2048]{1,0:T(8,128)(2,1)} %param.6) | copy-start | bytes 12582916
  68.3 78.1 %copy-start.1 = (bf16[768,1024]{1,0:T(8,128)(2,1)}, bf16[768,1024]{1,0:T(8,128)(2,1)S(1)}, u32[]{:S(2)}) copy-start(bf16[768,1024]{1,0:T(8,128)(2,1)S(1)} %add_convert_fusion.1.k0_ref) | copy-start | bytes 4718596
  68.3 38.6 %collective-permute-start.6 = (bf16[768,1024]{1,0:T(8,128)(2,1)S(1)}, bf16[768,1024]{1,0:T(8,128)(2,1)}, u32[]{:S(2)}, u32[]{:S(2)}) collective-permute-start(bf16[768,1024]{1,0:T(8,128)(2,1)S(1)} %add_convert_fusion.1.k0_ref), channel_id=1, source_target_pairs={{0,2},{2,4},{4,6},{6,8},{8,10},{10,12},{12,14},{14,16},{16,18},{18... | collective-permute-start | bytes 4718600 | tf_op jit(solution)/shard_map/ppermute | solution.py:19
  70.9 69.8 %collective-permute-start.9 = (bf16[768,1024]{1,0:T(8,128)(2,1)S(1)}, bf16[768,1024]{1,0:T(8,128)(2,1)}, u32[]{:S(2)}, u32[]{:S(2)}) collective-permute-start(bf16[768,1024]{1,0:T(8,128)(2,1)S(1)} %add_convert_fusion.v0_ref), channel_id=1, source_target_pairs={{0,2},{2,4},{4,6},{6,8},{8,10},{10,12},{12,14},{14,16},{16,18},{18... | collective-permute-start | bytes 4718600 | tf_op jit(solution)/shard_map/ppermute | solution.py:19
  74.4 71.0 %collective-permute-start.5 = (bf16[768,1024]{1,0:T(8,128)(2,1)S(1)}, bf16[768,1024]{1,0:T(8,128)(2,1)}, u32[]{:S(2)}, u32[]{:S(2)}) collective-permute-start(bf16[768,1024]{1,0:T(8,128)(2,1)S(1)} %add_convert_fusion.1.k0_ref), channel_id=1, source_target_pairs={{0,4},{4,8},{8,12},{12,16},{16,20},{20,24},{24,28},{28,32},{32,36}... | collective-permute-start | bytes 4718600 | tf_op jit(solution)/shard_map/ppermute | solution.py:194
  78.2 68.1 %collective-permute-start.8 = (bf16[768,1024]{1,0:T(8,128)(2,1)S(1)}, bf16[768,1024]{1,0:T(8,128)(2,1)}, u32[]{:S(2)}, u32[]{:S(2)}) collective-permute-start(bf16[768,1024]{1,0:T(8,128)(2,1)S(1)} %add_convert_fusion.v0_ref), channel_id=1, source_target_pairs={{0,4},{4,8},{8,12},{12,16},{16,20},{20,24},{24,28},{28,32},{32,36}... | collective-permute-start | bytes 4718600 | tf_op jit(solution)/shard_map/ppermute | solution.py:194
  107.0 39.4 %collective-permute-start.7 = (bf16[768,1024]{1,0:T(8,128)(2,1)}, bf16[768,1024]{1,0:T(8,128)(2,1)}, u32[]{:S(2)}, u32[]{:S(2)}) collective-permute-start(bf16[768,1024]{1,0:T(8,128)(2,1)} %collective-permute-done.6.k1_ref), channel_id=1, source_target_pairs={{0,2},{4,6},{8,10},{12,14},{16,18},{20,22},{24,26},{28,30},{32,34}... | collective-permute-start | bytes 4718600 | tf_op jit(solution)/shard_map/ppermute | solution.py:195
  140.8 5.6 %collective-permute-start.10 = (bf16[768,1024]{1,0:T(8,128)(2,1)}, bf16[768,1024]{1,0:T(8,128)(2,1)}, u32[]{:S(2)}, u32[]{:S(2)}) collective-permute-start(bf16[768,1024]{1,0:T(8,128)(2,1)} %collective-permute-done.9.v1_ref), channel_id=1, source_target_pairs={{0,2},{4,6},{8,10},{12,14},{16,18},{20,22},{24,26},{28,30},{32,34}... | collective-permute-start | bytes 4718600 | tf_op jit(solution)/shard_map/ppermute | solution.py:195
  143.2 18.7 %collective-permute-start.4 = (bf16[384,1024]{1,0:T(8,128)(2,1)}, bf16[384,1024]{1,0:T(8,128)(2,1)}, u32[]{:S(2)}, u32[]{:S(2)}) collective-permute-start(bf16[384,1024]{1,0:T(8,128)(2,1)} %get-tuple-element.11), channel_id=1, source_target_pairs={{0,1},{1,0},{2,3},{3,2},{4,5},{5,4},{6,7},{7,6},{8,9},{9,8},{10,11... | collective-permute-start | bytes 2359304 | tf_op jit(solution)/shard_map/ppermute | solution.py:23
  175.6 19.1 %collective-permute-start.11 = (bf16[384,640]{1,0:T(8,128)(2,1)}, bf16[384,640]{1,0:T(8,128)(2,1)S(1)}, u32[]{:S(2)}, u32[]{:S(2)}) collective-permute-start(bf16[384,640]{1,0:T(8,128)(2,1)} %shard_map.49), channel_id=1, source_target_pairs={{0,1},{1,0},{2,3},{3,2},{4,5},{5,4},{6,7},{7,6},{8,9},{9,8},{10,11... | collective-permute-start | bytes 1474568 | tf_op jit(solution)/shard_map/ppermute | solution.py:23
  186.0 8.7 %copy-start.2 = (bf16[384,768]{1,0:T(8,128)(2,1)S(1)}, bf16[384,768]{1,0:T(8,128)(2,1)}, u32[]{:S(2)}) copy-start(bf16[384,768]{1,0:T(8,128)(2,1)} %shard_map.46) | copy-start | bytes 1769476
  186.0 8.7 %collective-permute-start.12 = (bf16[384,384]{1,0:T(8,128)(2,1)}, bf16[384,384]{1,0:T(8,128)(2,1)S(1)}, u32[]{:S(2)}, u32[]{:S(2)}) collective-permute-start(bf16[384,384]{1,0:T(8,128)(2,1)} %shard_map.47), channel_id=1, source_target_pairs={{0,1},{1,0},{2,3},{3,2},{4,5},{5,4},{6,7},{7,6},{8,9},{9,8},{10,11... | collective-permute-start | bytes 884744 | tf_op jit(solution)/shard_map/ppermute | solution.py:23

commit v13 on v11

--- a/solution.py
+++ b/solution.py
@@ -192,8 +192,11 @@
         odd_two = lax.ppermute(one, "seg", forward_pairs)
         return (even_two, odd_two), one
 
-    key_two, key_one = shifted(own_key)
-    value_two, value_one = shifted(own_value)
+    key_one = from_behind(own_key, "seg", 1)
+    value_one = from_behind(own_value, "seg", 1)
+    both_two = lax.ppermute(jnp.stack([own_key, own_value]), "seg", even_pairs)
+    key_two = (both_two[0], lax.ppermute(key_one, "seg", forward_pairs))
+    value_two = (both_two[1], lax.ppermute(value_one, "seg", forward_pairs))
     keys = (*key_two, key_one, own_key)
     values = (*value_two, value_one, own_value)
 

time: 194 us -> 205 us (1.057)
  waiting for transfers between devices: 96 us -> 105 us
  starting transfers between devices: 28 us -> 21.5 us
  local copies, waits for them, and re-layouts: 4.33 us -> 9.85 us
  other arithmetic: 12.7 us -> 14.8 us
    ppermute x2, waiting for transfers between devices: 56.7 us -> 67.3 us  [from_behind(): lax.ppermute(value, axis, [(source, source + steps) for source in range(l...]
    ppermute x4 -> x3, starting transfers between devices: 12.6 us -> 6.57 us  [the longest x1 3.81 us: body(): both_two = lax.ppermute(jnp.stack([own_key, own_value]), 'seg', even_pairs)]
    squeeze x0 -> x1, local copies, waits for them, and re-layouts: none -> 3.87 us  [body(): value_two = (both_two[1], lax.ppermute(value_one, 'seg', forward_pairs))]
    another operation x0 -> x1, other arithmetic: none -> 2.11 us  [body(): both_two = lax.ppermute(jnp.stack([own_key, own_value]), 'seg', even_pairs)]
  transfers between devices with their start and end apart: 13 -> 12, of which waited for: 5 -> 4; matrix products, arithmetic and copies ran while one was open for 4% -> 5% of each run, Pallas kernels for 16% -> 16%
where the time goes in v13:
time: 205 us; the launch traced here: 204 us
  waiting for transfers between devices  105 us (51%)
  Pallas kernels  45.6 us (22%)
  starting transfers between devices  21.5 us (10%)
  other arithmetic  14.8 us (7%)
  local copies, waits for them, and re-layouts  9.85 us (5%)
  matrix products  6.85 us (3%)
    ppermute x2, waiting for transfers between devices, from_behind(): lax.ppermute(value, axis, [(source, source + steps) for source in range(l...  67.3 us
    pallas_call x4, Pallas kernels, attend(): pl.pallas_call(attention_kernel, grid_spec=grid_spec, out_shape=jax.Shape...  45.6 us
    ppermute x1, waiting for transfers between devices, body(): right_got = lax.ppermute(served[:, piece:], ('seg', 'fsdp'), wrap_pairs)  30.8 us
    ppermute x5, waiting for transfers between devices, swap_halves(): return lax.ppermute(value, 'fsdp', [(0, 1), (1, 0)])  7.16 us
    ppermute x5, starting transfers between devices, swap_halves(): return lax.ppermute(value, 'fsdp', [(0, 1), (1, 0)])  6.13 us
    select_n x2, other arithmetic, in_order(): lead = jnp.where(first_is_mine, mine, other)  5.91 us
    ppermute x2, starting transfers between devices, from_behind(): lax.ppermute(value, axis, [(source, source + steps) for source in range(l...  5.85 us
  transfers between devices with their start and end apart: 12, of which 4 were waited for; matrix products, arithmetic and copies ran while one was open for 5% of the time, Pallas kernels for 16%

profile of v13, /device:TPU:24, one launch (start us, length us, event | category | flops | bytes accessed | tf_op | source)
XLA Modules:
  0.0 204.2 jit_solution(1353367358633302398)
XLA Ops:
  0.0 3.2 %dynamic-slice_select_fusion = bf16[1024,1024]{1,0:T(8,128)(2,1)S(1)} fusion(bf16[1024,2048]{1,0:T(8,128)(2,1)} %param.7, s32[]{:T(128)S(6)} %select_n.76, bf16[1024,2048]{1,0:T(8,128)(2,1)} %param.6, pred[]{:T(512)S(6)} %eq.17), kind=kLoop, calls=%fused_computation.10 | loop fusion | flops 1048576 | bytes 6291461 | tf_op jit(solution)/shard_map/jit(_where)/select_n | solution.py:159
  3.2 0.2 slice.17
  3.4 2.8 %collective-permute-start.2 = (bf16[1024,896]{1,0:T(8,128)(2,1)S(1)}, bf16[1024,896]{1,0:T(8,128)(2,1)S(1)}, u32[]{:S(2)}, u32[]{:S(2)}) collective-permute-start(bf16[1024,896]{1,0:T(8,128)(2,1)S(1)} %slice.17), channel_id=1, source_target_pairs={{33,0},{32,1},{35,2},{34,3},{37,4},{36,5},{39,6},{38,7},{41,8},{40... | collective-permute-start | bytes 5505032 | tf_op jit(solution)/shard_map/ppermute | solution.py:166
  6.2 0.1 slice.16
  6.3 0.3 collective-permute-start.1
  6.6 1.8 collective-permute-start
  8.4 7.1 %collective-permute-done.1 = bf16[1024,128]{1,0:T(8,128)(2,1)S(1)} collective-permute-done((bf16[1024,128]{1,0:T(8,128)(2,1)S(1)}, bf16[1024,128]{1,0:T(8,128)(2,1)S(1)}, u32[]{:S(2)}, u32[]{:S(2)}) %collective-permute-start.1) | collective-permute-done | bytes 262176 | tf_op jit(solution)/shard_map/ppermute | solution.py:23
  15.5 0.1 constant_dynamic-update-slice_fusion.1
  15.6 30.8 %collective-permute-done.2 = bf16[1024,896]{1,0:T(8,128)(2,1)S(1)} collective-permute-done((bf16[1024,896]{1,0:T(8,128)(2,1)S(1)}, bf16[1024,896]{1,0:T(8,128)(2,1)S(1)}, u32[]{:S(2)}, u32[]{:S(2)}) %collective-permute-start.2) | collective-permute-done | bytes 1835040 | tf_op jit(solution)/shard_map/ppermute | solution.py:166
  46.4 0.3 constant_dynamic-update-slice_fusion
  46.7 0.1 collective-permute-start.3
  46.8 0.0 copy-start.5
  46.9 2.8 %constant_dynamic-slice_fusion = (bf16[384,1024]{1,0:T(8,128)(2,1)}, bf16[384,1024]{1,0:T(8,128)(2,1)}) fusion(bf16[384,2048]{1,0:T(8,128)(2,1)} %param.5, s32[]{:T(128)S(6)} %select_n.80, s32[]{:T(128)S(6)} %select_n.76), kind=kLoop, calls=%fused_computation.26 | loop fusion | bytes 3145736 | tf_op jit(solution)/shard_map/dynamic_slice | solution.py:154
  49.7 0.0 copy-start.4
  49.7 0.0 collective-permute-done
  49.7 2.2 %broadcast_select_fusion.7 = (bf16[384,2048]{1,0:T(8,128)(2,1)S(1)}, bf16[384,2048]{1,0:T(8,128)(2,1)S(1)}) fusion(bf16[384,2048]{1,0:T(8,128)(2,1)} %param.4, bf16[384,2048]{1,0:T(8,128)(2,1)} %collective-permute-done, pred[]{:T(512)S(6)} %eq.16), kind=kLoop, calls=%fused_computation.23 | loop fusion | flops 1572864 | bytes 6291457 | tf_op jit(solution)/shard_map/jit(_where)/select_n | solution.py:27
  51.9 0.0 collective-permute-done.3
  52.0 0.0 copy-done.5
  52.0 0.9 copy-done.4
  52.8 3.7 %broadcast_select_fusion.3 = (bf16[1024,1024]{1,0:T(8,128)(2,1)S(1)}, bf16[1024,1024]{1,0:T(8,128)(2,1)S(1)}, bf16[1024,1024]{1,0:T(8,128)(2,1)S(1)}, bf16[1024,1024]{1,0:T(8,128)(2,1)S(1)}) fusion(pred[]{:T(512)S(6)} %eq.16, bf16[1024,2048]{1,0:T(8,128)(2,1)S(1)} %copy-done.4, s32[]{:T(128)S(6)} %select_n.80, bf16[1024,1024]{1,0:T(8,128)(2,1)} %collective-permute-done.3, ...), kind=kLoop, calls=%fused_computation.14 | loop fusion | flops 6291456 | bytes 16777222 | tf_op jit(solution)/shard_map/jit(_where)/select_n | solution.py:27
  56.5 3.4 %fusion.8.v0_ref = bf16[768,1024]{1,0:T(8,128)(2,1)S(1)} fusion(bf16[1024,1024]{1,0:T(8,128)(2,1)S(1)} %get-tuple-element.18, bf16[1024,1024]{1,0:T(8,128)(2,1)S(1)} %get-tuple-element.17, bf16[384,2048]{1,0:T(8,128)(2,1)S(1)} %get-tuple-element.26, bf16[384,2048]{1,0:T(8,128)(2,1)S(1)} %get-tuple-element.25), kind=kOutput, calls=%fused_computation.17 | convolution fusion | flops 3236691968 | bytes 8912896 | tf_op jit(solution)/shard_map/dot_general | solution.py:180
  59.9 0.0 copy-start
  59.9 3.4 %fusion.11.k0_ref = bf16[768,1024]{1,0:T(8,128)(2,1)S(1)} fusion(bf16[1024,1024]{1,0:T(8,128)(2,1)S(1)} %get-tuple-element.21, bf16[1024,1024]{1,0:T(8,128)(2,1)S(1)} %get-tuple-element.22, bf16[384,2048]{1,0:T(8,128)(2,1)S(1)} %get-tuple-element.26, bf16[384,2048]{1,0:T(8,128)(2,1)S(1)} %get-tuple-element.25), kind=kOutput, calls=%fused_computation.18 | convolution fusion | flops 3236691968 | bytes 8912896 | tf_op jit(solution)/shard_map/dot_general | solution.py:179
  63.4 0.0 copy-start.1
  63.4 2.1 %pad_maximum_fusion.1 = bf16[2,768,1024]{2,1,0:T(8,128)(2,1)} fusion(bf16[1,768,1024]{2,1,0:T(8,128)(2,1)S(1)} %bitcast.10, bf16[1,768,1024]{2,1,0:T(8,128)(2,1)S(1)} %bitcast.11), kind=kLoop, calls=%fused_computation.9 | loop fusion | flops 1572864 | bytes 6291456 | tf_op jit(solution)/shard_map/stack | solution.py:197
  65.5 3.8 %collective-permute-start.5 = (bf16[2,768,1024]{2,1,0:T(8,128)(2,1)}, bf16[2,768,1024]{2,1,0:T(8,128)(2,1)}, u32[]{:S(2)}, u32[]{:S(2)}) collective-permute-start(bf16[2,768,1024]{2,1,0:T(8,128)(2,1)} %pad_maximum_fusion.1), channel_id=1, source_target_pairs={{0,4},{4,8},{8,12},{12,16},{16,20},{20,24},{24,28},{28,32},{32,36}... | collective-permute-start | bytes 9437192 | tf_op jit(solution)/shard_map/ppermute | solution.py:197
  69.3 0.0 copy-done.1
  69.3 1.9 collective-permute-start.6
  71.3 0.0 copy-done
  71.3 3.9 %collective-permute-start.8 = (bf16[768,1024]{1,0:T(8,128)(2,1)S(1)}, bf16[768,1024]{1,0:T(8,128)(2,1)}, u32[]{:S(2)}, u32[]{:S(2)}) collective-permute-start(bf16[768,1024]{1,0:T(8,128)(2,1)S(1)} %fusion.8.v0_ref), channel_id=1, source_target_pairs={{0,2},{2,4},{4,6},{6,8},{8,10},{10,12},{12,14},{14,16},{16,18},{18... | collective-permute-start | bytes 4718600 | tf_op jit(solution)/shard_map/ppermute | solution.py:19
  75.2 37.3 %collective-permute-done.6.k1_ref = bf16[768,1024]{1,0:T(8,128)(2,1)} collective-permute-done((bf16[768,1024]{1,0:T(8,128)(2,1)S(1)}, bf16[768,1024]{1,0:T(8,128)(2,1)}, u32[]{:S(2)}, u32[]{:S(2)}) %collective-permute-start.6) | collective-permute-done | bytes 1572896 | tf_op jit(solution)/shard_map/ppermute | solution.py:19
  112.5 1.4 collective-permute-start.7
  113.9 30.0 %collective-permute-done.8.v1_ref = bf16[768,1024]{1,0:T(8,128)(2,1)} collective-permute-done((bf16[768,1024]{1,0:T(8,128)(2,1)S(1)}, bf16[768,1024]{1,0:T(8,128)(2,1)}, u32[]{:S(2)}, u32[]{:S(2)}) %collective-permute-start.8) | collective-permute-done | bytes 1572896 | tf_op jit(solution)/shard_map/ppermute | solution.py:19
  144.0 1.4 collective-permute-start.9
  145.3 2.2 %collective-permute-start.4 = (bf16[384,1024]{1,0:T(8,128)(2,1)}, bf16[384,1024]{1,0:T(8,128)(2,1)}, u32[]{:S(2)}, u32[]{:S(2)}) collective-permute-start(bf16[384,1024]{1,0:T(8,128)(2,1)} %get-tuple-element.11), channel_id=1, source_target_pairs={{0,1},{1,0},{2,3},{3,2},{4,5},{5,4},{6,7},{7,6},{8,9},{9,8},{10,11... | collective-permute-start | bytes 2359304 | tf_op jit(solution)/shard_map/ppermute | solution.py:23
  147.5 0.7 add_add_fusion.seg_ref
  148.2 0.6 add_add_fusion.1.seg_ref
  148.8 0.0 collective-permute-done.5
  148.8 3.9 %slice_bitcast_fusion = (bf16[768,1024]{1,0:T(8,128)(2,1)}, bf16[768,1024]{1,0:T(8,128)(2,1)}) fusion(bf16[2,768,1024]{2,1,0:T(8,128)(2,1)} %collective-permute-done.5), kind=kLoop, calls=%fused_computation.19 | loop fusion | bytes 6291456 | tf_op jit(solution)/shard_map/squeeze | solution.py:199
  152.7 0.0 collective-permute-done.7.k2o_ref
  152.7 0.0 copy-start.2
  152.7 0.0 collective-permute-done.9.v2o_ref
  152.7 0.0 copy-start.3
  152.7 1.2 copy-done.2
  153.8 0.5 copy-done.3
  154.3 15.4 %shard_map.46 = bf16[384,768]{1,0:T(8,128)(2,1)} custom-call(s32[3]{0:T(128)} %add_add_fusion.seg_ref, bf16[384,1024]{1,0:T(8,128)(2,1)} %get-tuple-element.16.q_ref, bf16[768,1024]{1,0:T(8,128)(2,1)} %get-tuple-element.24.k2e_ref, bf16[768,1024]{1,0:T(8,128)(2,1)} %copy-done.2, bf16[768,1024]{1,0:T(8,128)(2,1)} %collective-permute-done.6.k1_ref, ...), custom_call_target="tpu_custom_call" | custom-call | tf_op jit(solution)/shard_map/pallas_call | solution.py:131
  169.8 0.0 collective-permute-done.4.q_ref
  169.8 13.8 %shard_map.49 = bf16[384,640]{1,0:T(8,128)(2,1)} custom-call(s32[3]{0:T(128)} %add_add_fusion.1.seg_ref, bf16[384,1024]{1,0:T(8,128)(2,1)} %collective-permute-done.4.q_ref, bf16[768,1024]{1,0:T(8,128)(2,1)} %get-tuple-element.24.k2e_ref, bf16[768,1024]{1,0:T(8,128)(2,1)} %copy-done.2, bf16[768,1024]{1,0:T(8,128)(2,1)} %collective-permute-done.6.k1_ref, ...), custom_call_target="tpu_custom_call" | custom-call | tf_op jit(solution)/shard_map/pallas_call | solution.py:131
  183.5 0.2 collective-permute-start.10
  183.8 9.4 %shard_map.47 = bf16[384,384]{1,0:T(8,128)(2,1)} custom-call(s32[3]{0:T(128)} %add_add_fusion.1.seg_ref, bf16[384,1024]{1,0:T(8,128)(2,1)} %collective-permute-done.4.q_ref, bf16[768,1024]{1,0:T(8,128)(2,1)} %get-tuple-element.24.k2e_ref, bf16[768,1024]{1,0:T(8,128)(2,1)} %copy-done.2, bf16[768,1024]{1,0:T(8,128)(2,1)} %collective-permute-done.6.k1_ref, ...), custom_call_target="tpu_custom_call" | custom-call | tf_op jit(solution)/shard_map/pallas_call | solution.py:131
  193.2 0.0 copy-start.6
  193.2 1.6 collective-permute-start.11
  194.8 7.0 %shard_map.48 = bf16[384,256]{1,0:T(8,128)(2,1)} custom-call(s32[3]{0:T(128)} %add_add_fusion.seg_ref, bf16[384,1024]{1,0:T(8,128)(2,1)} %get-tuple-element.16.q_ref, bf16[768,1024]{1,0:T(8,128)(2,1)} %get-tuple-element.24.k2e_ref, bf16[768,1024]{1,0:T(8,128)(2,1)} %copy-done.2, bf16[768,1024]{1,0:T(8,128)(2,1)} %collective-permute-done.6.k1_ref, ...), custom_call_target="tpu_custom_call" | custom-call | tf_op jit(solution)/shard_map/pallas_call | solution.py:131
  201.8 0.0 collective-permute-done.11
  201.8 0.0 collective-permute-done.10
  201.8 0.0 copy-done.6
  201.8 2.3 %maximum_select_fusion = bf16[384,2048]{1,0:T(8,128)(2,1)} fusion(bf16[384,384]{1,0:T(8,128)(2,1)S(1)} %collective-permute-done.11, bf16[384,640]{1,0:T(8,128)(2,1)S(1)} %collective-permute-done.10, bf16[384,256]{1,0:T(8,128)(2,1)} %shard_map.48, bf16[384,768]{1,0:T(8,128)(2,1)S(1)} %copy-done.6, pred[]{:T(512)S(6)} %eq.16), kind=kLoop, calls=%fused_computation.21 | loop fusion | flops 13369344 | bytes 3145729 | tf_op jit(solution)/shard_map/jit(_where)/select_n | solution.py:217
Async XLA Ops:
  3.4 43.0 %collective-permute-start.2 = (bf16[1024,896]{1,0:T(8,128)(2,1)S(1)}, bf16[1024,896]{1,0:T(8,128)(2,1)S(1)}, u32[]{:S(2)}, u32[]{:S(2)}) collective-permute-start(bf16[1024,896]{1,0:T(8,128)(2,1)S(1)} %slice.17), channel_id=1, source_target_pairs={{33,0},{32,1},{35,2},{34,3},{37,4},{36,5},{39,6},{38,7},{41,8},{40... | collective-permute-start | bytes 5505032 | tf_op jit(solution)/shard_map/ppermute | solution.py:166
  6.3 9.3 %collective-permute-start.1 = (bf16[1024,128]{1,0:T(8,128)(2,1)S(1)}, bf16[1024,128]{1,0:T(8,128)(2,1)S(1)}, u32[]{:S(2)}, u32[]{:S(2)}) collective-permute-start(bf16[1024,128]{1,0:T(8,128)(2,1)S(1)} %slice.16), channel_id=1, source_target_pairs={{0,1},{1,0},{2,3},{3,2},{4,5},{5,4},{6,7},{7,6},{8,9},{9,8},{10,11... | collective-permute-start | bytes 786440 | tf_op jit(solution)/shard_map/ppermute | solution.py:23
  6.6 43.1 %collective-permute-start = (bf16[384,2048]{1,0:T(8,128)(2,1)}, bf16[384,2048]{1,0:T(8,128)(2,1)}, u32[]{:S(2)}, u32[]{:S(2)}) collective-permute-start(bf16[384,2048]{1,0:T(8,128)(2,1)} %param.4), channel_id=1, source_target_pairs={{0,1},{1,0},{2,3},{3,2},{4,5},{5,4},{6,7},{7,6},{8,9},{9,8},{10,11... | collective-permute-start | bytes 4718600 | tf_op jit(solution)/shard_map/ppermute | solution.py:23
  46.7 5.2 %collective-permute-start.3 = (bf16[1024,1024]{1,0:T(8,128)(2,1)S(1)}, bf16[1024,1024]{1,0:T(8,128)(2,1)}, u32[]{:S(2)}, u32[]{:S(2)}) collective-permute-start(bf16[1024,1024]{1,0:T(8,128)(2,1)S(1)} %constant_dynamic-update-slice_fusion), channel_id=1, source_target_pairs={{0,2},{2,0},{4,6},{6,4},{8,10},{10,8},{12,14},{14,12},{16,18},{18,... | collective-permute-start | bytes 6291464 | tf_op jit(solution)/shard_map/ppermute | solution.py:169
  46.8 5.1 %copy-start.5 = (bf16[1024,2048]{1,0:T(8,128)(2,1)S(1)}, bf16[1024,2048]{1,0:T(8,128)(2,1)}, u32[]{:S(2)}) copy-start(bf16[1024,2048]{1,0:T(8,128)(2,1)} %param.6) | copy-start | bytes 12582916
  49.7 3.1 %copy-start.4 = (bf16[1024,2048]{1,0:T(8,128)(2,1)S(1)}, bf16[1024,2048]{1,0:T(8,128)(2,1)}, u32[]{:S(2)}) copy-start(bf16[1024,2048]{1,0:T(8,128)(2,1)} %param.7) | copy-start | bytes 12582916
  59.9 11.3 %copy-start = (bf16[768,1024]{1,0:T(8,128)(2,1)}, bf16[768,1024]{1,0:T(8,128)(2,1)S(1)}, u32[]{:S(2)}) copy-start(bf16[768,1024]{1,0:T(8,128)(2,1)S(1)} %fusion.8.v0_ref) | copy-start | bytes 4718596
  63.4 5.9 %copy-start.1 = (bf16[768,1024]{1,0:T(8,128)(2,1)}, bf16[768,1024]{1,0:T(8,128)(2,1)S(1)}, u32[]{:S(2)}) copy-start(bf16[768,1024]{1,0:T(8,128)(2,1)S(1)} %fusion.11.k0_ref) | copy-start | bytes 4718596
  65.5 83.3 %collective-permute-start.5 = (bf16[2,768,1024]{2,1,0:T(8,128)(2,1)}, bf16[2,768,1024]{2,1,0:T(8,128)(2,1)}, u32[]{:S(2)}, u32[]{:S(2)}) collective-permute-start(bf16[2,768,1024]{2,1,0:T(8,128)(2,1)} %pad_maximum_fusion.1), channel_id=1, source_target_pairs={{0,4},{4,8},{8,12},{12,16},{16,20},{20,24},{24,28},{28,32},{32,36}... | collective-permute-start | bytes 9437192 | tf_op jit(solution)/shard_map/ppermute | solution.py:197
  69.3 43.2 %collective-permute-start.6 = (bf16[768,1024]{1,0:T(8,128)(2,1)S(1)}, bf16[768,1024]{1,0:T(8,128)(2,1)}, u32[]{:S(2)}, u32[]{:S(2)}) collective-permute-start(bf16[768,1024]{1,0:T(8,128)(2,1)S(1)} %fusion.11.k0_ref), channel_id=1, source_target_pairs={{0,2},{2,4},{4,6},{6,8},{8,10},{10,12},{12,14},{14,16},{16,18},{18... | collective-permute-start | bytes 4718600 | tf_op jit(solution)/shard_map/ppermute | solution.py:19
  71.3 72.7 %collective-permute-start.8 = (bf16[768,1024]{1,0:T(8,128)(2,1)S(1)}, bf16[768,1024]{1,0:T(8,128)(2,1)}, u32[]{:S(2)}, u32[]{:S(2)}) collective-permute-start(bf16[768,1024]{1,0:T(8,128)(2,1)S(1)} %fusion.8.v0_ref), channel_id=1, source_target_pairs={{0,2},{2,4},{4,6},{6,8},{8,10},{10,12},{12,14},{14,16},{16,18},{18... | collective-permute-start | bytes 4718600 | tf_op jit(solution)/shard_map/ppermute | solution.py:19
  112.5 40.1 %collective-permute-start.7 = (bf16[768,1024]{1,0:T(8,128)(2,1)}, bf16[768,1024]{1,0:T(8,128)(2,1)S(1)}, u32[]{:S(2)}, u32[]{:S(2)}) collective-permute-start(bf16[768,1024]{1,0:T(8,128)(2,1)} %collective-permute-done.6.k1_ref), channel_id=1, source_target_pairs={{0,2},{4,6},{8,10},{12,14},{16,18},{20,22},{24,26},{28,30},{32,34}... | collective-permute-start | bytes 4718600 | tf_op jit(solution)/shard_map/ppermute | solution.py:198
  144.0 8.7 %collective-permute-start.9 = (bf16[768,1024]{1,0:T(8,128)(2,1)}, bf16[768,1024]{1,0:T(8,128)(2,1)S(1)}, u32[]{:S(2)}, u32[]{:S(2)}) collective-permute-start(bf16[768,1024]{1,0:T(8,128)(2,1)} %collective-permute-done.8.v1_ref), channel_id=1, source_target_pairs={{0,2},{4,6},{8,10},{12,14},{16,18},{20,22},{24,26},{28,30},{32,34}... | collective-permute-start | bytes 4718600 | tf_op jit(solution)/shard_map/ppermute | solution.py:199
  145.3 24.4 %collective-permute-start.4 = (bf16[384,1024]{1,0:T(8,128)(2,1)}, bf16[384,1024]{1,0:T(8,128)(2,1)}, u32[]{:S(2)}, u32[]{:S(2)}) collective-permute-start(bf16[384,1024]{1,0:T(8,128)(2,1)} %get-tuple-element.11), channel_id=1, source_target_pairs={{0,1},{1,0},{2,3},{3,2},{4,5},{5,4},{6,7},{7,6},{8,9},{9,8},{10,11... | collective-permute-start | bytes 2359304 | tf_op jit(solution)/shard_map/ppermute | solution.py:23
  152.7 1.2 copy-start.2
  152.7 1.6 copy-start.3
  183.5 18.3 %collective-permute-start.10 = (bf16[384,640]{1,0:T(8,128)(2,1)}, bf16[384,640]{1,0:T(8,128)(2,1)S(1)}, u32[]{:S(2)}, u32[]{:S(2)}) collective-permute-start(bf16[384,640]{1,0:T(8,128)(2,1)} %shard_map.49), channel_id=1, source_target_pairs={{0,1},{1,0},{2,3},{3,2},{4,5},{5,4},{6,7},{7,6},{8,9},{9,8},{10,11... | collective-permute-start | bytes 1474568 | tf_op jit(solution)/shard_map/ppermute | solution.py:23
  193.2 8.7 %copy-start.6 = (bf16[384,768]{1,0:T(8,128)(2,1)S(1)}, bf16[384,768]{1,0:T(8,128)(2,1)}, u32[]{:S(2)}) copy-start(bf16[384,768]{1,0:T(8,128)(2,1)} %shard_map.46) | copy-start | bytes 1769476
  193.2 8.7 %collective-permute-start.11 = (bf16[384,384]{1,0:T(8,128)(2,1)}, bf16[384,384]{1,0:T(8,128)(2,1)S(1)}, u32[]{:S(2)}, u32[]{:S(2)}) collective-permute-start(bf16[384,384]{1,0:T(8,128)(2,1)} %shard_map.47), channel_id=1, source_target_pairs={{0,1},{1,0},{2,3},{3,2},{4,5},{5,4},{6,7},{7,6},{8,9},{9,8},{10,11... | collective-permute-start | bytes 884744 | tf_op jit(solution)/shard_map/ppermute | solution.py:23
